TPU v7x, 32 devices: a whole 2x2x4 slice. The times are simulated.
32 devices in a mesh: lat: 16 (over z, y, core), tm: 2 (over x).
Axes of the slice: x: 2, y: 2, z: 4, core: 2. Of those that a mesh axis runs over, the one named last changes fastest.
Arguments:
- fields: bfloat16 [3, 20, 640, 16, 64], P(None, None, 'lat', None, 'tm'), may hold values from -6 to 6
- vmodes: bfloat16 [20, 16], replicated, may hold values from -1.25 to 1.25
- owner_map: int32 [16], replicated, may hold values from 0 to 15, each once
- hough_table: bfloat16 [16, 15360, 1920], P('tm', 'lat'), may hold values from -0.125 to 0.125
- keep_mask: int32 [16, 15360], P('tm', 'lat'), may hold values 0 or 1
Outputs:
- filtered_fields: bfloat16 [16, 3, 640, 16, 64], P(None, None, 'lat', None, 'tm')
Inputs may be any that keep to these rules, and one draw needn't show every extreme that they name: owner_map is a permutation of 0 to 15; order m uses the rows of hough_table and keep_mask of owner slot owner_map[m].
All inputs are finite; a program needn't handle non-finite values. No bound on the sum of `keep_mask` on one device may be relied on, other than what follows from the above.
Results may differ from a plain program's by a relative error of at most 0.0055.
Values may be sent and summed in bfloat16 or wider, within the bound.
No kernel may reach another device: no remote copies, remote signals or barrier semaphores. Data moves between devices by JAX's collectives and lax.ppermute only.
A program may use at most 128 MiB of HBM per device.

v0:
```python
import jax
import jax.numpy as jnp
from jax import lax
from jax.sharding import PartitionSpec as P

AXES = ("lat", "tm")


def order_of_slot(owner_map):
    ids = jnp.arange(owner_map.shape[0], dtype=jnp.int32)
    hit = owner_map[None, :] == ids[:, None]
    return jnp.sum(jnp.where(hit, ids[None, :], 0), axis=1).astype(jnp.int32)


def body(fields, vmodes, owner_map, hough_table, keep_mask):
    n_lat = lax.axis_size("lat")
    n_tm = lax.axis_size("tm")
    orders = owner_map.shape[0]
    group_size = n_lat // orders
    variables, lev, lat_count, _, span = fields.shape
    kmodes = vmodes.shape[1]
    k_loc = kmodes // n_tm
    vm = vmodes.reshape(lev, n_tm, k_loc)
    projected = jnp.einsum(
        "vlamc,lus->muvsac", fields, vm, preferred_element_type=jnp.float32
    ).astype(jnp.bfloat16)
    dest_order = order_of_slot(owner_map)[jnp.arange(n_lat, dtype=jnp.int32) // group_size]
    outgoing = jnp.take(projected, dest_order, axis=0)
    outgoing = outgoing.reshape(n_lat * n_tm, -1)
    incoming = lax.all_to_all(outgoing, AXES, 0, 0, tiled=True)
    incoming = incoming.reshape(n_lat, n_tm, variables, k_loc, lat_count, span)
    columns = incoming.transpose(3, 2, 0, 4, 1, 5).reshape(
        k_loc, variables * n_lat * lat_count, n_tm * span
    )
    coefficients = jnp.einsum(
        "knj,kjc->knc", hough_table, columns, preferred_element_type=jnp.float32
    )
    kept = (coefficients * keep_mask.astype(jnp.float32)[:, :, None]).astype(jnp.bfloat16)
    synth = jnp.einsum("knj,knc->kjc", hough_table, kept, preferred_element_type=jnp.float32)
    synth = synth.reshape(k_loc, variables, n_lat, lat_count, n_tm, span)
    synth = synth.transpose(2, 4, 0, 1, 3, 5)
    if group_size == 1:
        synth = synth.astype(jnp.bfloat16)
    returned = lax.all_to_all(synth.reshape(n_lat * n_tm, -1), AXES, 0, 0, tiled=True)
    returned = returned.reshape(orders, group_size, n_tm, k_loc, variables, lat_count, span)
    returned = returned.sum(axis=1) if group_size > 1 else returned[:, 0]
    result = jnp.take(returned, owner_map, axis=0)
    result = result.reshape(orders, kmodes, variables, lat_count, span)
    return result.transpose(1, 2, 3, 0, 4).astype(jnp.bfloat16)


def solution(mesh):
    in_specs = (P(None, None, "lat", None, "tm"), P(), P(), P("tm", "lat", None), P("tm", "lat"))
    out_specs = P(None, None, "lat", None, "tm")
    return jax.shard_map(body, mesh=mesh, in_specs=in_specs, out_specs=out_specs, check_vma=False)
```

profile of v0, /device:TPU:0, one launch (start us, length us, event | category | flops | bytes accessed | tf_op | source)
XLA Modules:
  0.0 324.2 jit_solution(8314536987223966941)
XLA Ops:
  0.0 0.8 select_reduce_fusion
  0.8 0.7 gather_fusion
  1.5 11.9 %convert_bitcast_fusion = bf16[16,2,3,8,40,32]{4,3,5,0,2,1:T(8,128)(2,1)} fusion(bf16[3,20,40,16,32]{2,4,3,1,0:T(8,128)(2,1)} %param.5, bf16[20,16]{0,1:T(8,128)(2,1)S(1)} %copy-done), kind=kOutput, calls=%fused_computation.8 | convolution fusion | flops 40304640 | bytes 4424320 | tf_op jit(solution)/shard_map/vlamc,lus->muvsac/dot_general | solution.py:24
  13.4 6.8 %gather_fusion.1 = bf16[16,2,3,8,40,32]{4,3,5,2,1,0:T(8,128)(2,1)} fusion(bf16[16,2,3,8,40,32]{4,3,5,0,2,1:T(8,128)(2,1)} %convert_bitcast_fusion, s32[1024]{0:T(1024)S(1)} %pad_clamp_fusion.1), kind=kCustom, calls=%fused_computation.1 | custom fusion | bytes 3932224 | tf_op jit(solution)/shard_map/jit(_take)/gather | solution.py:28
  20.3 11.0 %copy.22 = bf16[16,2,3,8,40,32]{5,4,3,2,1,0:T(8,128)(2,1)} copy(bf16[16,2,3,8,40,32]{4,3,5,2,1,0:T(8,128)(2,1)} %gather_fusion.1) | data formatting | bytes 3932160 | tf_op jit(solution)/shard_map/jit(_take)/gather | solution.py:28
  31.3 9.9 %gather.20 = bf16[32,1,30720]{2,0,1:T(8,128)(2,1)S(1)} reshape(bf16[16,2,3,8,40,32]{5,4,3,2,1,0:T(8,128)(2,1)} %copy.22) | data formatting | bytes 3932160 | tf_op jit(solution)/shard_map/jit(_take)/gather | solution.py:28
  41.3 0.1 broadcast_in_dim.47
  41.4 1.5 broadcast_select_fusion
  43.0 0.6 broadcast.108
  43.5 3.7 %reduce.2 = bf16[32,30720]{1,0:T(8,128)(2,1)S(1)} reduce(bf16[32,1,30720]{2,0,1:T(8,128)(2,1)} %broadcast_select_fusion, bf16[]{:T(256)} %broadcast.108), dimensions={1}, to_apply=%copy.23.reduce_sub_computation | reduce | bytes 3932162 | tf_op jit(solution)/shard_map/jit(_take)/select_n | solution.py:28
  47.2 2.4 reshape.120
  49.6 7.5 %all-to-all-start = ((bf16[32,2,15360]{2,1,0:T(2,128)(2,1)}), bf16[32,2,15360]{2,1,0:T(2,128)(2,1)S(1)}, u32[]{:S(2)}, u32[]{:S(2)}) async-start(bf16[32,2,15360]{2,1,0:T(2,128)(2,1)} %reshape.120), calls=%async_computation | async-start | bytes 3932160 | tf_op jit(solution)/shard_map/all_to_all | solution.py:30
  57.2 45.7 %all-to-all-done = bf16[32,2,15360]{2,1,0:T(2,128)(2,1)S(1)} async-done(((bf16[32,2,15360]{2,1,0:T(2,128)(2,1)}), bf16[32,2,15360]{2,1,0:T(2,128)(2,1)S(1)}, u32[]{:S(2)}, u32[]{:S(2)}) %all-to-all-start) | async-done | bytes 1966112 | tf_op jit(solution)/shard_map/all_to_all | solution.py:30
  102.8 6.4 %reshape.121 = bf16[32,1,30720]{2,1,0:T(2,128)(2,1)} reshape(bf16[32,2,15360]{2,1,0:T(2,128)(2,1)S(1)} %all-to-all-done) | data formatting | bytes 3932160
  109.2 12.1 %reduce = bf16[32,30720]{1,0:T(8,128)(2,1)S(1)} reduce(bf16[32,1,30720]{2,1,0:T(2,128)(2,1)} %reshape.121, bf16[]{:T(256)} %constant.44), dimensions={1}, to_apply=%all_to_all.10.reduce_sub_computation | reduce | bytes 3932162 | tf_op jit(solution)/shard_map/all_to_all | solution.py:30
  121.3 7.6 %reshape.89 = bf16[16,2,3,8,40,32]{5,4,3,2,1,0:T(8,128)(2,1)} reshape(bf16[32,30720]{1,0:T(8,128)(2,1)S(1)} %reduce) | data formatting | bytes 3932160 | tf_op jit(solution)/shard_map/reshape | solution.py:31
  128.8 11.6 %copy.24 = bf16[8,3,16,40,2,32]{3,2,1,5,4,0:T(8,128)(2,1)} copy(bf16[8,3,16,40,2,32]{5,3,0,1,4,2:T(8,128)(2,1)} %bitcast.39) | data formatting | bytes 3932160 | tf_op jit(solution)/shard_map/transpose | solution.py:32
  140.4 8.9 %reshape.90 = bf16[8,1920,64]{1,2,0:T(8,128)(2,1)S(1)} reshape(bf16[8,3,16,40,2,32]{3,2,1,5,4,0:T(8,128)(2,1)} %copy.24) | data formatting | bytes 3932160 | tf_op jit(solution)/shard_map/reshape | solution.py:32
  149.3 24.0 %fusion.6 = bf16[8,1920,64]{1,2,0:T(8,128)(2,1)} fusion(bf16[8,960,1920]{2,1,0:T(8,128)(2,1)} %param.8, bf16[8,1920,64]{1,2,0:T(8,128)(2,1)S(1)} %reshape.90, f32[8,960]{1,0:T(8,128)S(1)} %convert_element_type.27), kind=kOutput, calls=%fused_computation.10 | convolution fusion | flops 3776839680 | bytes 33454080 | tf_op jit(solution)/shard_map/knj,knc->kjc/dot_general | solution.py:39
  173.4 11.6 %convert_element_type.31 = bf16[8,3,16,40,2,32]{3,2,1,5,4,0:T(8,128)(2,1)} reshape(bf16[8,1920,64]{1,2,0:T(8,128)(2,1)} %fusion.6) | data formatting | bytes 3932160 | tf_op jit(solution)/shard_map/convert_element_type | solution.py:43
  185.0 11.7 %copy.25 = bf16[8,3,16,40,2,32]{5,3,1,0,4,2:T(8,128)(2,1)} copy(bf16[8,3,16,40,2,32]{3,2,1,5,4,0:T(8,128)(2,1)} %convert_element_type.31) | data formatting | bytes 3932160 | tf_op jit(solution)/shard_map/convert_element_type | solution.py:43
  196.6 13.2 %all_to_all.13 = bf16[32,1,30720]{2,1,0:T(2,128)(2,1)} reshape(bf16[16,2,8,3,40,32]{5,4,3,2,1,0:T(8,128)(2,1)} %bitcast.40) | data formatting | bytes 3932160 | tf_op jit(solution)/shard_map/all_to_all | solution.py:44
  209.8 12.7 %reduce.3 = bf16[32,30720]{1,0:T(8,128)(2,1)S(1)} reduce(bf16[32,1,30720]{2,1,0:T(2,128)(2,1)} %all_to_all.13, bf16[]{:T(256)} %broadcast.108), dimensions={1}, to_apply=%all_to_all.13.reduce_sub_computation | reduce | bytes 3932162 | tf_op jit(solution)/shard_map/all_to_all | solution.py:44
  222.5 2.4 reshape.122
  224.9 3.9 %all-to-all-start.1 = ((bf16[32,2,15360]{2,1,0:T(2,128)(2,1)}), bf16[32,2,15360]{2,1,0:T(2,128)(2,1)S(1)}, u32[]{:S(2)}, u32[]{:S(2)}) async-start(bf16[32,2,15360]{2,1,0:T(2,128)(2,1)} %reshape.122), calls=%async_computation.1 | async-start | bytes 3932160 | tf_op jit(solution)/shard_map/all_to_all | solution.py:44
  228.9 45.6 %all-to-all-done.1 = bf16[32,2,15360]{2,1,0:T(2,128)(2,1)S(1)} async-done(((bf16[32,2,15360]{2,1,0:T(2,128)(2,1)}), bf16[32,2,15360]{2,1,0:T(2,128)(2,1)S(1)}, u32[]{:S(2)}, u32[]{:S(2)}) %all-to-all-start.1) | async-done | bytes 1966112 | tf_op jit(solution)/shard_map/all_to_all | solution.py:44
  274.4 6.4 %reshape.123 = bf16[32,1,30720]{2,1,0:T(2,128)(2,1)} reshape(bf16[32,2,15360]{2,1,0:T(2,128)(2,1)S(1)} %all-to-all-done.1) | data formatting | bytes 3932160
  280.8 12.1 %reduce.1 = bf16[32,30720]{1,0:T(8,128)(2,1)S(1)} reduce(bf16[32,1,30720]{2,1,0:T(2,128)(2,1)} %reshape.123, bf16[]{:T(256)} %constant.44), dimensions={1}, to_apply=%all_to_all.12.reduce_sub_computation | reduce | bytes 3932162 | tf_op jit(solution)/shard_map/all_to_all | solution.py:44
  292.9 7.6 %squeeze_reshape.3 = bf16[16,2,8,3,40,32]{5,4,3,2,1,0:T(8,128)(2,1)} reshape(bf16[32,30720]{1,0:T(8,128)(2,1)S(1)} %reduce.1) | data formatting | bytes 3932160 | tf_op jit(solution)/shard_map/squeeze;reshape | solution.py:46
  300.5 10.8 %copy.27 = bf16[16,2,8,3,40,32]{4,5,3,2,1,0:T(8,128)(2,1)} copy(bf16[16,2,8,3,40,32]{5,4,3,2,1,0:T(8,128)(2,1)} %squeeze_reshape.3) | data formatting | bytes 3932160 | tf_op jit(solution)/shard_map/squeeze;reshape | solution.py:46
  311.2 6.8 %gather_fusion.2 = bf16[16,2,8,3,40,32]{4,5,3,2,1,0:T(8,128)(2,1)} fusion(bf16[16,2,8,3,40,32]{4,5,3,2,1,0:T(8,128)(2,1)} %copy.27, s32[1024]{0:T(1024)S(1)} %pad_clamp_fusion), kind=kCustom, calls=%fused_computation.2 | custom fusion | bytes 3932224 | tf_op jit(solution)/shard_map/jit(_take)/gather | solution.py:47
  318.0 6.2 %fusion.3 = bf16[16,3,40,16,32]{2,4,3,1,0:T(8,128)(2,1)} fusion(bf16[16,16,3,40,32]{3,4,2,1,0:T(8,128)(2,1)} %bitcast.38, pred[16]{0:T(512)(128)(4,1)S(1)} %compare_and_fusion.1), kind=kLoop, calls=%fused_computation.7 | loop fusion | flops 983040 | bytes 3932176 | tf_op jit(solution)/shard_map/transpose | solution.py:49
  (18 shorter events, 0.1 us)
Async XLA Ops:
  0.0 1.5 copy-start
  42.9 14.2 %copy-start.2 = (s32[8,960]{1,0:T(8,128)S(1)}, s32[8,960]{1,0:T(8,128)}, u32[]{:S(2)}) copy-start(s32[8,960]{1,0:T(8,128)} %param.9) | copy-start | bytes 92164
  49.6 53.2 %all-to-all-start = ((bf16[32,2,15360]{2,1,0:T(2,128)(2,1)}), bf16[32,2,15360]{2,1,0:T(2,128)(2,1)S(1)}, u32[]{:S(2)}, u32[]{:S(2)}) async-start(bf16[32,2,15360]{2,1,0:T(2,128)(2,1)} %reshape.120), calls=%async_computation | async-start | bytes 3932160 | tf_op jit(solution)/shard_map/all_to_all | solution.py:30
  209.8 19.0 %copy-start.3 = (s32[16]{0:T(128)S(1)}, s32[16]{0:T(128)}, u32[]{:S(2)}) copy-start(s32[16]{0:T(128)} %param.7) | copy-start | bytes 196
  224.9 49.5 %all-to-all-start.1 = ((bf16[32,2,15360]{2,1,0:T(2,128)(2,1)}), bf16[32,2,15360]{2,1,0:T(2,128)(2,1)S(1)}, u32[]{:S(2)}, u32[]{:S(2)}) async-start(bf16[32,2,15360]{2,1,0:T(2,128)(2,1)} %reshape.122), calls=%async_computation.1 | async-start | bytes 3932160 | tf_op jit(solution)/shard_map/all_to_all | solution.py:44
  318.0 6.2 %copy-start.1 = (bf16[20,16]{0,1:T(8,128)(2,1)S(1)}, bf16[20,16]{0,1:T(8,128)(2,1)}, u32[]{:S(2)}) copy-start(bf16[20,16]{0,1:T(8,128)(2,1)} %param.6) | copy-start | bytes 1924
where the time goes:
time: 326 us; the launch traced here: 324 us
  local copies, waits for them, and re-layouts  136 us (42%)
  waiting for transfers between devices  91.3 us (28%)
  other arithmetic  49.1 us (15%)
  matrix products  36 us (11%)
  starting transfers between devices  11.4 us (3%)
    all_to_all x1, waiting for transfers between devices, body(): incoming = lax.all_to_all(outgoing, AXES, 0, 0, tiled=True)  45.7 us
    all_to_all x1, waiting for transfers between devices, body(): lax.all_to_all(synth.reshape(n_lat * n_tm, -1), AXES, 0, 0, tiled=True)  45.6 us
    gather x3, local copies, waits for them, and re-layouts, body(): outgoing = jnp.take(projected, dest_order, axis=0)  27.8 us
    all_to_all x2, other arithmetic, body(): lax.all_to_all(synth.reshape(n_lat * n_tm, -1), AXES, 0, 0, tiled=True)  24.8 us
    dot_general x1, matrix products, body(): jnp.einsum('knj,knc->kjc', hough_table, kept, preferred_element_type=jnp....  24 us
    convert_element_type x2, local copies, waits for them, and re-layouts, body(): synth = synth.astype(jnp.bfloat16)  23.3 us
    another operation x2, local copies, waits for them, and re-layouts, body(): returned = returned.sum(axis=1) if group_size > 1 else returned[:, 0]  18.3 us
    unnamed x12, local copies, waits for them, and re-layouts  17.6 us
  transfers between devices with their start and end apart: 2, of which 2 were waited for; matrix products, arithmetic and copies ran while one was open for 0% of the time, Pallas kernels for 0%

commit v1 on v0

--- a/solution.py
+++ b/solution.py
@@ -20,16 +20,18 @@
     variables, lev, lat_count, _, span = fields.shape
     kmodes = vmodes.shape[1]
     k_loc = kmodes // n_tm
+    block = lat_count * span
+    flat = fields.transpose(3, 0, 1, 2, 4).reshape(orders, variables, lev, block)
+    dest_order = order_of_slot(owner_map)[jnp.arange(n_lat, dtype=jnp.int32) // group_size]
+    picked = jnp.take(flat, dest_order, axis=0, mode="clip")
     vm = vmodes.reshape(lev, n_tm, k_loc)
-    projected = jnp.einsum(
-        "vlamc,lus->muvsac", fields, vm, preferred_element_type=jnp.float32
+    outgoing = jnp.einsum(
+        "jvlx,lus->jusvx", picked, vm, preferred_element_type=jnp.float32
     ).astype(jnp.bfloat16)
-    dest_order = order_of_slot(owner_map)[jnp.arange(n_lat, dtype=jnp.int32) // group_size]
-    outgoing = jnp.take(projected, dest_order, axis=0)
-    outgoing = outgoing.reshape(n_lat * n_tm, -1)
+    outgoing = outgoing.reshape(n_lat * n_tm, k_loc * variables, block)
     incoming = lax.all_to_all(outgoing, AXES, 0, 0, tiled=True)
-    incoming = incoming.reshape(n_lat, n_tm, variables, k_loc, lat_count, span)
-    columns = incoming.transpose(3, 2, 0, 4, 1, 5).reshape(
+    incoming = incoming.reshape(n_lat, n_tm, k_loc, variables, lat_count, span)
+    columns = incoming.transpose(2, 3, 0, 4, 1, 5).reshape(
         k_loc, variables * n_lat * lat_count, n_tm * span
     )
     coefficients = jnp.einsum(
@@ -41,10 +43,11 @@
     synth = synth.transpose(2, 4, 0, 1, 3, 5)
     if group_size == 1:
         synth = synth.astype(jnp.bfloat16)
-    returned = lax.all_to_all(synth.reshape(n_lat * n_tm, -1), AXES, 0, 0, tiled=True)
+    synth = synth.reshape(n_lat * n_tm, k_loc * variables, block)
+    returned = lax.all_to_all(synth, AXES, 0, 0, tiled=True)
     returned = returned.reshape(orders, group_size, n_tm, k_loc, variables, lat_count, span)
     returned = returned.sum(axis=1) if group_size > 1 else returned[:, 0]
-    result = jnp.take(returned, owner_map, axis=0)
+    result = jnp.take(returned, owner_map, axis=0, mode="clip")
     result = result.reshape(orders, kmodes, variables, lat_count, span)
     return result.transpose(1, 2, 3, 0, 4).astype(jnp.bfloat16)
 

time: 326 us -> 255 us (0.78)
  other arithmetic: 49.1 us -> 0.14 us
  local copies, waits for them, and re-layouts: 136 us -> 123 us
  matrix products: 36 us -> 26.6 us
    reshape x2 -> x8, local copies, waits for them, and re-layouts: 16.5 us -> 60.7 us  [the longest x2 23.1 us: body(): fields.transpose(3, 0, 1, 2, 4).reshape(orders, variables, lev, block)]
    all_to_all x3 -> x0, other arithmetic: 36.9 us -> none  [the longest x2 24.8 us: body(): lax.all_to_all(synth.reshape(n_lat * n_tm, -1), AXES, 0, 0, tiled=True)]
    gather x4 -> x2, local copies, waits for them, and re-layouts: 34.6 us -> 9.13 us  [the longest x1 6.79 us: body(): result = jnp.take(returned, owner_map, axis=0, mode='clip')]
    unnamed x12 -> x8, local copies, waits for them, and re-layouts: 17.6 us -> 0.02 us
    all_to_all x1 -> x0, local copies, waits for them, and re-layouts: 13.2 us -> none  [body(): lax.all_to_all(synth.reshape(n_lat * n_tm, -1), AXES, 0, 0, tiled=True)]
    dot_general x1, matrix products: 11.9 us -> 2.49 us  [body(): jnp.einsum('jvlx,lus->jusvx', picked, vm, preferred_element_type=jnp.floa...]
    transpose x1 -> x0, other arithmetic: 6.17 us -> none  [body(): return result.transpose(1, 2, 3, 0, 4).astype(jnp.bfloat16)]
    select_n x4 -> x0, other arithmetic: 5.24 us -> none  [the longest x3 5.23 us: body(): outgoing = jnp.take(projected, dest_order, axis=0)]
where the time goes in v1:
time: 255 us; the launch traced here: 253 us
  local copies, waits for them, and re-layouts  123 us (48%)
  waiting for transfers between devices  91.5 us (36%)
  matrix products  26.6 us (10%)
  starting transfers between devices  11.2 us (4%)
    all_to_all x1, waiting for transfers between devices, body(): incoming = lax.all_to_all(outgoing, AXES, 0, 0, tiled=True)  45.8 us
    all_to_all x1, waiting for transfers between devices, body(): returned = lax.all_to_all(synth, AXES, 0, 0, tiled=True)  45.7 us
    dot_general x1, matrix products, body(): jnp.einsum('knj,knc->kjc', hough_table, kept, preferred_element_type=jnp....  24.1 us
    convert_element_type x2, local copies, waits for them, and re-layouts, body(): synth = synth.astype(jnp.bfloat16)  23.3 us
    reshape x2, local copies, waits for them, and re-layouts, body(): fields.transpose(3, 0, 1, 2, 4).reshape(orders, variables, lev, block)  23.1 us
    another operation x2, local copies, waits for them, and re-layouts, body(): returned = returned.sum(axis=1) if group_size > 1 else returned[:, 0]  18 us
    transpose x1, local copies, waits for them, and re-layouts, body(): incoming.transpose(2, 3, 0, 4, 1, 5)  11.6 us
    reshape x1, local copies, waits for them, and re-layouts, body(): synth = synth.reshape(n_lat * n_tm, k_loc * variables, block)  9.86 us
  transfers between devices with their start and end apart: 2, of which 2 were waited for; matrix products, arithmetic and copies ran while one was open for 0% of the time, Pallas kernels for 0%

profile of v1, /device:TPU:0, one launch (start us, length us, event | category | flops | bytes accessed | tf_op | source)
XLA Modules:
  0.0 252.9 jit_solution(14160212759625856349)
XLA Ops:
  0.0 0.0 copy-start
  0.0 12.0 %copy.40 = bf16[16,3,20,40,32]{4,3,2,1,0:T(8,128)(2,1)} copy(bf16[16,3,20,40,32]{3,4,0,2,1:T(8,128)(2,1)} %bitcast.39) | data formatting | bytes 4915200 | tf_op jit(solution)/shard_map/reshape | solution.py:24
  12.0 0.0 copy-start.3
  12.0 11.1 %reshape.61 = bf16[16,3,20,1280]{3,2,1,0:T(8,128)(2,1)S(1)} reshape(bf16[16,3,20,40,32]{4,3,2,1,0:T(8,128)(2,1)} %copy.40) | data formatting | bytes 4915200 | tf_op jit(solution)/shard_map/reshape | solution.py:24
  23.1 0.0 copy-done.3
  23.1 0.1 select_reduce_fusion
  23.2 0.7 gather_fusion
  23.9 2.3 gather_fusion.1
  26.2 0.0 copy-done
  26.2 2.5 fusion
  28.7 1.4 copy.41
  30.1 2.8 %reshape.62 = bf16[32,24,1280]{2,1,0:T(8,128)(2,1)} reshape(bf16[16,2,8,3,1280]{4,3,2,1,0:T(4,128)(2,1)S(1)} %copy.41) | data formatting | bytes 3932160 | tf_op jit(solution)/shard_map/reshape | solution.py:31
  32.9 0.0 copy-start.2
  32.9 7.3 %all-to-all-start = ((bf16[32,24,1280]{2,1,0:T(8,128)(2,1)}), bf16[32,24,1280]{2,1,0:T(8,128)(2,1)S(1)}, u32[]{:S(2)}, u32[]{:S(2)}) async-start(bf16[32,24,1280]{2,1,0:T(8,128)(2,1)} %reshape.62), calls=%async_computation | async-start | bytes 3932160 | tf_op jit(solution)/shard_map/all_to_all | solution.py:32
  40.3 0.0 copy-done.2
  40.3 45.8 %all-to-all-done = bf16[32,24,1280]{2,1,0:T(8,128)(2,1)S(1)} async-done(((bf16[32,24,1280]{2,1,0:T(8,128)(2,1)}), bf16[32,24,1280]{2,1,0:T(8,128)(2,1)S(1)}, u32[]{:S(2)}, u32[]{:S(2)}) %all-to-all-start) | async-done | bytes 1966112 | tf_op jit(solution)/shard_map/all_to_all | solution.py:32
  86.1 7.2 %reshape.29 = bf16[16,2,8,3,40,32]{5,4,3,2,1,0:T(8,128)(2,1)} reshape(bf16[32,24,1280]{2,1,0:T(8,128)(2,1)S(1)} %all-to-all-done) | data formatting | bytes 3932160 | tf_op jit(solution)/shard_map/reshape | solution.py:33
  93.4 11.6 %copy.34 = bf16[8,3,16,40,2,32]{3,2,1,5,4,0:T(8,128)(2,1)} copy(bf16[8,3,16,40,2,32]{5,3,1,0,4,2:T(8,128)(2,1)} %bitcast.37) | data formatting | bytes 3932160 | tf_op jit(solution)/shard_map/transpose | solution.py:34
  105.0 8.9 %reshape.30 = bf16[8,1920,64]{1,2,0:T(8,128)(2,1)S(1)} reshape(bf16[8,3,16,40,2,32]{3,2,1,5,4,0:T(8,128)(2,1)} %copy.34) | data formatting | bytes 3932160 | tf_op jit(solution)/shard_map/reshape | solution.py:34
  113.9 24.1 %fusion.2 = bf16[8,1920,64]{1,2,0:T(8,128)(2,1)} fusion(bf16[8,960,1920]{2,1,0:T(8,128)(2,1)} %param.8, bf16[8,1920,64]{1,2,0:T(8,128)(2,1)S(1)} %reshape.30, f32[8,960]{1,0:T(8,128)S(1)} %convert_element_type.27), kind=kOutput, calls=%fused_computation.8 | convolution fusion | flops 3776839680 | bytes 33454080 | tf_op jit(solution)/shard_map/knj,knc->kjc/dot_general | solution.py:41
  137.9 11.6 %convert_element_type.31 = bf16[8,3,16,40,2,32]{3,2,1,5,4,0:T(8,128)(2,1)} reshape(bf16[8,1920,64]{1,2,0:T(8,128)(2,1)} %fusion.2) | data formatting | bytes 3932160 | tf_op jit(solution)/shard_map/convert_element_type | solution.py:45
  149.5 11.7 %copy.35 = bf16[8,3,16,40,2,32]{5,3,1,0,4,2:T(8,128)(2,1)} copy(bf16[8,3,16,40,2,32]{3,2,1,5,4,0:T(8,128)(2,1)} %convert_element_type.31) | data formatting | bytes 3932160 | tf_op jit(solution)/shard_map/convert_element_type | solution.py:45
  161.2 9.9 %reshape.31 = bf16[32,24,1280]{2,1,0:T(8,128)(2,1)} reshape(bf16[16,2,8,3,40,32]{5,4,3,2,1,0:T(8,128)(2,1)} %bitcast.38) | data formatting | bytes 3932160 | tf_op jit(solution)/shard_map/reshape | solution.py:46
  171.1 3.8 %all-to-all-start.1 = ((bf16[32,24,1280]{2,1,0:T(8,128)(2,1)}), bf16[32,24,1280]{2,1,0:T(8,128)(2,1)S(1)}, u32[]{:S(2)}, u32[]{:S(2)}) async-start(bf16[32,24,1280]{2,1,0:T(8,128)(2,1)} %reshape.31), calls=%async_computation.1 | async-start | bytes 3932160 | tf_op jit(solution)/shard_map/all_to_all | solution.py:47
  174.9 45.7 %all-to-all-done.1 = bf16[32,24,1280]{2,1,0:T(8,128)(2,1)S(1)} async-done(((bf16[32,24,1280]{2,1,0:T(8,128)(2,1)}), bf16[32,24,1280]{2,1,0:T(8,128)(2,1)S(1)}, u32[]{:S(2)}, u32[]{:S(2)}) %all-to-all-start.1) | async-done | bytes 1966112 | tf_op jit(solution)/shard_map/all_to_all | solution.py:47
  220.6 7.2 %squeeze_reshape.3 = bf16[16,2,8,3,40,32]{5,4,3,2,1,0:T(8,128)(2,1)} reshape(bf16[32,24,1280]{2,1,0:T(8,128)(2,1)S(1)} %all-to-all-done.1) | data formatting | bytes 3932160 | tf_op jit(solution)/shard_map/squeeze;reshape | solution.py:49
  227.8 10.8 %copy.36 = bf16[16,2,8,3,40,32]{4,5,3,2,1,0:T(8,128)(2,1)} copy(bf16[16,2,8,3,40,32]{5,4,3,2,1,0:T(8,128)(2,1)} %squeeze_reshape.3) | data formatting | bytes 3932160 | tf_op jit(solution)/shard_map/squeeze;reshape | solution.py:49
  238.6 6.8 %gather_fusion.2 = bf16[16,2,8,3,40,32]{4,5,3,2,1,0:T(8,128)(2,1)} fusion(bf16[16,2,8,3,40,32]{4,5,3,2,1,0:T(8,128)(2,1)} %copy.36, s32[1024]{0:T(1024)S(1)} %pad_clamp_fusion), kind=kCustom, calls=%fused_computation.2 | custom fusion | bytes 3932224 | tf_op jit(solution)/shard_map/jit(_take)/gather | solution.py:50
  245.4 0.0 copy-start.1
  245.4 7.5 %copy.45 = bf16[16,16,3,40,32]{3,4,0,2,1:T(8,128)(2,1)} copy(bf16[16,16,3,40,32]{3,4,2,1,0:T(8,128)(2,1)} %bitcast.36) | data formatting | bytes 3932160 | tf_op jit(solution)/shard_map/reshape | solution.py:51
  252.9 0.0 copy-done.1
  (5 shorter events, 0.0 us)
Async XLA Ops:
  0.0 26.2 %copy-start = (bf16[20,16]{0,1:T(8,128)(2,1)S(1)}, bf16[20,16]{0,1:T(8,128)(2,1)}, u32[]{:S(2)}) copy-start(bf16[20,16]{0,1:T(8,128)(2,1)} %param.6) | copy-start | bytes 1924
  12.0 11.1 %copy-start.3 = (s32[16]{0:T(128)S(1)}, s32[16]{0:T(128)}, u32[]{:S(2)}) copy-start(s32[16]{0:T(128)} %param.7) | copy-start | bytes 196
  32.9 7.3 %copy-start.2 = (s32[8,960]{1,0:T(8,128)S(1)}, s32[8,960]{1,0:T(8,128)}, u32[]{:S(2)}) copy-start(s32[8,960]{1,0:T(8,128)} %param.9) | copy-start | bytes 92164
  32.9 53.2 %all-to-all-start = ((bf16[32,24,1280]{2,1,0:T(8,128)(2,1)}), bf16[32,24,1280]{2,1,0:T(8,128)(2,1)S(1)}, u32[]{:S(2)}, u32[]{:S(2)}) async-start(bf16[32,24,1280]{2,1,0:T(8,128)(2,1)} %reshape.62), calls=%async_computation | async-start | bytes 3932160 | tf_op jit(solution)/shard_map/all_to_all | solution.py:32
  171.1 49.5 %all-to-all-start.1 = ((bf16[32,24,1280]{2,1,0:T(8,128)(2,1)}), bf16[32,24,1280]{2,1,0:T(8,128)(2,1)S(1)}, u32[]{:S(2)}, u32[]{:S(2)}) async-start(bf16[32,24,1280]{2,1,0:T(8,128)(2,1)} %reshape.31), calls=%async_computation.1 | async-start | bytes 3932160 | tf_op jit(solution)/shard_map/all_to_all | solution.py:47
  245.4 7.5 %copy-start.1 = (bf16[20,16]{0,1:T(8,128)(2,1)S(1)}, bf16[20,16]{0,1:T(8,128)(2,1)}, u32[]{:S(2)}) copy-start(bf16[20,16]{0,1:T(8,128)(2,1)} %param.6) | copy-start | bytes 1924

commit v2 on v1

--- a/solution.py
+++ b/solution.py
@@ -21,7 +21,7 @@
     kmodes = vmodes.shape[1]
     k_loc = kmodes // n_tm
     block = lat_count * span
-    flat = fields.transpose(3, 0, 1, 2, 4).reshape(orders, variables, lev, block)
+    flat = fields.transpose(3, 0, 1, 4, 2).reshape(orders, variables, lev, block)
     dest_order = order_of_slot(owner_map)[jnp.arange(n_lat, dtype=jnp.int32) // group_size]
     picked = jnp.take(flat, dest_order, axis=0, mode="clip")
     vm = vmodes.reshape(lev, n_tm, k_loc)
@@ -30,26 +30,26 @@
     ).astype(jnp.bfloat16)
     outgoing = outgoing.reshape(n_lat * n_tm, k_loc * variables, block)
     incoming = lax.all_to_all(outgoing, AXES, 0, 0, tiled=True)
-    incoming = incoming.reshape(n_lat, n_tm, k_loc, variables, lat_count, span)
-    columns = incoming.transpose(2, 3, 0, 4, 1, 5).reshape(
-        k_loc, variables * n_lat * lat_count, n_tm * span
+    incoming = incoming.reshape(n_lat, n_tm, k_loc, variables, span, lat_count)
+    columns = incoming.transpose(2, 1, 4, 3, 0, 5).reshape(
+        k_loc, n_tm * span, variables * n_lat * lat_count
     )
     coefficients = jnp.einsum(
-        "knj,kjc->knc", hough_table, columns, preferred_element_type=jnp.float32
+        "knj,kcj->knc", hough_table, columns, preferred_element_type=jnp.float32
     )
     kept = (coefficients * keep_mask.astype(jnp.float32)[:, :, None]).astype(jnp.bfloat16)
-    synth = jnp.einsum("knj,knc->kjc", hough_table, kept, preferred_element_type=jnp.float32)
-    synth = synth.reshape(k_loc, variables, n_lat, lat_count, n_tm, span)
-    synth = synth.transpose(2, 4, 0, 1, 3, 5)
+    synth = jnp.einsum("knj,knc->kcj", hough_table, kept, preferred_element_type=jnp.float32)
+    synth = synth.reshape(k_loc, n_tm, span, variables, n_lat, lat_count)
+    synth = synth.transpose(4, 1, 0, 3, 2, 5)
     if group_size == 1:
         synth = synth.astype(jnp.bfloat16)
     synth = synth.reshape(n_lat * n_tm, k_loc * variables, block)
     returned = lax.all_to_all(synth, AXES, 0, 0, tiled=True)
-    returned = returned.reshape(orders, group_size, n_tm, k_loc, variables, lat_count, span)
+    returned = returned.reshape(orders, group_size, n_tm, k_loc, variables, span, lat_count)
     returned = returned.sum(axis=1) if group_size > 1 else returned[:, 0]
     result = jnp.take(returned, owner_map, axis=0, mode="clip")
-    result = result.reshape(orders, kmodes, variables, lat_count, span)
-    return result.transpose(1, 2, 3, 0, 4).astype(jnp.bfloat16)
+    result = result.reshape(orders, kmodes, variables, span, lat_count)
+    return result.transpose(1, 2, 4, 0, 3).astype(jnp.bfloat16)
 
 
 def solution(mesh):

time: 255 us -> 240 us (0.941)
  local copies, waits for them, and re-layouts: 123 us -> 109 us
    transpose x1 -> x0, local copies, waits for them, and re-layouts: 11.6 us -> none  [body(): incoming.transpose(2, 3, 0, 4, 1, 5)]
    reshape x5 -> x6, local copies, waits for them, and re-layouts: 46.7 us -> 53.7 us  [the longest x2 21.9 us: body(): incoming = incoming.reshape(n_lat, n_tm, k_loc, variables, span, lat_count)]
    another operation x2 -> x1, local copies, waits for them, and re-layouts: 18 us -> 12.5 us  [body(): returned = returned.sum(axis=1) if group_size > 1 else returned[:, 0]]
    convert_element_type x2, local copies, waits for them, and re-layouts: 23.3 us -> 18.6 us  [body(): synth = synth.astype(jnp.bfloat16)]
where the time goes in v2:
time: 240 us; the launch traced here: 239 us
  local copies, waits for them, and re-layouts  109 us (45%)
  waiting for transfers between devices  91.5 us (38%)
  matrix products  26.6 us (11%)
  starting transfers between devices  11.2 us (5%)
    all_to_all x1, waiting for transfers between devices, body(): returned = lax.all_to_all(synth, AXES, 0, 0, tiled=True)  45.9 us
    all_to_all x1, waiting for transfers between devices, body(): incoming = lax.all_to_all(outgoing, AXES, 0, 0, tiled=True)  45.7 us
    dot_general x1, matrix products, body(): jnp.einsum('knj,knc->kcj', hough_table, kept, preferred_element_type=jnp....  24.1 us
    reshape x2, local copies, waits for them, and re-layouts, body(): incoming = incoming.reshape(n_lat, n_tm, k_loc, variables, span, lat_count)  21.9 us
    convert_element_type x2, local copies, waits for them, and re-layouts, body(): synth = synth.astype(jnp.bfloat16)  18.6 us
    reshape x2, local copies, waits for them, and re-layouts, body(): fields.transpose(3, 0, 1, 4, 2).reshape(orders, variables, lev, block)  15.4 us
    another operation x1, local copies, waits for them, and re-layouts, body(): returned = returned.sum(axis=1) if group_size > 1 else returned[:, 0]  12.5 us
    reshape x1, local copies, waits for them, and re-layouts, body(): synth = synth.reshape(n_lat * n_tm, k_loc * variables, block)  10.6 us
  transfers between devices with their start and end apart: 2, of which 2 were waited for; matrix products, arithmetic and copies ran while one was open for 0% of the time, Pallas kernels for 0%

profile of v2, /device:TPU:0, one launch (start us, length us, event | category | flops | bytes accessed | tf_op | source)
XLA Modules:
  0.0 238.9 jit_solution(18005413776725580513)
XLA Ops:
  0.0 0.0 copy-start
  0.0 12.9 %reshape.26 = bf16[16,3,20,1280]{3,0,2,1:T(8,128)(2,1)} reshape(bf16[16,3,20,32,40]{4,3,0,2,1:T(8,128)(2,1)} %bitcast.39) | data formatting | bytes 4915200 | tf_op jit(solution)/shard_map/reshape | solution.py:24
  12.9 0.0 copy-start.3
  12.9 2.5 %copy.22 = bf16[16,3,20,1280]{3,2,1,0:T(8,128)(2,1)S(1)} copy(bf16[16,3,20,1280]{3,0,2,1:T(8,128)(2,1)} %reshape.26) | data formatting | bytes 4915200 | tf_op jit(solution)/shard_map/reshape | solution.py:24
  15.4 0.0 copy-done.3
  15.4 0.1 select_reduce_fusion
  15.5 0.7 gather_fusion
  16.2 2.3 gather_fusion.1
  18.5 0.0 copy-done
  18.6 2.5 %fusion = bf16[16,2,8,3,1280]{4,2,1,3,0:T(8,128)(2,1)S(1)} fusion(bf16[16,3,20,1280]{3,2,1,0:T(8,128)(2,1)} %gather_fusion.1, bf16[20,16]{0,1:T(8,128)(2,1)S(1)} %copy-done), kind=kOutput, calls=%fused_computation.8 | convolution fusion | flops 40304640 | bytes 4424320 | tf_op jit(solution)/shard_map/jvlx,lus->jusvx/dot_general | solution.py:28
  21.0 1.4 copy.30
  22.4 2.8 %reshape.61 = bf16[32,24,1280]{2,1,0:T(8,128)(2,1)} reshape(bf16[16,2,8,3,1280]{4,3,2,1,0:T(4,128)(2,1)S(1)} %copy.30) | data formatting | bytes 3932160 | tf_op jit(solution)/shard_map/reshape | solution.py:31
  25.2 0.0 copy-start.2
  25.2 7.5 %all-to-all-start = ((bf16[32,24,1280]{2,1,0:T(8,128)(2,1)}), bf16[32,24,1280]{2,1,0:T(8,128)(2,1)S(1)}, u32[]{:S(2)}, u32[]{:S(2)}) async-start(bf16[32,24,1280]{2,1,0:T(8,128)(2,1)} %reshape.61), calls=%async_computation | async-start | bytes 3932160 | tf_op jit(solution)/shard_map/all_to_all | solution.py:32
  32.7 0.0 copy-done.2
  32.8 45.7 %all-to-all-done = bf16[32,24,1280]{2,1,0:T(8,128)(2,1)S(1)} async-done(((bf16[32,24,1280]{2,1,0:T(8,128)(2,1)}), bf16[32,24,1280]{2,1,0:T(8,128)(2,1)S(1)}, u32[]{:S(2)}, u32[]{:S(2)}) %all-to-all-start) | async-done | bytes 1966112 | tf_op jit(solution)/shard_map/all_to_all | solution.py:32
  78.4 12.5 %reshape.29 = bf16[16,2,8,3,32,40]{5,4,3,2,1,0:T(8,128)(2,1)} reshape(bf16[32,24,1280]{2,1,0:T(8,128)(2,1)S(1)} %all-to-all-done) | data formatting | bytes 3932160 | tf_op jit(solution)/shard_map/reshape | solution.py:33
  90.9 9.5 %copy.37 = bf16[16,2,8,3,32,40]{5,0,3,4,1,2:T(8,128)(2,1)} copy(bf16[16,2,8,3,32,40]{5,4,3,2,1,0:T(8,128)(2,1)} %reshape.29) | data formatting | bytes 3932160 | tf_op jit(solution)/shard_map/reshape | solution.py:33
  100.4 8.9 %reshape.30 = bf16[8,64,1920]{2,1,0:T(8,128)(2,1)S(1)} reshape(bf16[8,2,32,3,16,40]{5,4,3,2,1,0:T(8,128)(2,1)} %bitcast.37) | data formatting | bytes 3932160 | tf_op jit(solution)/shard_map/reshape | solution.py:34
  109.3 24.1 %convolution_convert_fusion.1 = bf16[8,64,1920]{2,1,0:T(8,128)(2,1)} fusion(bf16[8,960,1920]{2,1,0:T(8,128)(2,1)} %param.8, bf16[8,64,1920]{2,1,0:T(8,128)(2,1)S(1)} %reshape.30, f32[8,960]{1,0:T(8,128)S(1)} %convert_element_type.24), kind=kOutput, calls=%fused_computation.7 | convolution fusion | flops 3776839680 | bytes 33454080 | tf_op jit(solution)/shard_map/knj,knc->kcj/dot_general | solution.py:41
  133.3 11.6 %convert_element_type.27 = bf16[8,2,32,3,16,40]{5,4,3,2,1,0:T(8,128)(2,1)} reshape(bf16[8,64,1920]{2,1,0:T(8,128)(2,1)} %convolution_convert_fusion.1) | data formatting | bytes 3932160 | tf_op jit(solution)/shard_map/convert_element_type | solution.py:45
  144.9 7.1 %copy.36 = bf16[8,2,32,3,16,40]{5,2,3,0,1,4:T(8,128)(2,1)} copy(bf16[8,2,32,3,16,40]{5,4,3,2,1,0:T(8,128)(2,1)} %convert_element_type.27) | data formatting | bytes 3932160 | tf_op jit(solution)/shard_map/convert_element_type | solution.py:45
  152.0 10.6 %reshape.31 = bf16[32,24,1280]{2,1,0:T(8,128)(2,1)} reshape(bf16[16,2,8,3,32,40]{5,4,3,2,1,0:T(8,128)(2,1)} %bitcast.38) | data formatting | bytes 3932160 | tf_op jit(solution)/shard_map/reshape | solution.py:46
  162.6 3.7 %all-to-all-start.1 = ((bf16[32,24,1280]{2,1,0:T(8,128)(2,1)}), bf16[32,24,1280]{2,1,0:T(8,128)(2,1)S(1)}, u32[]{:S(2)}, u32[]{:S(2)}) async-start(bf16[32,24,1280]{2,1,0:T(8,128)(2,1)} %reshape.31), calls=%async_computation.1 | async-start | bytes 3932160 | tf_op jit(solution)/shard_map/all_to_all | solution.py:47
  166.3 45.9 %all-to-all-done.1 = bf16[32,24,1280]{2,1,0:T(8,128)(2,1)S(1)} async-done(((bf16[32,24,1280]{2,1,0:T(8,128)(2,1)}), bf16[32,24,1280]{2,1,0:T(8,128)(2,1)S(1)}, u32[]{:S(2)}, u32[]{:S(2)}) %all-to-all-start.1) | async-done | bytes 1966112 | tf_op jit(solution)/shard_map/all_to_all | solution.py:47
  212.2 12.5 %squeeze_reshape.3 = bf16[16,2,8,3,32,40]{5,4,3,2,1,0:T(8,128)(2,1)} reshape(bf16[32,24,1280]{2,1,0:T(8,128)(2,1)S(1)} %all-to-all-done.1) | data formatting | bytes 3932160 | tf_op jit(solution)/shard_map/squeeze;reshape | solution.py:49
  224.6 6.8 %gather_fusion.2 = bf16[16,2,8,3,32,40]{5,4,3,2,1,0:T(8,128)(2,1)} fusion(bf16[16,2,8,3,32,40]{5,4,3,2,1,0:T(8,128)(2,1)} %squeeze_reshape.3, s32[1024]{0:T(1024)S(1)} %pad_clamp_fusion), kind=kCustom, calls=%fused_computation.2 | custom fusion | bytes 3932224 | tf_op jit(solution)/shard_map/jit(_take)/gather | solution.py:50
  231.4 0.0 copy-start.1
  231.4 7.5 %copy.35 = bf16[16,16,3,32,40]{4,3,0,2,1:T(8,128)(2,1)} copy(bf16[16,16,3,32,40]{4,3,2,1,0:T(8,128)(2,1)} %bitcast.36) | data formatting | bytes 3932160 | tf_op jit(solution)/shard_map/reshape | solution.py:51
  238.9 0.0 copy-done.1
  (5 shorter events, 0.0 us)
Async XLA Ops:
  0.0 18.6 %copy-start = (bf16[20,16]{0,1:T(8,128)(2,1)S(1)}, bf16[20,16]{0,1:T(8,128)(2,1)}, u32[]{:S(2)}) copy-start(bf16[20,16]{0,1:T(8,128)(2,1)} %param.6) | copy-start | bytes 1924
  12.9 2.5 %copy-start.3 = (s32[16]{0:T(128)S(1)}, s32[16]{0:T(128)}, u32[]{:S(2)}) copy-start(s32[16]{0:T(128)} %param.7) | copy-start | bytes 196
  25.2 7.5 %copy-start.2 = (s32[8,960]{1,0:T(8,128)S(1)}, s32[8,960]{1,0:T(8,128)}, u32[]{:S(2)}) copy-start(s32[8,960]{1,0:T(8,128)} %param.9) | copy-start | bytes 92164
  25.2 53.2 %all-to-all-start = ((bf16[32,24,1280]{2,1,0:T(8,128)(2,1)}), bf16[32,24,1280]{2,1,0:T(8,128)(2,1)S(1)}, u32[]{:S(2)}, u32[]{:S(2)}) async-start(bf16[32,24,1280]{2,1,0:T(8,128)(2,1)} %reshape.61), calls=%async_computation | async-start | bytes 3932160 | tf_op jit(solution)/shard_map/all_to_all | solution.py:32
  162.6 49.5 %all-to-all-start.1 = ((bf16[32,24,1280]{2,1,0:T(8,128)(2,1)}), bf16[32,24,1280]{2,1,0:T(8,128)(2,1)S(1)}, u32[]{:S(2)}, u32[]{:S(2)}) async-start(bf16[32,24,1280]{2,1,0:T(8,128)(2,1)} %reshape.31), calls=%async_computation.1 | async-start | bytes 3932160 | tf_op jit(solution)/shard_map/all_to_all | solution.py:47
  231.4 7.5 %copy-start.1 = (bf16[20,16]{0,1:T(8,128)(2,1)S(1)}, bf16[20,16]{0,1:T(8,128)(2,1)}, u32[]{:S(2)}) copy-start(bf16[20,16]{0,1:T(8,128)(2,1)} %param.6) | copy-start | bytes 1924

commit v3 on v2

--- a/solution.py
+++ b/solution.py
@@ -1,6 +1,7 @@
 import jax
 import jax.numpy as jnp
 from jax import lax
+from jax.experimental import pallas as pl
 from jax.sharding import PartitionSpec as P
 
 AXES = ("lat", "tm")
@@ -10,6 +11,32 @@
     ids = jnp.arange(owner_map.shape[0], dtype=jnp.int32)
     hit = owner_map[None, :] == ids[:, None]
     return jnp.sum(jnp.where(hit, ids[None, :], 0), axis=1).astype(jnp.int32)
+
+
+def filter_kernel(t_ref, x_ref, m_ref, o_ref):
+    table = t_ref[0]
+    coefficients = lax.dot_general(
+        x_ref[0], table, (((1,), (1,)), ((), ())), preferred_element_type=jnp.float32
+    )
+    kept = (coefficients * m_ref[0]).astype(jnp.bfloat16)
+    synth = jnp.dot(kept, table, preferred_element_type=jnp.float32)
+    o_ref[0] = synth.astype(o_ref.dtype)
+
+
+def filter_rows(hough_table, columns, mask, out_dtype):
+    k_loc, rows, width = hough_table.shape
+    cols = columns.shape[1]
+    return pl.pallas_call(
+        filter_kernel,
+        grid=(k_loc,),
+        in_specs=[
+            pl.BlockSpec((1, rows, width), lambda k: (k, 0, 0)),
+            pl.BlockSpec((1, cols, width), lambda k: (k, 0, 0)),
+            pl.BlockSpec((1, 1, rows), lambda k: (k, 0, 0)),
+        ],
+        out_specs=pl.BlockSpec((1, cols, width), lambda k: (k, 0, 0)),
+        out_shape=jax.ShapeDtypeStruct((k_loc, cols, width), out_dtype),
+    )(hough_table, columns, mask)
 
 
 def body(fields, vmodes, owner_map, hough_table, keep_mask):
@@ -34,15 +61,11 @@
     columns = incoming.transpose(2, 1, 4, 3, 0, 5).reshape(
         k_loc, n_tm * span, variables * n_lat * lat_count
     )
-    coefficients = jnp.einsum(
-        "knj,kcj->knc", hough_table, columns, preferred_element_type=jnp.float32
-    )
-    kept = (coefficients * keep_mask.astype(jnp.float32)[:, :, None]).astype(jnp.bfloat16)
-    synth = jnp.einsum("knj,knc->kcj", hough_table, kept, preferred_element_type=jnp.float32)
+    mask = keep_mask.astype(jnp.float32).reshape(k_loc, 1, -1)
+    out_dtype = jnp.bfloat16 if group_size == 1 else jnp.float32
+    synth = filter_rows(hough_table, columns, mask, out_dtype)
     synth = synth.reshape(k_loc, n_tm, span, variables, n_lat, lat_count)
     synth = synth.transpose(4, 1, 0, 3, 2, 5)
-    if group_size == 1:
-        synth = synth.astype(jnp.bfloat16)
     synth = synth.reshape(n_lat * n_tm, k_loc * variables, block)
     returned = lax.all_to_all(synth, AXES, 0, 0, tiled=True)
     returned = returned.reshape(orders, group_size, n_tm, k_loc, variables, span, lat_count)

time: 240 us -> 236 us (0.983)
  matrix products: 26.6 us -> 2.49 us
  Pallas kernels: 0 us -> 19.5 us
    dot_general x1 -> x0, matrix products: 24.1 us -> none  [body(): jnp.einsum('knj,knc->kcj', hough_table, kept, preferred_element_type=jnp....]
    pallas_call x0 -> x1, Pallas kernels: none -> 19.5 us  [filter_rows(): pl.pallas_call(filter_kernel, grid=(k_loc,), in_specs=[pl.BlockSpec((1, r...]
    reshape x0 -> x3, local copies, waits for them, and re-layouts: none -> 19.3 us  [the longest x2 18.6 us: body(): synth = synth.reshape(k_loc, n_tm, span, variables, n_lat, lat_count)]
    convert_element_type x2 -> x0, local copies, waits for them, and re-layouts: 18.6 us -> none  [body(): synth = synth.astype(jnp.bfloat16)]
    transpose x0 -> x1, local copies, waits for them, and re-layouts: none -> 9.48 us  [body(): incoming.transpose(2, 1, 4, 3, 0, 5)]
    reshape x2 -> x1, local copies, waits for them, and re-layouts: 21.9 us -> 12.5 us  [body(): incoming = incoming.reshape(n_lat, n_tm, k_loc, variables, span, lat_count)]
where the time goes in v3:
time: 236 us; the launch traced here: 235 us
  local copies, waits for them, and re-layouts  111 us (47%)
  waiting for transfers between devices  90.9 us (39%)
  Pallas kernels  19.5 us (8%)
  starting transfers between devices  11.1 us (5%)
  matrix products  2.49 us (1%)
    all_to_all x1, waiting for transfers between devices, body(): returned = lax.all_to_all(synth, AXES, 0, 0, tiled=True)  45.9 us
    all_to_all x1, waiting for transfers between devices, body(): incoming = lax.all_to_all(outgoing, AXES, 0, 0, tiled=True)  45 us
    pallas_call x1, Pallas kernels, filter_rows(): pl.pallas_call(filter_kernel, grid=(k_loc,), in_specs=[pl.BlockSpec((1, r...  19.5 us
    reshape x2, local copies, waits for them, and re-layouts, body(): synth = synth.reshape(k_loc, n_tm, span, variables, n_lat, lat_count)  18.6 us
    reshape x2, local copies, waits for them, and re-layouts, body(): fields.transpose(3, 0, 1, 4, 2).reshape(orders, variables, lev, block)  15.4 us
    reshape x1, local copies, waits for them, and re-layouts, body(): incoming = incoming.reshape(n_lat, n_tm, k_loc, variables, span, lat_count)  12.5 us
    another operation x1, local copies, waits for them, and re-layouts, body(): returned = returned.sum(axis=1) if group_size > 1 else returned[:, 0]  12.5 us
    reshape x1, local copies, waits for them, and re-layouts, body(): synth = synth.reshape(n_lat * n_tm, k_loc * variables, block)  10.6 us
  transfers between devices with their start and end apart: 2, of which 2 were waited for; matrix products, arithmetic and copies ran while one was open for 0% of the time, Pallas kernels for 0%

profile of v3, /device:TPU:0, one launch (start us, length us, event | category | flops | bytes accessed | tf_op | source)
XLA Modules:
  0.0 235.3 jit_solution(12443044648326954068)
XLA Ops:
  0.0 0.0 copy-start
  0.0 12.9 %reshape.29 = bf16[16,3,20,1280]{3,0,2,1:T(8,128)(2,1)} reshape(bf16[16,3,20,32,40]{4,3,0,2,1:T(8,128)(2,1)} %bitcast.34) | data formatting | bytes 4915200 | tf_op jit(solution)/shard_map/reshape | solution.py:51
  12.9 0.0 copy-start.3
  12.9 2.5 %copy.24 = bf16[16,3,20,1280]{3,2,1,0:T(8,128)(2,1)S(1)} copy(bf16[16,3,20,1280]{3,0,2,1:T(8,128)(2,1)} %reshape.29) | data formatting | bytes 4915200 | tf_op jit(solution)/shard_map/reshape | solution.py:51
  15.4 0.0 copy-done.3
  15.4 0.1 select_reduce_fusion
  15.5 0.7 gather_fusion
  16.2 2.3 gather_fusion.1
  18.5 0.0 copy-done
  18.6 2.5 %fusion = bf16[16,2,8,3,1280]{4,2,1,3,0:T(8,128)(2,1)S(1)} fusion(bf16[16,3,20,1280]{3,2,1,0:T(8,128)(2,1)} %gather_fusion.1, bf16[20,16]{0,1:T(8,128)(2,1)S(1)} %copy-done), kind=kOutput, calls=%fused_computation.6 | convolution fusion | flops 40304640 | bytes 4424320 | tf_op jit(solution)/shard_map/jvlx,lus->jusvx/dot_general | solution.py:55
  21.0 1.4 copy.32
  22.4 2.8 %reshape.66 = bf16[32,24,1280]{2,1,0:T(8,128)(2,1)} reshape(bf16[16,2,8,3,1280]{4,3,2,1,0:T(4,128)(2,1)S(1)} %copy.32) | data formatting | bytes 3932160 | tf_op jit(solution)/shard_map/reshape | solution.py:58
  25.2 0.0 copy-start.2
  25.2 7.5 %all-to-all-start = ((bf16[32,24,1280]{2,1,0:T(8,128)(2,1)}), bf16[32,24,1280]{2,1,0:T(8,128)(2,1)S(1)}, u32[]{:S(2)}, u32[]{:S(2)}) async-start(bf16[32,24,1280]{2,1,0:T(8,128)(2,1)} %reshape.66), calls=%async_computation | async-start | bytes 3932160 | tf_op jit(solution)/shard_map/all_to_all | solution.py:59
  32.7 0.0 copy-done.2
  32.8 0.6 reshape.34.m_ref
  33.4 45.0 %all-to-all-done = bf16[32,24,1280]{2,1,0:T(8,128)(2,1)S(1)} async-done(((bf16[32,24,1280]{2,1,0:T(8,128)(2,1)}), bf16[32,24,1280]{2,1,0:T(8,128)(2,1)S(1)}, u32[]{:S(2)}, u32[]{:S(2)}) %all-to-all-start) | async-done | bytes 1966112 | tf_op jit(solution)/shard_map/all_to_all | solution.py:59
  78.4 12.5 %reshape.32 = bf16[16,2,8,3,32,40]{5,4,3,2,1,0:T(8,128)(2,1)} reshape(bf16[32,24,1280]{2,1,0:T(8,128)(2,1)S(1)} %all-to-all-done) | data formatting | bytes 3932160 | tf_op jit(solution)/shard_map/reshape | solution.py:60
  90.9 9.5 %copy.27 = bf16[8,2,32,3,16,40]{5,4,3,2,1,0:T(8,128)(2,1)} copy(bf16[8,2,32,3,16,40]{5,2,3,0,1,4:T(8,128)(2,1)} %bitcast.32) | data formatting | bytes 3932160 | tf_op jit(solution)/shard_map/transpose | solution.py:61
  100.4 9.9 %reshape.33.x_ref = bf16[8,64,1920]{2,1,0:T(8,128)(2,1)} reshape(bf16[8,2,32,3,16,40]{5,4,3,2,1,0:T(8,128)(2,1)} %copy.27) | data formatting | bytes 3932160 | tf_op jit(solution)/shard_map/reshape | solution.py:61
  110.3 19.5 %shard_map.55 = bf16[8,64,1920]{2,1,0:T(8,128)(2,1)} custom-call(bf16[8,960,1920]{2,1,0:T(8,128)(2,1)} %t_ref.1, bf16[8,64,1920]{2,1,0:T(8,128)(2,1)} %reshape.33.x_ref, f32[8,1,960]{2,1,0:T(1,128)} %reshape.34.m_ref), custom_call_target="tpu_custom_call" | custom-call | tf_op jit(solution)/shard_map/pallas_call | solution.py:29
  129.8 11.6 %reshape.35 = bf16[8,2,32,3,16,40]{5,4,3,2,1,0:T(8,128)(2,1)} reshape(bf16[8,64,1920]{2,1,0:T(8,128)(2,1)} %shard_map.55) | data formatting | bytes 3932160 | tf_op jit(solution)/shard_map/reshape | solution.py:67
  141.3 7.1 %copy.37 = bf16[8,2,32,3,16,40]{5,2,3,0,1,4:T(8,128)(2,1)} copy(bf16[8,2,32,3,16,40]{5,4,3,2,1,0:T(8,128)(2,1)} %reshape.35) | data formatting | bytes 3932160 | tf_op jit(solution)/shard_map/reshape | solution.py:67
  148.4 10.6 %reshape.36 = bf16[32,24,1280]{2,1,0:T(8,128)(2,1)} reshape(bf16[16,2,8,3,32,40]{5,4,3,2,1,0:T(8,128)(2,1)} %bitcast.33) | data formatting | bytes 3932160 | tf_op jit(solution)/shard_map/reshape | solution.py:69
  159.0 3.6 %all-to-all-start.1 = ((bf16[32,24,1280]{2,1,0:T(8,128)(2,1)}), bf16[32,24,1280]{2,1,0:T(8,128)(2,1)S(1)}, u32[]{:S(2)}, u32[]{:S(2)}) async-start(bf16[32,24,1280]{2,1,0:T(8,128)(2,1)} %reshape.36), calls=%async_computation.1 | async-start | bytes 3932160 | tf_op jit(solution)/shard_map/all_to_all | solution.py:70
  162.7 45.9 %all-to-all-done.1 = bf16[32,24,1280]{2,1,0:T(8,128)(2,1)S(1)} async-done(((bf16[32,24,1280]{2,1,0:T(8,128)(2,1)}), bf16[32,24,1280]{2,1,0:T(8,128)(2,1)S(1)}, u32[]{:S(2)}, u32[]{:S(2)}) %all-to-all-start.1) | async-done | bytes 1966112 | tf_op jit(solution)/shard_map/all_to_all | solution.py:70
  208.6 12.5 %squeeze_reshape.3 = bf16[16,2,8,3,32,40]{5,4,3,2,1,0:T(8,128)(2,1)} reshape(bf16[32,24,1280]{2,1,0:T(8,128)(2,1)S(1)} %all-to-all-done.1) | data formatting | bytes 3932160 | tf_op jit(solution)/shard_map/squeeze;reshape | solution.py:72
  221.0 6.8 %gather_fusion.2 = bf16[16,2,8,3,32,40]{5,4,3,2,1,0:T(8,128)(2,1)} fusion(bf16[16,2,8,3,32,40]{5,4,3,2,1,0:T(8,128)(2,1)} %squeeze_reshape.3, s32[1024]{0:T(1024)S(1)} %pad_clamp_fusion), kind=kCustom, calls=%fused_computation.2 | custom fusion | bytes 3932224 | tf_op jit(solution)/shard_map/jit(_take)/gather | solution.py:73
  227.8 0.0 copy-start.1
  227.8 7.5 %copy.36 = bf16[16,16,3,32,40]{4,3,0,2,1:T(8,128)(2,1)} copy(bf16[16,16,3,32,40]{4,3,2,1,0:T(8,128)(2,1)} %bitcast.31) | data formatting | bytes 3932160 | tf_op jit(solution)/shard_map/reshape | solution.py:74
  235.3 0.0 copy-done.1
  (5 shorter events, 0.0 us)
Async XLA Ops:
  0.0 18.6 %copy-start = (bf16[20,16]{0,1:T(8,128)(2,1)S(1)}, bf16[20,16]{0,1:T(8,128)(2,1)}, u32[]{:S(2)}) copy-start(bf16[20,16]{0,1:T(8,128)(2,1)} %param.6) | copy-start | bytes 1924
  12.9 2.5 %copy-start.3 = (s32[16]{0:T(128)S(1)}, s32[16]{0:T(128)}, u32[]{:S(2)}) copy-start(s32[16]{0:T(128)} %param.7) | copy-start | bytes 196
  25.2 7.5 %copy-start.2 = (s32[8,960]{1,0:T(8,128)S(1)}, s32[8,960]{1,0:T(8,128)}, u32[]{:S(2)}) copy-start(s32[8,960]{1,0:T(8,128)} %param.9) | copy-start | bytes 92164
  25.2 53.2 %all-to-all-start = ((bf16[32,24,1280]{2,1,0:T(8,128)(2,1)}), bf16[32,24,1280]{2,1,0:T(8,128)(2,1)S(1)}, u32[]{:S(2)}, u32[]{:S(2)}) async-start(bf16[32,24,1280]{2,1,0:T(8,128)(2,1)} %reshape.66), calls=%async_computation | async-start | bytes 3932160 | tf_op jit(solution)/shard_map/all_to_all | solution.py:59
  159.0 49.5 %all-to-all-start.1 = ((bf16[32,24,1280]{2,1,0:T(8,128)(2,1)}), bf16[32,24,1280]{2,1,0:T(8,128)(2,1)S(1)}, u32[]{:S(2)}, u32[]{:S(2)}) async-start(bf16[32,24,1280]{2,1,0:T(8,128)(2,1)} %reshape.36), calls=%async_computation.1 | async-start | bytes 3932160 | tf_op jit(solution)/shard_map/all_to_all | solution.py:70
  227.8 7.5 %copy-start.1 = (bf16[20,16]{0,1:T(8,128)(2,1)S(1)}, bf16[20,16]{0,1:T(8,128)(2,1)}, u32[]{:S(2)}) copy-start(bf16[20,16]{0,1:T(8,128)(2,1)} %param.6) | copy-start | bytes 1924

commit v4 on v3

--- a/solution.py
+++ b/solution.py
@@ -2,6 +2,7 @@
 import jax.numpy as jnp
 from jax import lax
 from jax.experimental import pallas as pl
+from jax.experimental.pallas import tpu as pltpu
 from jax.sharding import PartitionSpec as P
 
 AXES = ("lat", "tm")
@@ -13,30 +14,43 @@
     return jnp.sum(jnp.where(hit, ids[None, :], 0), axis=1).astype(jnp.int32)
 
 
-def filter_kernel(t_ref, x_ref, m_ref, o_ref):
+def filter_kernel(t_ref, r_ref, m_ref, o_ref, x_scr, y_scr):
+    n_lat, n_tm, _, variables, span, lat_count = r_ref.shape
+    seg = n_lat * lat_count
+    for t in range(n_tm):
+        for v in range(variables):
+            for i in range(n_lat):
+                x_scr[pl.ds(t * span, span), pl.ds(v * seg + i * lat_count, lat_count)] = r_ref[i, t, 0, v]
     table = t_ref[0]
     coefficients = lax.dot_general(
-        x_ref[0], table, (((1,), (1,)), ((), ())), preferred_element_type=jnp.float32
+        x_scr[...], table, (((1,), (1,)), ((), ())), preferred_element_type=jnp.float32
     )
     kept = (coefficients * m_ref[0]).astype(jnp.bfloat16)
     synth = jnp.dot(kept, table, preferred_element_type=jnp.float32)
-    o_ref[0] = synth.astype(o_ref.dtype)
+    y_scr[...] = synth.astype(y_scr.dtype)
+    for t in range(n_tm):
+        for v in range(variables):
+            for i in range(n_lat):
+                o_ref[i, t, 0, v] = y_scr[pl.ds(t * span, span), pl.ds(v * seg + i * lat_count, lat_count)]
 
 
-def filter_rows(hough_table, columns, mask, out_dtype):
+def filter_rows(hough_table, received, mask, out_dtype):
     k_loc, rows, width = hough_table.shape
-    cols = columns.shape[1]
+    n_lat, n_tm, _, variables, span, lat_count = received.shape
+    cols = n_tm * span
+    block = (n_lat, n_tm, 1, variables, span, lat_count)
     return pl.pallas_call(
         filter_kernel,
         grid=(k_loc,),
         in_specs=[
             pl.BlockSpec((1, rows, width), lambda k: (k, 0, 0)),
-            pl.BlockSpec((1, cols, width), lambda k: (k, 0, 0)),
+            pl.BlockSpec(block, lambda k: (0, 0, k, 0, 0, 0)),
             pl.BlockSpec((1, 1, rows), lambda k: (k, 0, 0)),
         ],
-        out_specs=pl.BlockSpec((1, cols, width), lambda k: (k, 0, 0)),
-        out_shape=jax.ShapeDtypeStruct((k_loc, cols, width), out_dtype),
-    )(hough_table, columns, mask)
+        out_specs=pl.BlockSpec(block, lambda k: (0, 0, k, 0, 0, 0)),
+        out_shape=jax.ShapeDtypeStruct(received.shape, out_dtype),
+        scratch_shapes=[pltpu.VMEM((cols, width), jnp.bfloat16), pltpu.VMEM((cols, width), out_dtype)],
+    )(hough_table, received, mask)
 
 
 def body(fields, vmodes, owner_map, hough_table, keep_mask):
@@ -58,14 +72,9 @@
     outgoing = outgoing.reshape(n_lat * n_tm, k_loc * variables, block)
     incoming = lax.all_to_all(outgoing, AXES, 0, 0, tiled=True)
     incoming = incoming.reshape(n_lat, n_tm, k_loc, variables, span, lat_count)
-    columns = incoming.transpose(2, 1, 4, 3, 0, 5).reshape(
-        k_loc, n_tm * span, variables * n_lat * lat_count
-    )
     mask = keep_mask.astype(jnp.float32).reshape(k_loc, 1, -1)
     out_dtype = jnp.bfloat16 if group_size == 1 else jnp.float32
-    synth = filter_rows(hough_table, columns, mask, out_dtype)
-    synth = synth.reshape(k_loc, n_tm, span, variables, n_lat, lat_count)
-    synth = synth.transpose(4, 1, 0, 3, 2, 5)
+    synth = filter_rows(hough_table, incoming, mask, out_dtype)
     synth = synth.reshape(n_lat * n_tm, k_loc * variables, block)
     returned = lax.all_to_all(synth, AXES, 0, 0, tiled=True)
     returned = returned.reshape(orders, group_size, n_tm, k_loc, variables, span, lat_count)

time: 236 us -> 200 us (0.85)
  local copies, waits for them, and re-layouts: 111 us -> 73 us
    reshape x3 -> x0, local copies, waits for them, and re-layouts: 28.5 us -> none  [the longest x2 18.6 us: body(): synth = synth.reshape(k_loc, n_tm, span, variables, n_lat, lat_count)]
    transpose x1 -> x0, local copies, waits for them, and re-layouts: 9.48 us -> none  [body(): incoming.transpose(2, 1, 4, 3, 0, 5)]
where the time goes in v4:
time: 200 us; the launch traced here: 199 us
  waiting for transfers between devices  90.9 us (45%)
  local copies, waits for them, and re-layouts  73 us (36%)
  Pallas kernels  21.6 us (11%)
  starting transfers between devices  11.2 us (6%)
  matrix products  2.48 us (1%)
    all_to_all x1, waiting for transfers between devices, body(): returned = lax.all_to_all(synth, AXES, 0, 0, tiled=True)  45.7 us
    all_to_all x1, waiting for transfers between devices, body(): incoming = lax.all_to_all(outgoing, AXES, 0, 0, tiled=True)  45.2 us
    pallas_call x1, Pallas kernels, filter_rows(): pl.pallas_call(filter_kernel, grid=(k_loc,), in_specs=[pl.BlockSpec((1, r...  21.6 us
    reshape x2, local copies, waits for them, and re-layouts, body(): fields.transpose(3, 0, 1, 4, 2).reshape(orders, variables, lev, block)  15.4 us
    another operation x1, local copies, waits for them, and re-layouts, body(): returned = returned.sum(axis=1) if group_size > 1 else returned[:, 0]  12.5 us
    reshape x1, local copies, waits for them, and re-layouts, body(): incoming = incoming.reshape(n_lat, n_tm, k_loc, variables, span, lat_count)  12.5 us
    reshape x1, local copies, waits for them, and re-layouts, body(): synth = synth.reshape(n_lat * n_tm, k_loc * variables, block)  10.6 us
    reshape x1, local copies, waits for them, and re-layouts, body(): result = result.reshape(orders, kmodes, variables, span, lat_count)  7.45 us
  transfers between devices with their start and end apart: 2, of which 2 were waited for; matrix products, arithmetic and copies ran while one was open for 0% of the time, Pallas kernels for 0%

profile of v4, /device:TPU:0, one launch (start us, length us, event | category | flops | bytes accessed | tf_op | source)
XLA Modules:
  0.0 199.4 jit_solution(15420635672421461870)
XLA Ops:
  0.0 0.0 copy-start
  0.0 12.9 %reshape.23 = bf16[16,3,20,1280]{3,0,2,1:T(8,128)(2,1)} reshape(bf16[16,3,20,32,40]{4,3,0,2,1:T(8,128)(2,1)} %bitcast.26) | data formatting | bytes 4915200 | tf_op jit(solution)/shard_map/reshape | solution.py:65
  12.9 0.0 copy-start.3
  12.9 2.5 %copy.18 = bf16[16,3,20,1280]{3,2,1,0:T(8,128)(2,1)S(1)} copy(bf16[16,3,20,1280]{3,0,2,1:T(8,128)(2,1)} %reshape.23) | data formatting | bytes 4915200 | tf_op jit(solution)/shard_map/reshape | solution.py:65
  15.4 0.0 copy-done.3
  15.4 0.1 select_reduce_fusion
  15.5 0.7 gather_fusion
  16.2 2.3 %gather_fusion.1 = bf16[16,3,20,1280]{3,2,1,0:T(8,128)(2,1)} fusion(bf16[16,3,20,1280]{3,2,1,0:T(8,128)(2,1)S(1)} %copy.18, s32[1024]{0:T(1024)S(1)} %pad_clamp_fusion.1), kind=kCustom, calls=%fused_computation.1 | custom fusion | bytes 4915264 | tf_op jit(solution)/shard_map/jit(_take)/gather | solution.py:67
  18.5 0.0 copy-done
  18.6 2.5 %fusion = bf16[16,2,8,3,1280]{4,2,1,3,0:T(8,128)(2,1)S(1)} fusion(bf16[16,3,20,1280]{3,2,1,0:T(8,128)(2,1)} %gather_fusion.1, bf16[20,16]{0,1:T(8,128)(2,1)S(1)} %copy-done), kind=kOutput, calls=%fused_computation.5 | convolution fusion | flops 40304640 | bytes 4424320 | tf_op jit(solution)/shard_map/jvlx,lus->jusvx/dot_general | solution.py:69
  21.0 1.4 copy.24
  22.4 2.8 %reshape.58 = bf16[32,24,1280]{2,1,0:T(8,128)(2,1)} reshape(bf16[16,2,8,3,1280]{4,3,2,1,0:T(4,128)(2,1)S(1)} %copy.24) | data formatting | bytes 3932160 | tf_op jit(solution)/shard_map/reshape | solution.py:72
  25.2 0.0 copy-start.2
  25.2 7.3 %all-to-all-start = ((bf16[32,24,1280]{2,1,0:T(8,128)(2,1)}), bf16[32,24,1280]{2,1,0:T(8,128)(2,1)S(1)}, u32[]{:S(2)}, u32[]{:S(2)}) async-start(bf16[32,24,1280]{2,1,0:T(8,128)(2,1)} %reshape.58), calls=%async_computation | async-start | bytes 3932160 | tf_op jit(solution)/shard_map/all_to_all | solution.py:73
  32.6 0.0 copy-done.2
  32.6 0.6 reshape.27.m_ref
  33.2 45.2 %all-to-all-done = bf16[32,24,1280]{2,1,0:T(8,128)(2,1)S(1)} async-done(((bf16[32,24,1280]{2,1,0:T(8,128)(2,1)}), bf16[32,24,1280]{2,1,0:T(8,128)(2,1)S(1)}, u32[]{:S(2)}, u32[]{:S(2)}) %all-to-all-start) | async-done | bytes 1966112 | tf_op jit(solution)/shard_map/all_to_all | solution.py:73
  78.4 12.5 %reshape.26.r_ref = bf16[16,2,8,3,32,40]{5,4,3,2,1,0:T(8,128)(2,1)} reshape(bf16[32,24,1280]{2,1,0:T(8,128)(2,1)S(1)} %all-to-all-done) | data formatting | bytes 3932160 | tf_op jit(solution)/shard_map/reshape | solution.py:74
  90.9 21.6 %shard_map.55 = bf16[16,2,8,3,32,40]{5,4,3,2,1,0:T(8,128)(2,1)} custom-call(bf16[8,960,1920]{2,1,0:T(8,128)(2,1)} %t_ref.1, bf16[16,2,8,3,32,40]{5,4,3,2,1,0:T(8,128)(2,1)} %reshape.26.r_ref, f32[8,1,960]{2,1,0:T(1,128)} %reshape.27.m_ref), custom_call_target="tpu_custom_call" | custom-call | tf_op jit(solution)/shard_map/pallas_call | solution.py:42
  112.5 10.6 %reshape.28 = bf16[32,24,1280]{2,1,0:T(8,128)(2,1)} reshape(bf16[16,2,8,3,32,40]{5,4,3,2,1,0:T(8,128)(2,1)} %shard_map.55) | data formatting | bytes 3932160 | tf_op jit(solution)/shard_map/reshape | solution.py:78
  123.2 3.8 %all-to-all-start.1 = ((bf16[32,24,1280]{2,1,0:T(8,128)(2,1)}), bf16[32,24,1280]{2,1,0:T(8,128)(2,1)S(1)}, u32[]{:S(2)}, u32[]{:S(2)}) async-start(bf16[32,24,1280]{2,1,0:T(8,128)(2,1)} %reshape.28), calls=%async_computation.1 | async-start | bytes 3932160 | tf_op jit(solution)/shard_map/all_to_all | solution.py:79
  127.0 45.7 %all-to-all-done.1 = bf16[32,24,1280]{2,1,0:T(8,128)(2,1)S(1)} async-done(((bf16[32,24,1280]{2,1,0:T(8,128)(2,1)}), bf16[32,24,1280]{2,1,0:T(8,128)(2,1)S(1)}, u32[]{:S(2)}, u32[]{:S(2)}) %all-to-all-start.1) | async-done | bytes 1966112 | tf_op jit(solution)/shard_map/all_to_all | solution.py:79
  172.7 12.5 %squeeze_reshape.3 = bf16[16,2,8,3,32,40]{5,4,3,2,1,0:T(8,128)(2,1)} reshape(bf16[32,24,1280]{2,1,0:T(8,128)(2,1)S(1)} %all-to-all-done.1) | data formatting | bytes 3932160 | tf_op jit(solution)/shard_map/squeeze;reshape | solution.py:81
  185.2 6.8 %gather_fusion.2 = bf16[16,2,8,3,32,40]{5,4,3,2,1,0:T(8,128)(2,1)} fusion(bf16[16,2,8,3,32,40]{5,4,3,2,1,0:T(8,128)(2,1)} %squeeze_reshape.3, s32[1024]{0:T(1024)S(1)} %pad_clamp_fusion), kind=kCustom, calls=%fused_computation.2 | custom fusion | bytes 3932224 | tf_op jit(solution)/shard_map/jit(_take)/gather | solution.py:82
  192.0 0.0 copy-start.1
  192.0 7.5 %copy.27 = bf16[16,16,3,32,40]{4,3,0,2,1:T(8,128)(2,1)} copy(bf16[16,16,3,32,40]{4,3,2,1,0:T(8,128)(2,1)} %bitcast.25) | data formatting | bytes 3932160 | tf_op jit(solution)/shard_map/reshape | solution.py:83
  199.4 0.0 copy-done.1
  (5 shorter events, 0.0 us)
Async XLA Ops:
  0.0 18.6 %copy-start = (bf16[20,16]{0,1:T(8,128)(2,1)S(1)}, bf16[20,16]{0,1:T(8,128)(2,1)}, u32[]{:S(2)}) copy-start(bf16[20,16]{0,1:T(8,128)(2,1)} %param.6) | copy-start | bytes 1924
  12.9 2.5 %copy-start.3 = (s32[16]{0:T(128)S(1)}, s32[16]{0:T(128)}, u32[]{:S(2)}) copy-start(s32[16]{0:T(128)} %param.7) | copy-start | bytes 196
  25.2 7.3 %copy-start.2 = (s32[8,960]{1,0:T(8,128)S(1)}, s32[8,960]{1,0:T(8,128)}, u32[]{:S(2)}) copy-start(s32[8,960]{1,0:T(8,128)} %param.9) | copy-start | bytes 92164
  25.2 53.2 %all-to-all-start = ((bf16[32,24,1280]{2,1,0:T(8,128)(2,1)}), bf16[32,24,1280]{2,1,0:T(8,128)(2,1)S(1)}, u32[]{:S(2)}, u32[]{:S(2)}) async-start(bf16[32,24,1280]{2,1,0:T(8,128)(2,1)} %reshape.58), calls=%async_computation | async-start | bytes 3932160 | tf_op jit(solution)/shard_map/all_to_all | solution.py:73
  123.2 49.5 %all-to-all-start.1 = ((bf16[32,24,1280]{2,1,0:T(8,128)(2,1)}), bf16[32,24,1280]{2,1,0:T(8,128)(2,1)S(1)}, u32[]{:S(2)}, u32[]{:S(2)}) async-start(bf16[32,24,1280]{2,1,0:T(8,128)(2,1)} %reshape.28), calls=%async_computation.1 | async-start | bytes 3932160 | tf_op jit(solution)/shard_map/all_to_all | solution.py:79
  192.0 7.5 %copy-start.1 = (bf16[20,16]{0,1:T(8,128)(2,1)S(1)}, bf16[20,16]{0,1:T(8,128)(2,1)}, u32[]{:S(2)}) copy-start(bf16[20,16]{0,1:T(8,128)(2,1)} %param.6) | copy-start | bytes 1924

commit v5 on v4

v5 whole, which is shorter than its diff:
```python
import functools

import jax
import jax.numpy as jnp
from jax import lax
from jax.experimental import pallas as pl
from jax.experimental.pallas import tpu as pltpu
from jax.sharding import PartitionSpec as P

AXES = ("lat", "tm")


def order_of_slot(owner_map):
    ids = jnp.arange(owner_map.shape[0], dtype=jnp.int32)
    hit = owner_map[None, :] == ids[:, None]
    return jnp.sum(jnp.where(hit, ids[None, :], 0), axis=1).astype(jnp.int32)


def filter_kernel(variables, t_ref, r_ref, m_ref, o_ref, x_scr, y_scr):
    n_lat, n_tm, _, span, lanes = r_ref.shape
    lat_count = lanes // variables
    seg = n_lat * lat_count
    for t in range(n_tm):
        for v in range(variables):
            for i in range(n_lat):
                x_scr[pl.ds(t * span, span), pl.ds(v * seg + i * lat_count, lat_count)] = r_ref[
                    i, t, 0, :, pl.ds(v * lat_count, lat_count)
                ]
    table = t_ref[0]
    coefficients = lax.dot_general(
        x_scr[...], table, (((1,), (1,)), ((), ())), preferred_element_type=jnp.float32
    )
    kept = (coefficients * m_ref[0]).astype(jnp.bfloat16)
    synth = jnp.dot(kept, table, preferred_element_type=jnp.float32)
    y_scr[...] = synth.astype(y_scr.dtype)
    for t in range(n_tm):
        for v in range(variables):
            for i in range(n_lat):
                o_ref[i, t, 0, :, pl.ds(v * lat_count, lat_count)] = y_scr[
                    pl.ds(t * span, span), pl.ds(v * seg + i * lat_count, lat_count)
                ]


def filter_rows(hough_table, received, mask, out_dtype, variables):
    k_loc, rows, width = hough_table.shape
    n_lat, n_tm, _, span, lanes = received.shape
    cols = n_tm * span
    block = (n_lat, n_tm, 1, span, lanes)
    return pl.pallas_call(
        functools.partial(filter_kernel, variables),
        grid=(k_loc,),
        in_specs=[
            pl.BlockSpec((1, rows, width), lambda k: (k, 0, 0)),
            pl.BlockSpec(block, lambda k: (0, 0, k, 0, 0)),
            pl.BlockSpec((1, 1, rows), lambda k: (k, 0, 0)),
        ],
        out_specs=pl.BlockSpec(block, lambda k: (0, 0, k, 0, 0)),
        out_shape=jax.ShapeDtypeStruct(received.shape, out_dtype),
        scratch_shapes=[pltpu.VMEM((cols, width), jnp.bfloat16), pltpu.VMEM((cols, width), out_dtype)],
    )(hough_table, received, mask)


def body(fields, vmodes, owner_map, hough_table, keep_mask):
    n_lat = lax.axis_size("lat")
    n_tm = lax.axis_size("tm")
    orders = owner_map.shape[0]
    group_size = n_lat // orders
    variables, lev, lat_count, _, span = fields.shape
    kmodes = vmodes.shape[1]
    k_loc = kmodes // n_tm
    by_order = fields.transpose(3, 0, 1, 4, 2)
    dest_order = order_of_slot(owner_map)[jnp.arange(n_lat, dtype=jnp.int32) // group_size]
    picked = jnp.take(by_order, dest_order, axis=0, mode="clip")
    vm = vmodes.reshape(lev, n_tm, k_loc)
    outgoing = jnp.einsum(
        "jvlca,lus->juscva", picked, vm, preferred_element_type=jnp.float32
    ).astype(jnp.bfloat16)
    outgoing = outgoing.reshape(n_lat * n_tm, k_loc * span, variables * lat_count)
    incoming = lax.all_to_all(outgoing, AXES, 0, 0, tiled=True)
    incoming = incoming.reshape(n_lat, n_tm, k_loc, span, variables * lat_count)
    mask = keep_mask.astype(jnp.float32).reshape(k_loc, 1, -1)
    out_dtype = jnp.bfloat16 if group_size == 1 else jnp.float32
    synth = filter_rows(hough_table, incoming, mask, out_dtype, variables)
    synth = synth.reshape(n_lat * n_tm, k_loc * span, variables * lat_count)
    returned = lax.all_to_all(synth, AXES, 0, 0, tiled=True)
    returned = returned.reshape(orders, group_size, n_tm, k_loc, span, variables, lat_count)
    returned = returned.sum(axis=1) if group_size > 1 else returned[:, 0]
    result = jnp.take(returned, owner_map, axis=0, mode="clip")
    result = result.reshape(orders, kmodes, span, variables, lat_count)
    return result.transpose(1, 3, 4, 0, 2).astype(jnp.bfloat16)


def solution(mesh):
    in_specs = (P(None, None, "lat", None, "tm"), P(), P(), P("tm", "lat", None), P("tm", "lat"))
    out_specs = P(None, None, "lat", None, "tm")
    return jax.shard_map(body, mesh=mesh, in_specs=in_specs, out_specs=out_specs, check_vma=False)
```

time: 200 us -> 204 us (1.020)
  matrix products: 2.48 us -> 8.84 us
  local copies, waits for them, and re-layouts: 73 us -> 70.4 us
    reshape x7 -> x3, local copies, waits for them, and re-layouts: 50.1 us -> 21.7 us  [the longest x1 10.2 us: body(): outgoing.reshape(n_lat * n_tm, k_loc * span, variables * lat_count)]
    convert_element_type x0 -> x1, local copies, waits for them, and re-layouts: none -> 12.9 us  [body(): outgoing = jnp.einsum('jvlca,lus->juscva', picked, vm, preferred_element_...]
    dot_general x1, matrix products: 2.48 us -> 8.84 us  [body(): jnp.einsum('jvlca,lus->juscva', picked, vm, preferred_element_type=jnp.fl...]
    gather x1, local copies, waits for them, and re-layouts: 2.34 us -> 7.81 us  [body(): picked = jnp.take(by_order, dest_order, axis=0, mode='clip')]
    another operation x1 -> x2, local copies, waits for them, and re-layouts: 12.5 us -> 17.1 us  [body(): returned = returned.sum(axis=1) if group_size > 1 else returned[:, 0]]
    all_to_all x0 -> x1, local copies, waits for them, and re-layouts: none -> 2.74 us  [body(): incoming = lax.all_to_all(outgoing, AXES, 0, 0, tiled=True)]
where the time goes in v5:
time: 204 us; the launch traced here: 202 us
  waiting for transfers between devices  91.1 us (45%)
  local copies, waits for them, and re-layouts  70.4 us (35%)
  Pallas kernels  20.2 us (10%)
  starting transfers between devices  11 us (5%)
  matrix products  8.84 us (4%)
    all_to_all x1, waiting for transfers between devices, body(): returned = lax.all_to_all(synth, AXES, 0, 0, tiled=True)  45.8 us
    all_to_all x1, waiting for transfers between devices, body(): incoming = lax.all_to_all(outgoing, AXES, 0, 0, tiled=True)  45.2 us
    pallas_call x1, Pallas kernels, filter_rows(): pl.pallas_call(functools.partial(filter_kernel, variables), grid=(k_loc,)...  20.2 us
    another operation x2, local copies, waits for them, and re-layouts, body(): returned = returned.sum(axis=1) if group_size > 1 else returned[:, 0]  17.1 us
    convert_element_type x1, local copies, waits for them, and re-layouts, body(): outgoing = jnp.einsum('jvlca,lus->juscva', picked, vm, preferred_element_...  12.9 us
    reshape x1, local copies, waits for them, and re-layouts, body(): outgoing.reshape(n_lat * n_tm, k_loc * span, variables * lat_count)  10.2 us
    dot_general x1, matrix products, body(): jnp.einsum('jvlca,lus->juscva', picked, vm, preferred_element_type=jnp.fl...  8.84 us
    gather x1, local copies, waits for them, and re-layouts, body(): picked = jnp.take(by_order, dest_order, axis=0, mode='clip')  7.81 us
  transfers between devices with their start and end apart: 2, of which 2 were waited for; matrix products, arithmetic and copies ran while one was open for 0% of the time, Pallas kernels for 0%

profile of v5, /device:TPU:0, one launch (start us, length us, event | category | flops | bytes accessed | tf_op | source)
XLA Modules:
  0.0 202.3 jit_solution(1261664449364225376)
XLA Ops:
  0.0 0.0 copy-start
  0.0 0.8 select_reduce_fusion
  0.8 0.7 gather_fusion
  1.5 7.8 %gather_fusion.1 = bf16[16,3,20,32,40]{4,3,2,1,0:T(8,128)(2,1)} fusion(bf16[16,3,20,32,40]{4,3,0,2,1:T(8,128)(2,1)} %bitcast.27, s32[1024]{0:T(1024)S(1)} %pad_clamp_fusion.1), kind=kCustom, calls=%fused_computation.1 | custom fusion | bytes 4915264 | tf_op jit(solution)/shard_map/jit(_take)/gather | solution.py:73
  9.3 0.0 copy-done
  9.3 8.8 %convert_bitcast_fusion = bf16[16,2,8,32,3,40]{5,2,1,3,4,0:T(8,128)(2,1)} fusion(bf16[16,3,20,32,40,1]{4,3,2,1,0,5:T(8,128)(2,1)} %bitcast.23, bf16[20,16]{0,1:T(8,128)(2,1)S(1)} %copy-done), kind=kOutput, calls=%fused_computation.6 | convolution fusion | flops 40304640 | bytes 4424320 | tf_op jit(solution)/shard_map/jvlca,lus->juscva/dot_general | solution.py:75
  18.1 12.9 %copy.14 = bf16[16,2,8,32,3,40]{3,2,5,4,1,0:T(8,128)(2,1)} copy(bf16[16,2,8,32,3,40]{5,2,1,3,4,0:T(8,128)(2,1)} %convert_bitcast_fusion) | data formatting | bytes 3932160 | tf_op jit(solution)/shard_map/convert_element_type | solution.py:77
  31.0 0.0 copy-start.2
  31.0 10.2 %reshape.21 = bf16[32,256,120]{1,2,0:T(8,128)(2,1)} reshape(bf16[16,2,8,32,3,40]{3,2,5,4,1,0:T(8,128)(2,1)} %copy.14) | data formatting | bytes 3932160 | tf_op jit(solution)/shard_map/reshape | solution.py:78
  41.3 7.3 %all-to-all-start = ((bf16[32,256,120]{1,2,0:T(8,128)(2,1)}), bf16[32,256,120]{1,2,0:T(8,128)(2,1)S(1)}, u32[]{:S(2)}, u32[]{:S(2)}) async-start(bf16[32,256,120]{1,2,0:T(8,128)(2,1)} %reshape.21), calls=%async_computation | async-start | bytes 3932160 | tf_op jit(solution)/shard_map/all_to_all | solution.py:79
  48.6 0.0 copy-done.2
  48.6 0.6 reshape.23.m_ref
  49.2 45.2 %all-to-all-done = bf16[32,256,120]{1,2,0:T(8,128)(2,1)S(1)} async-done(((bf16[32,256,120]{1,2,0:T(8,128)(2,1)}), bf16[32,256,120]{1,2,0:T(8,128)(2,1)S(1)}, u32[]{:S(2)}, u32[]{:S(2)}) %all-to-all-start) | async-done | bytes 1966112 | tf_op jit(solution)/shard_map/all_to_all | solution.py:79
  94.5 2.7 %copy.15 = bf16[32,256,120]{2,1,0:T(8,128)(2,1)} copy(bf16[32,256,120]{1,2,0:T(8,128)(2,1)S(1)} %all-to-all-done) | data formatting | bytes 3932160 | tf_op jit(solution)/shard_map/all_to_all | solution.py:79
  97.2 20.2 %shard_map.55 = bf16[16,2,8,32,120]{4,3,2,1,0:T(8,128)(2,1)} custom-call(bf16[8,960,1920]{2,1,0:T(8,128)(2,1)} %t_ref.1, bf16[16,2,8,32,120]{4,3,2,1,0:T(8,128)(2,1)} %bitcast.25, f32[8,1,960]{2,1,0:T(1,128)} %reshape.23.m_ref), custom_call_target="tpu_custom_call" | custom-call | tf_op jit(solution)/shard_map/pallas_call | solution.py:49
  117.4 0.0 copy-start.3
  117.4 4.1 %copy.16 = bf16[32,256,120]{1,2,0:T(8,128)(2,1)} copy(bf16[32,256,120]{2,1,0:T(8,128)(2,1)} %bitcast.26) | data formatting | bytes 3932160 | tf_op jit(solution)/shard_map/reshape | solution.py:84
  121.4 3.7 %all-to-all-start.1 = ((bf16[32,256,120]{1,2,0:T(8,128)(2,1)}), bf16[32,256,120]{1,2,0:T(8,128)(2,1)S(1)}, u32[]{:S(2)}, u32[]{:S(2)}) async-start(bf16[32,256,120]{1,2,0:T(8,128)(2,1)} %copy.16), calls=%async_computation.1 | async-start | bytes 3932160 | tf_op jit(solution)/shard_map/all_to_all | solution.py:85
  125.1 0.0 copy-done.3
  125.1 45.8 %all-to-all-done.1 = bf16[32,256,120]{1,2,0:T(8,128)(2,1)S(1)} async-done(((bf16[32,256,120]{1,2,0:T(8,128)(2,1)}), bf16[32,256,120]{1,2,0:T(8,128)(2,1)S(1)}, u32[]{:S(2)}, u32[]{:S(2)}) %all-to-all-start.1) | async-done | bytes 1966112 | tf_op jit(solution)/shard_map/all_to_all | solution.py:85
  171.0 5.9 %squeeze_reshape.3 = bf16[16,2,8,32,3,40]{3,2,5,4,1,0:T(8,128)(2,1)} reshape(bf16[32,256,120]{1,2,0:T(8,128)(2,1)S(1)} %all-to-all-done.1) | data formatting | bytes 3932160 | tf_op jit(solution)/shard_map/squeeze;reshape | solution.py:87
  176.9 11.2 %copy.17 = bf16[16,2,8,32,3,40]{5,3,4,2,1,0:T(8,128)(2,1)} copy(bf16[16,2,8,32,3,40]{3,2,5,4,1,0:T(8,128)(2,1)} %squeeze_reshape.3) | data formatting | bytes 3932160 | tf_op jit(solution)/shard_map/squeeze;reshape | solution.py:87
  188.1 0.0 copy-start.1
  188.1 6.8 %gather_fusion.2 = bf16[16,2,8,32,3,40]{5,3,4,2,1,0:T(8,128)(2,1)} fusion(bf16[16,2,8,32,3,40]{5,3,4,2,1,0:T(8,128)(2,1)} %copy.17, s32[1024]{0:T(1024)S(1)} %pad_clamp_fusion), kind=kCustom, calls=%fused_computation.2 | custom fusion | bytes 3932224 | tf_op jit(solution)/shard_map/jit(_take)/gather | solution.py:88
  194.9 7.4 %copy.28 = bf16[16,16,32,3,40]{4,2,0,3,1:T(8,128)(2,1)} copy(bf16[16,16,32,3,40]{4,2,3,1,0:T(8,128)(2,1)} %bitcast.24) | data formatting | bytes 3932160 | tf_op jit(solution)/shard_map/reshape | solution.py:89
  202.3 0.0 copy-done.1
  (5 shorter events, 0.0 us)
Async XLA Ops:
  0.0 9.3 %copy-start = (bf16[20,16]{0,1:T(8,128)(2,1)S(1)}, bf16[20,16]{0,1:T(8,128)(2,1)}, u32[]{:S(2)}) copy-start(bf16[20,16]{0,1:T(8,128)(2,1)} %param.6) | copy-start | bytes 1924
  31.0 17.6 %copy-start.2 = (s32[8,960]{1,0:T(8,128)S(1)}, s32[8,960]{1,0:T(8,128)}, u32[]{:S(2)}) copy-start(s32[8,960]{1,0:T(8,128)} %param.9) | copy-start | bytes 92164
  41.3 53.2 %all-to-all-start = ((bf16[32,256,120]{1,2,0:T(8,128)(2,1)}), bf16[32,256,120]{1,2,0:T(8,128)(2,1)S(1)}, u32[]{:S(2)}, u32[]{:S(2)}) async-start(bf16[32,256,120]{1,2,0:T(8,128)(2,1)} %reshape.21), calls=%async_computation | async-start | bytes 3932160 | tf_op jit(solution)/shard_map/all_to_all | solution.py:79
  117.4 7.7 %copy-start.3 = (s32[16]{0:T(128)S(1)}, s32[16]{0:T(128)}, u32[]{:S(2)}) copy-start(s32[16]{0:T(128)} %param.7) | copy-start | bytes 196
  121.4 49.5 %all-to-all-start.1 = ((bf16[32,256,120]{1,2,0:T(8,128)(2,1)}), bf16[32,256,120]{1,2,0:T(8,128)(2,1)S(1)}, u32[]{:S(2)}, u32[]{:S(2)}) async-start(bf16[32,256,120]{1,2,0:T(8,128)(2,1)} %copy.16), calls=%async_computation.1 | async-start | bytes 3932160 | tf_op jit(solution)/shard_map/all_to_all | solution.py:85
  188.1 14.2 %copy-start.1 = (bf16[20,16]{0,1:T(8,128)(2,1)S(1)}, bf16[20,16]{0,1:T(8,128)(2,1)}, u32[]{:S(2)}) copy-start(bf16[20,16]{0,1:T(8,128)(2,1)} %param.6) | copy-start | bytes 1924

commit v6 on v4

--- a/solution.py
+++ b/solution.py
@@ -23,10 +23,12 @@
                 x_scr[pl.ds(t * span, span), pl.ds(v * seg + i * lat_count, lat_count)] = r_ref[i, t, 0, v]
     table = t_ref[0]
     coefficients = lax.dot_general(
-        x_scr[...], table, (((1,), (1,)), ((), ())), preferred_element_type=jnp.float32
+        table, x_scr[...], (((1,), (1,)), ((), ())), preferred_element_type=jnp.float32
     )
     kept = (coefficients * m_ref[0]).astype(jnp.bfloat16)
-    synth = jnp.dot(kept, table, preferred_element_type=jnp.float32)
+    synth = lax.dot_general(
+        kept, table, (((0,), (0,)), ((), ())), preferred_element_type=jnp.float32
+    )
     y_scr[...] = synth.astype(y_scr.dtype)
     for t in range(n_tm):
         for v in range(variables):
@@ -45,7 +47,7 @@
         in_specs=[
             pl.BlockSpec((1, rows, width), lambda k: (k, 0, 0)),
             pl.BlockSpec(block, lambda k: (0, 0, k, 0, 0, 0)),
-            pl.BlockSpec((1, 1, rows), lambda k: (k, 0, 0)),
+            pl.BlockSpec((1, rows, 1), lambda k: (k, 0, 0)),
         ],
         out_specs=pl.BlockSpec(block, lambda k: (0, 0, k, 0, 0, 0)),
         out_shape=jax.ShapeDtypeStruct(received.shape, out_dtype),
@@ -72,7 +74,7 @@
     outgoing = outgoing.reshape(n_lat * n_tm, k_loc * variables, block)
     incoming = lax.all_to_all(outgoing, AXES, 0, 0, tiled=True)
     incoming = incoming.reshape(n_lat, n_tm, k_loc, variables, span, lat_count)
-    mask = keep_mask.astype(jnp.float32).reshape(k_loc, 1, -1)
+    mask = keep_mask.astype(jnp.float32).reshape(k_loc, -1, 1)
     out_dtype = jnp.bfloat16 if group_size == 1 else jnp.float32
     synth = filter_rows(hough_table, incoming, mask, out_dtype)
     synth = synth.reshape(n_lat * n_tm, k_loc * variables, block)

time: 200 us -> 206 us (1.030)
  Pallas kernels: 21.6 us -> 27.4 us
    pallas_call x1, Pallas kernels: 21.6 us -> 27.4 us  [filter_rows(): pl.pallas_call(filter_kernel, grid=(k_loc,), in_specs=[pl.BlockSpec((1, r...]
  transfers between devices with their start and end apart: 2 -> 2, of which waited for: 2 -> 2; matrix products, arithmetic and copies ran while one was open for 0% -> 1% of each run, Pallas kernels for 0% -> 0%
where the time goes in v6:
time: 206 us; the launch traced here: 205 us
  waiting for transfers between devices  88.9 us (43%)
  local copies, waits for them, and re-layouts  74.9 us (36%)
  Pallas kernels  27.4 us (13%)
  starting transfers between devices  11.2 us (5%)
  matrix products  2.49 us (1%)
    all_to_all x1, waiting for transfers between devices, body(): returned = lax.all_to_all(synth, AXES, 0, 0, tiled=True)  45.7 us
    all_to_all x1, waiting for transfers between devices, body(): incoming = lax.all_to_all(outgoing, AXES, 0, 0, tiled=True)  43.3 us
    pallas_call x1, Pallas kernels, filter_rows(): pl.pallas_call(filter_kernel, grid=(k_loc,), in_specs=[pl.BlockSpec((1, r...  27.4 us
    reshape x2, local copies, waits for them, and re-layouts, body(): fields.transpose(3, 0, 1, 4, 2).reshape(orders, variables, lev, block)  15.4 us
    reshape x1, local copies, waits for them, and re-layouts, body(): incoming = incoming.reshape(n_lat, n_tm, k_loc, variables, span, lat_count)  12.5 us
    another operation x1, local copies, waits for them, and re-layouts, body(): returned = returned.sum(axis=1) if group_size > 1 else returned[:, 0]  12.5 us
    reshape x1, local copies, waits for them, and re-layouts, body(): synth = synth.reshape(n_lat * n_tm, k_loc * variables, block)  10.6 us
    reshape x1, local copies, waits for them, and re-layouts, body(): result = result.reshape(orders, kmodes, variables, span, lat_count)  7.45 us
  transfers between devices with their start and end apart: 2, of which 2 were waited for; matrix products, arithmetic and copies ran while one was open for 1% of the time, Pallas kernels for 0%

profile of v6, /device:TPU:0, one launch (start us, length us, event | category | flops | bytes accessed | tf_op | source)
XLA Modules:
  0.0 205.2 jit_solution(9944912753681547268)
XLA Ops:
  0.0 0.0 copy-start
  0.0 12.9 %reshape.23 = bf16[16,3,20,1280]{3,0,2,1:T(8,128)(2,1)} reshape(bf16[16,3,20,32,40]{4,3,0,2,1:T(8,128)(2,1)} %bitcast.28) | data formatting | bytes 4915200 | tf_op jit(solution)/shard_map/reshape | solution.py:67
  12.9 0.0 copy-start.3
  12.9 2.5 %copy.21 = bf16[16,3,20,1280]{3,2,1,0:T(8,128)(2,1)S(1)} copy(bf16[16,3,20,1280]{3,0,2,1:T(8,128)(2,1)} %reshape.23) | data formatting | bytes 4915200 | tf_op jit(solution)/shard_map/reshape | solution.py:67
  15.4 0.0 copy-done.3
  15.4 0.1 select_reduce_fusion
  15.5 0.7 gather_fusion
  16.2 2.3 %gather_fusion.1 = bf16[16,3,20,1280]{3,2,1,0:T(8,128)(2,1)} fusion(bf16[16,3,20,1280]{3,2,1,0:T(8,128)(2,1)S(1)} %copy.21, s32[1024]{0:T(1024)S(1)} %pad_clamp_fusion.1), kind=kCustom, calls=%fused_computation.1 | custom fusion | bytes 4915264 | tf_op jit(solution)/shard_map/jit(_take)/gather | solution.py:69
  18.6 0.0 copy-done
  18.6 2.5 %fusion = bf16[16,2,8,3,1280]{4,2,1,3,0:T(8,128)(2,1)S(1)} fusion(bf16[16,3,20,1280]{3,2,1,0:T(8,128)(2,1)} %gather_fusion.1, bf16[20,16]{0,1:T(8,128)(2,1)S(1)} %copy-done), kind=kOutput, calls=%fused_computation.5 | convolution fusion | flops 40304640 | bytes 4424320 | tf_op jit(solution)/shard_map/jvlx,lus->jusvx/dot_general | solution.py:71
  21.0 1.4 copy.28
  22.4 2.8 %reshape.58 = bf16[32,24,1280]{2,1,0:T(8,128)(2,1)} reshape(bf16[16,2,8,3,1280]{4,3,2,1,0:T(4,128)(2,1)S(1)} %copy.28) | data formatting | bytes 3932160 | tf_op jit(solution)/shard_map/reshape | solution.py:74
  25.2 0.0 copy-start.2
  25.2 7.3 %all-to-all-start = ((bf16[32,24,1280]{2,1,0:T(8,128)(2,1)}), bf16[32,24,1280]{2,1,0:T(8,128)(2,1)S(1)}, u32[]{:S(2)}, u32[]{:S(2)}) async-start(bf16[32,24,1280]{2,1,0:T(8,128)(2,1)} %reshape.58), calls=%async_computation | async-start | bytes 3932160 | tf_op jit(solution)/shard_map/all_to_all | solution.py:75
  32.6 0.0 copy-done.2
  32.6 2.6 %copy.24.m_ref = f32[8,960,1]{2,1,0:T(8,128)} copy(f32[8,960,1]{1,0,2:T(8,128)S(1)} %convert_bitcast_fusion) | data formatting | bytes 61440 | tf_op jit(solution)/shard_map/reshape | solution.py:77
  35.2 43.3 %all-to-all-done = bf16[32,24,1280]{2,1,0:T(8,128)(2,1)S(1)} async-done(((bf16[32,24,1280]{2,1,0:T(8,128)(2,1)}), bf16[32,24,1280]{2,1,0:T(8,128)(2,1)S(1)}, u32[]{:S(2)}, u32[]{:S(2)}) %all-to-all-start) | async-done | bytes 1966112 | tf_op jit(solution)/shard_map/all_to_all | solution.py:75
  78.4 12.5 %reshape.26.r_ref = bf16[16,2,8,3,32,40]{5,4,3,2,1,0:T(8,128)(2,1)} reshape(bf16[32,24,1280]{2,1,0:T(8,128)(2,1)S(1)} %all-to-all-done) | data formatting | bytes 3932160 | tf_op jit(solution)/shard_map/reshape | solution.py:76
  90.9 27.4 %shard_map.55 = bf16[16,2,8,3,32,40]{5,4,3,2,1,0:T(8,128)(2,1)} custom-call(bf16[8,960,1920]{2,1,0:T(8,128)(2,1)} %t_ref.1, bf16[16,2,8,3,32,40]{5,4,3,2,1,0:T(8,128)(2,1)} %reshape.26.r_ref, f32[8,960,1]{2,1,0:T(8,128)} %copy.24.m_ref), custom_call_target="tpu_custom_call" | custom-call | tf_op jit(solution)/shard_map/pallas_call | solution.py:44
  118.3 10.6 %reshape.28 = bf16[32,24,1280]{2,1,0:T(8,128)(2,1)} reshape(bf16[16,2,8,3,32,40]{5,4,3,2,1,0:T(8,128)(2,1)} %shard_map.55) | data formatting | bytes 3932160 | tf_op jit(solution)/shard_map/reshape | solution.py:80
  129.0 3.8 %all-to-all-start.1 = ((bf16[32,24,1280]{2,1,0:T(8,128)(2,1)}), bf16[32,24,1280]{2,1,0:T(8,128)(2,1)S(1)}, u32[]{:S(2)}, u32[]{:S(2)}) async-start(bf16[32,24,1280]{2,1,0:T(8,128)(2,1)} %reshape.28), calls=%async_computation.1 | async-start | bytes 3932160 | tf_op jit(solution)/shard_map/all_to_all | solution.py:81
  132.8 45.7 %all-to-all-done.1 = bf16[32,24,1280]{2,1,0:T(8,128)(2,1)S(1)} async-done(((bf16[32,24,1280]{2,1,0:T(8,128)(2,1)}), bf16[32,24,1280]{2,1,0:T(8,128)(2,1)S(1)}, u32[]{:S(2)}, u32[]{:S(2)}) %all-to-all-start.1) | async-done | bytes 1966112 | tf_op jit(solution)/shard_map/all_to_all | solution.py:81
  178.5 12.5 %squeeze_reshape.3 = bf16[16,2,8,3,32,40]{5,4,3,2,1,0:T(8,128)(2,1)} reshape(bf16[32,24,1280]{2,1,0:T(8,128)(2,1)S(1)} %all-to-all-done.1) | data formatting | bytes 3932160 | tf_op jit(solution)/shard_map/squeeze;reshape | solution.py:83
  190.9 6.8 %gather_fusion.2 = bf16[16,2,8,3,32,40]{5,4,3,2,1,0:T(8,128)(2,1)} fusion(bf16[16,2,8,3,32,40]{5,4,3,2,1,0:T(8,128)(2,1)} %squeeze_reshape.3, s32[1024]{0:T(1024)S(1)} %pad_clamp_fusion), kind=kCustom, calls=%fused_computation.2 | custom fusion | bytes 3932224 | tf_op jit(solution)/shard_map/jit(_take)/gather | solution.py:84
  197.7 0.0 copy-start.1
  197.7 7.5 %copy.31 = bf16[16,16,3,32,40]{4,3,0,2,1:T(8,128)(2,1)} copy(bf16[16,16,3,32,40]{4,3,2,1,0:T(8,128)(2,1)} %bitcast.27) | data formatting | bytes 3932160 | tf_op jit(solution)/shard_map/reshape | solution.py:85
  205.2 0.0 copy-done.1
  (5 shorter events, 0.0 us)
Async XLA Ops:
  0.0 18.6 %copy-start = (bf16[20,16]{0,1:T(8,128)(2,1)S(1)}, bf16[20,16]{0,1:T(8,128)(2,1)}, u32[]{:S(2)}) copy-start(bf16[20,16]{0,1:T(8,128)(2,1)} %param.6) | copy-start | bytes 1924
  12.9 2.5 %copy-start.3 = (s32[16]{0:T(128)S(1)}, s32[16]{0:T(128)}, u32[]{:S(2)}) copy-start(s32[16]{0:T(128)} %param.7) | copy-start | bytes 196
  25.2 7.3 %copy-start.2 = (s32[8,960]{1,0:T(8,128)S(1)}, s32[8,960]{1,0:T(8,128)}, u32[]{:S(2)}) copy-start(s32[8,960]{1,0:T(8,128)} %param.9) | copy-start | bytes 92164
  25.2 53.2 %all-to-all-start = ((bf16[32,24,1280]{2,1,0:T(8,128)(2,1)}), bf16[32,24,1280]{2,1,0:T(8,128)(2,1)S(1)}, u32[]{:S(2)}, u32[]{:S(2)}) async-start(bf16[32,24,1280]{2,1,0:T(8,128)(2,1)} %reshape.58), calls=%async_computation | async-start | bytes 3932160 | tf_op jit(solution)/shard_map/all_to_all | solution.py:75
  129.0 49.5 %all-to-all-start.1 = ((bf16[32,24,1280]{2,1,0:T(8,128)(2,1)}), bf16[32,24,1280]{2,1,0:T(8,128)(2,1)S(1)}, u32[]{:S(2)}, u32[]{:S(2)}) async-start(bf16[32,24,1280]{2,1,0:T(8,128)(2,1)} %reshape.28), calls=%async_computation.1 | async-start | bytes 3932160 | tf_op jit(solution)/shard_map/all_to_all | solution.py:81
  197.7 7.5 %copy-start.1 = (bf16[20,16]{0,1:T(8,128)(2,1)S(1)}, bf16[20,16]{0,1:T(8,128)(2,1)}, u32[]{:S(2)}) copy-start(bf16[20,16]{0,1:T(8,128)(2,1)} %param.6) | copy-start | bytes 1924

commit v7 on v4

--- a/solution.py
+++ b/solution.py
@@ -77,7 +77,7 @@
     synth = filter_rows(hough_table, incoming, mask, out_dtype)
     synth = synth.reshape(n_lat * n_tm, k_loc * variables, block)
     returned = lax.all_to_all(synth, AXES, 0, 0, tiled=True)
-    returned = returned.reshape(orders, group_size, n_tm, k_loc, variables, span, lat_count)
+    returned = returned.reshape(orders, group_size, n_tm * k_loc * variables, block)
     returned = returned.sum(axis=1) if group_size > 1 else returned[:, 0]
     result = jnp.take(returned, owner_map, axis=0, mode="clip")
     result = result.reshape(orders, kmodes, variables, span, lat_count)

time: 200 us -> 196 us (0.980)
  local copies, waits for them, and re-layouts: 73 us -> 69 us
    reshape x1 -> x2, local copies, waits for them, and re-layouts: 7.45 us -> 20.7 us  [body(): result = result.reshape(orders, kmodes, variables, span, lat_count)]
    another operation x1 -> x0, local copies, waits for them, and re-layouts: 12.5 us -> none  [body(): returned = returned.sum(axis=1) if group_size > 1 else returned[:, 0]]
    gather x1, local copies, waits for them, and re-layouts: 6.79 us -> 1.94 us  [body(): result = jnp.take(returned, owner_map, axis=0, mode='clip')]
where the time goes in v7:
time: 196 us; the launch traced here: 195 us
  waiting for transfers between devices  90.9 us (46%)
  local copies, waits for them, and re-layouts  69 us (35%)
  Pallas kernels  21.6 us (11%)
  starting transfers between devices  11.2 us (6%)
  matrix products  2.49 us (1%)
    all_to_all x1, waiting for transfers between devices, body(): returned = lax.all_to_all(synth, AXES, 0, 0, tiled=True)  45.7 us
    all_to_all x1, waiting for transfers between devices, body(): incoming = lax.all_to_all(outgoing, AXES, 0, 0, tiled=True)  45.2 us
    pallas_call x1, Pallas kernels, filter_rows(): pl.pallas_call(filter_kernel, grid=(k_loc,), in_specs=[pl.BlockSpec((1, r...  21.6 us
    reshape x2, local copies, waits for them, and re-layouts, body(): result = result.reshape(orders, kmodes, variables, span, lat_count)  20.7 us
    reshape x2, local copies, waits for them, and re-layouts, body(): fields.transpose(3, 0, 1, 4, 2).reshape(orders, variables, lev, block)  15.4 us
    reshape x1, local copies, waits for them, and re-layouts, body(): incoming = incoming.reshape(n_lat, n_tm, k_loc, variables, span, lat_count)  12.5 us
    reshape x1, local copies, waits for them, and re-layouts, body(): synth = synth.reshape(n_lat * n_tm, k_loc * variables, block)  10.6 us
    all_to_all x1, starting transfers between devices, body(): incoming = lax.all_to_all(outgoing, AXES, 0, 0, tiled=True)  7.33 us
  transfers between devices with their start and end apart: 2, of which 2 were waited for; matrix products, arithmetic and copies ran while one was open for 0% of the time, Pallas kernels for 0%

profile of v7, /device:TPU:0, one launch (start us, length us, event | category | flops | bytes accessed | tf_op | source)
XLA Modules:
  0.0 195.4 jit_solution(16815339502895993252)
XLA Ops:
  0.0 0.0 copy-start
  0.0 12.9 %reshape.23 = bf16[16,3,20,1280]{3,0,2,1:T(8,128)(2,1)} reshape(bf16[16,3,20,32,40]{4,3,0,2,1:T(8,128)(2,1)} %bitcast.25) | data formatting | bytes 4915200 | tf_op jit(solution)/shard_map/reshape | solution.py:65
  12.9 0.0 copy-start.3
  12.9 2.5 %copy.18 = bf16[16,3,20,1280]{3,2,1,0:T(8,128)(2,1)S(1)} copy(bf16[16,3,20,1280]{3,0,2,1:T(8,128)(2,1)} %reshape.23) | data formatting | bytes 4915200 | tf_op jit(solution)/shard_map/reshape | solution.py:65
  15.4 0.0 copy-done.3
  15.4 0.1 select_reduce_fusion
  15.5 0.7 gather_fusion
  16.2 2.3 %gather_fusion.1 = bf16[16,3,20,1280]{3,2,1,0:T(8,128)(2,1)} fusion(bf16[16,3,20,1280]{3,2,1,0:T(8,128)(2,1)S(1)} %copy.18, s32[1024]{0:T(1024)S(1)} %pad_clamp_fusion.1), kind=kCustom, calls=%fused_computation.1 | custom fusion | bytes 4915264 | tf_op jit(solution)/shard_map/jit(_take)/gather | solution.py:67
  18.6 0.0 copy-done
  18.6 2.5 %fusion = bf16[16,2,8,3,1280]{4,2,1,3,0:T(8,128)(2,1)S(1)} fusion(bf16[16,3,20,1280]{3,2,1,0:T(8,128)(2,1)} %gather_fusion.1, bf16[20,16]{0,1:T(8,128)(2,1)S(1)} %copy-done), kind=kOutput, calls=%fused_computation.5 | convolution fusion | flops 40304640 | bytes 4424320 | tf_op jit(solution)/shard_map/jvlx,lus->jusvx/dot_general | solution.py:69
  21.0 1.4 copy.24
  22.4 2.8 %reshape.58 = bf16[32,24,1280]{2,1,0:T(8,128)(2,1)} reshape(bf16[16,2,8,3,1280]{4,3,2,1,0:T(4,128)(2,1)S(1)} %copy.24) | data formatting | bytes 3932160 | tf_op jit(solution)/shard_map/reshape | solution.py:72
  25.2 0.0 copy-start.2
  25.2 7.3 %all-to-all-start = ((bf16[32,24,1280]{2,1,0:T(8,128)(2,1)}), bf16[32,24,1280]{2,1,0:T(8,128)(2,1)S(1)}, u32[]{:S(2)}, u32[]{:S(2)}) async-start(bf16[32,24,1280]{2,1,0:T(8,128)(2,1)} %reshape.58), calls=%async_computation | async-start | bytes 3932160 | tf_op jit(solution)/shard_map/all_to_all | solution.py:73
  32.6 0.0 copy-done.2
  32.6 0.6 reshape.27.m_ref
  33.2 45.2 %all-to-all-done = bf16[32,24,1280]{2,1,0:T(8,128)(2,1)S(1)} async-done(((bf16[32,24,1280]{2,1,0:T(8,128)(2,1)}), bf16[32,24,1280]{2,1,0:T(8,128)(2,1)S(1)}, u32[]{:S(2)}, u32[]{:S(2)}) %all-to-all-start) | async-done | bytes 1966112 | tf_op jit(solution)/shard_map/all_to_all | solution.py:73
  78.4 12.5 %reshape.26.r_ref = bf16[16,2,8,3,32,40]{5,4,3,2,1,0:T(8,128)(2,1)} reshape(bf16[32,24,1280]{2,1,0:T(8,128)(2,1)S(1)} %all-to-all-done) | data formatting | bytes 3932160 | tf_op jit(solution)/shard_map/reshape | solution.py:74
  90.9 21.6 %shard_map.55 = bf16[16,2,8,3,32,40]{5,4,3,2,1,0:T(8,128)(2,1)} custom-call(bf16[8,960,1920]{2,1,0:T(8,128)(2,1)} %t_ref.1, bf16[16,2,8,3,32,40]{5,4,3,2,1,0:T(8,128)(2,1)} %reshape.26.r_ref, f32[8,1,960]{2,1,0:T(1,128)} %reshape.27.m_ref), custom_call_target="tpu_custom_call" | custom-call | tf_op jit(solution)/shard_map/pallas_call | solution.py:42
  112.5 10.6 %reshape.28 = bf16[32,24,1280]{2,1,0:T(8,128)(2,1)} reshape(bf16[16,2,8,3,32,40]{5,4,3,2,1,0:T(8,128)(2,1)} %shard_map.55) | data formatting | bytes 3932160 | tf_op jit(solution)/shard_map/reshape | solution.py:78
  123.2 3.8 %all-to-all-start.1 = ((bf16[32,24,1280]{2,1,0:T(8,128)(2,1)}), bf16[32,24,1280]{2,1,0:T(8,128)(2,1)S(1)}, u32[]{:S(2)}, u32[]{:S(2)}) async-start(bf16[32,24,1280]{2,1,0:T(8,128)(2,1)} %reshape.28), calls=%async_computation.1 | async-start | bytes 3932160 | tf_op jit(solution)/shard_map/all_to_all | solution.py:79
  127.0 45.7 %all-to-all-done.1 = bf16[32,24,1280]{2,1,0:T(8,128)(2,1)S(1)} async-done(((bf16[32,24,1280]{2,1,0:T(8,128)(2,1)}), bf16[32,24,1280]{2,1,0:T(8,128)(2,1)S(1)}, u32[]{:S(2)}, u32[]{:S(2)}) %all-to-all-start.1) | async-done | bytes 1966112 | tf_op jit(solution)/shard_map/all_to_all | solution.py:79
  172.7 1.9 gather_fusion.2
  174.7 13.3 %reshape.29 = bf16[16,16,3,32,40]{4,3,2,1,0:T(8,128)(2,1)} reshape(bf16[16,48,1280]{2,1,0:T(8,128)(2,1)} %gather_fusion.2) | data formatting | bytes 3932160 | tf_op jit(solution)/shard_map/reshape | solution.py:83
  187.9 0.0 copy-start.1
  187.9 7.5 %copy.27 = bf16[16,16,3,32,40]{4,3,0,2,1:T(8,128)(2,1)} copy(bf16[16,16,3,32,40]{4,3,2,1,0:T(8,128)(2,1)} %reshape.29) | data formatting | bytes 3932160 | tf_op jit(solution)/shard_map/reshape | solution.py:83
  195.4 0.0 copy-done.1
  (5 shorter events, 0.0 us)
Async XLA Ops:
  0.0 18.6 %copy-start = (bf16[20,16]{0,1:T(8,128)(2,1)S(1)}, bf16[20,16]{0,1:T(8,128)(2,1)}, u32[]{:S(2)}) copy-start(bf16[20,16]{0,1:T(8,128)(2,1)} %param.6) | copy-start | bytes 1924
  12.9 2.5 %copy-start.3 = (s32[16]{0:T(128)S(1)}, s32[16]{0:T(128)}, u32[]{:S(2)}) copy-start(s32[16]{0:T(128)} %param.7) | copy-start | bytes 196
  25.2 7.3 %copy-start.2 = (s32[8,960]{1,0:T(8,128)S(1)}, s32[8,960]{1,0:T(8,128)}, u32[]{:S(2)}) copy-start(s32[8,960]{1,0:T(8,128)} %param.9) | copy-start | bytes 92164
  25.2 53.2 %all-to-all-start = ((bf16[32,24,1280]{2,1,0:T(8,128)(2,1)}), bf16[32,24,1280]{2,1,0:T(8,128)(2,1)S(1)}, u32[]{:S(2)}, u32[]{:S(2)}) async-start(bf16[32,24,1280]{2,1,0:T(8,128)(2,1)} %reshape.58), calls=%async_computation | async-start | bytes 3932160 | tf_op jit(solution)/shard_map/all_to_all | solution.py:73
  123.2 49.5 %all-to-all-start.1 = ((bf16[32,24,1280]{2,1,0:T(8,128)(2,1)}), bf16[32,24,1280]{2,1,0:T(8,128)(2,1)S(1)}, u32[]{:S(2)}, u32[]{:S(2)}) async-start(bf16[32,24,1280]{2,1,0:T(8,128)(2,1)} %reshape.28), calls=%async_computation.1 | async-start | bytes 3932160 | tf_op jit(solution)/shard_map/all_to_all | solution.py:79
  187.9 7.5 %copy-start.1 = (bf16[20,16]{0,1:T(8,128)(2,1)S(1)}, bf16[20,16]{0,1:T(8,128)(2,1)}, u32[]{:S(2)}) copy-start(bf16[20,16]{0,1:T(8,128)(2,1)} %param.6) | copy-start | bytes 1924

commit v8 on v7

--- a/solution.py
+++ b/solution.py
@@ -1,3 +1,4 @@
+import math
 import jax
 import jax.numpy as jnp
 from jax import lax
@@ -6,6 +7,7 @@
 from jax.sharding import PartitionSpec as P
 
 AXES = ("lat", "tm")
+CHUNKS = 2
 
 
 def order_of_slot(owner_map):
@@ -34,8 +36,9 @@
                 o_ref[i, t, 0, v] = y_scr[pl.ds(t * span, span), pl.ds(v * seg + i * lat_count, lat_count)]
 
 
-def filter_rows(hough_table, received, mask, out_dtype):
-    k_loc, rows, width = hough_table.shape
+def filter_rows(hough_table, received, mask, out_dtype, first):
+    _, rows, width = hough_table.shape
+    k_loc = received.shape[2]
     n_lat, n_tm, _, variables, span, lat_count = received.shape
     cols = n_tm * span
     block = (n_lat, n_tm, 1, variables, span, lat_count)
@@ -43,9 +46,9 @@
         filter_kernel,
         grid=(k_loc,),
         in_specs=[
-            pl.BlockSpec((1, rows, width), lambda k: (k, 0, 0)),
+            pl.BlockSpec((1, rows, width), lambda k: (k + first, 0, 0)),
             pl.BlockSpec(block, lambda k: (0, 0, k, 0, 0, 0)),
-            pl.BlockSpec((1, 1, rows), lambda k: (k, 0, 0)),
+            pl.BlockSpec((1, 1, rows), lambda k: (k + first, 0, 0)),
         ],
         out_specs=pl.BlockSpec(block, lambda k: (0, 0, k, 0, 0, 0)),
         out_shape=jax.ShapeDtypeStruct(received.shape, out_dtype),
@@ -69,14 +72,21 @@
     outgoing = jnp.einsum(
         "jvlx,lus->jusvx", picked, vm, preferred_element_type=jnp.float32
     ).astype(jnp.bfloat16)
-    outgoing = outgoing.reshape(n_lat * n_tm, k_loc * variables, block)
-    incoming = lax.all_to_all(outgoing, AXES, 0, 0, tiled=True)
-    incoming = incoming.reshape(n_lat, n_tm, k_loc, variables, span, lat_count)
     mask = keep_mask.astype(jnp.float32).reshape(k_loc, 1, -1)
     out_dtype = jnp.bfloat16 if group_size == 1 else jnp.float32
-    synth = filter_rows(hough_table, incoming, mask, out_dtype)
-    synth = synth.reshape(n_lat * n_tm, k_loc * variables, block)
-    returned = lax.all_to_all(synth, AXES, 0, 0, tiled=True)
+    chunks = math.gcd(k_loc, CHUNKS)
+    k_chunk = k_loc // chunks
+    pieces = []
+    for q in range(chunks):
+        part = outgoing[:, :, q * k_chunk:(q + 1) * k_chunk]
+        part = part.reshape(n_lat * n_tm, k_chunk * variables, block)
+        incoming = lax.all_to_all(part, AXES, 0, 0, tiled=True)
+        incoming = incoming.reshape(n_lat, n_tm, k_chunk, variables, span, lat_count)
+        synth = filter_rows(hough_table, incoming, mask, out_dtype, q * k_chunk)
+        synth = synth.reshape(n_lat * n_tm, k_chunk * variables, block)
+        back = lax.all_to_all(synth, AXES, 0, 0, tiled=True)
+        pieces.append(back.reshape(n_lat * n_tm, k_chunk, variables * block))
+    returned = jnp.concatenate(pieces, axis=1) if chunks > 1 else pieces[0]
     returned = returned.reshape(orders, group_size, n_tm * k_loc * variables, block)
     returned = returned.sum(axis=1) if group_size > 1 else returned[:, 0]
     result = jnp.take(returned, owner_map, axis=0, mode="clip")

time: 196 us -> 201 us (1.026)
  waiting for transfers between devices: 90.9 us -> 69 us
  local copies, waits for them, and re-layouts: 69 us -> 82.6 us
  starting transfers between devices: 11.2 us -> 18.4 us
  other arithmetic: 0.14 us -> 3.26 us
  Pallas kernels: 21.6 us -> 24.4 us
    all_to_all x2 -> x4, waiting for transfers between devices: 90.9 us -> 69 us  [the longest x2 36.1 us: body(): back = lax.all_to_all(synth, AXES, 0, 0, tiled=True)]
    reshape x4 -> x10, local copies, waits for them, and re-layouts: 27.3 us -> 36.9 us  [the longest x2 14.1 us: body(): incoming.reshape(n_lat, n_tm, k_chunk, variables, span, lat_count)]
    all_to_all x2 -> x4, starting transfers between devices: 11.2 us -> 18.4 us  [the longest x2 10.9 us: body(): incoming = lax.all_to_all(part, AXES, 0, 0, tiled=True)]
    pallas_call x1 -> x2, Pallas kernels: 21.6 us -> 24.4 us  [filter_rows(): pl.pallas_call(filter_kernel, grid=(k_loc,), in_specs=[pl.BlockSpec((1, r...]
    concatenate x0 -> x1, other arithmetic: none -> 2.45 us  [body(): returned = jnp.concatenate(pieces, axis=1) if chunks > 1 else pieces[0]]
  transfers between devices with their start and end apart: 2 -> 4, of which waited for: 2 -> 4; matrix products, arithmetic and copies ran while one was open for 0% -> 17% of each run, Pallas kernels for 0% -> 12%
where the time goes in v8:
time: 201 us; the launch traced here: 200 us
  local copies, waits for them, and re-layouts  82.6 us (41%)
  waiting for transfers between devices  69 us (34%)
  Pallas kernels  24.4 us (12%)
  starting transfers between devices  18.4 us (9%)
  other arithmetic  3.26 us (2%)
  matrix products  2.49 us (1%)
    all_to_all x2, waiting for transfers between devices, body(): back = lax.all_to_all(synth, AXES, 0, 0, tiled=True)  36.1 us
    all_to_all x2, waiting for transfers between devices, body(): incoming = lax.all_to_all(part, AXES, 0, 0, tiled=True)  32.9 us
    pallas_call x2, Pallas kernels, filter_rows(): pl.pallas_call(filter_kernel, grid=(k_loc,), in_specs=[pl.BlockSpec((1, r...  24.4 us
    reshape x2, local copies, waits for them, and re-layouts, body(): result = result.reshape(orders, kmodes, variables, span, lat_count)  20 us
    reshape x2, local copies, waits for them, and re-layouts, body(): fields.transpose(3, 0, 1, 4, 2).reshape(orders, variables, lev, block)  15.4 us
    reshape x2, local copies, waits for them, and re-layouts, body(): incoming.reshape(n_lat, n_tm, k_chunk, variables, span, lat_count)  14.1 us
    reshape x2, local copies, waits for them, and re-layouts, body(): synth = synth.reshape(n_lat * n_tm, k_chunk * variables, block)  13.9 us
    all_to_all x2, starting transfers between devices, body(): incoming = lax.all_to_all(part, AXES, 0, 0, tiled=True)  10.9 us
  transfers between devices with their start and end apart: 4, of which 4 were waited for; matrix products, arithmetic and copies ran while one was open for 17% of the time, Pallas kernels for 12%

profile of v8, /device:TPU:0, one launch (start us, length us, event | category | flops | bytes accessed | tf_op | source)
XLA Modules:
  0.0 200.2 jit_solution(12142924506579733004)
XLA Ops:
  0.0 0.8 select_reduce_fusion
  0.8 0.7 gather_fusion
  1.5 12.9 %reshape.38 = bf16[16,3,20,1280]{3,0,2,1:T(8,128)(2,1)} reshape(bf16[16,3,20,32,40]{4,3,0,2,1:T(8,128)(2,1)} %bitcast.26) | data formatting | bytes 4915200 | tf_op jit(solution)/shard_map/reshape | solution.py:68
  14.4 2.5 %copy.40 = bf16[16,3,20,1280]{3,2,1,0:T(8,128)(2,1)S(1)} copy(bf16[16,3,20,1280]{3,0,2,1:T(8,128)(2,1)} %reshape.38) | data formatting | bytes 4915200 | tf_op jit(solution)/shard_map/reshape | solution.py:68
  16.8 2.3 %gather_fusion.1 = bf16[16,3,20,1280]{3,2,1,0:T(8,128)(2,1)} fusion(bf16[16,3,20,1280]{3,2,1,0:T(8,128)(2,1)S(1)} %copy.40, s32[1024]{0:T(1024)S(1)} %pad_clamp_fusion.1), kind=kCustom, calls=%fused_computation.1 | custom fusion | bytes 4915264 | tf_op jit(solution)/shard_map/jit(_take)/gather | solution.py:70
  19.2 2.5 %fusion = bf16[16,2,8,3,1280]{4,2,1,3,0:T(8,128)(2,1)S(1)} fusion(bf16[16,3,20,1280]{3,2,1,0:T(8,128)(2,1)} %gather_fusion.1, bf16[20,16]{0,1:T(8,128)(2,1)S(1)} %copy-done), kind=kOutput, calls=%fused_computation.5 | convolution fusion | flops 40304640 | bytes 4424320 | tf_op jit(solution)/shard_map/jvlx,lus->jusvx/dot_general | solution.py:72
  21.7 1.6 fusion.3
  23.9 1.7 reshape.81
  25.6 7.3 %all-to-all-start.2 = ((bf16[32,12,1280]{2,1,0:T(8,128)(2,1)}), bf16[32,12,1280]{2,1,0:T(8,128)(2,1)S(1)}, u32[]{:S(2)}, u32[]{:S(2)}) async-start(bf16[32,12,1280]{2,1,0:T(8,128)(2,1)} %reshape.81), calls=%async_computation.2 | async-start | bytes 2621440 | tf_op jit(solution)/shard_map/all_to_all | solution.py:83
  32.9 1.8 copy.56
  34.8 1.7 reshape.78
  36.5 28.3 %all-to-all-done.2 = bf16[32,12,1280]{2,1,0:T(8,128)(2,1)S(1)} async-done(((bf16[32,12,1280]{2,1,0:T(8,128)(2,1)}), bf16[32,12,1280]{2,1,0:T(8,128)(2,1)S(1)}, u32[]{:S(2)}, u32[]{:S(2)}) %all-to-all-start.2) | async-done | bytes 983072 | tf_op jit(solution)/shard_map/all_to_all | solution.py:83
  64.8 1.1 copy-done.2
  65.8 3.6 %all-to-all-start = ((bf16[32,12,1280]{2,1,0:T(8,128)(2,1)}), bf16[32,12,1280]{2,1,0:T(8,128)(2,1)S(1)}, u32[]{:S(2)}, u32[]{:S(2)}) async-start(bf16[32,12,1280]{2,1,0:T(8,128)(2,1)} %reshape.78), calls=%async_computation | async-start | bytes 2621440 | tf_op jit(solution)/shard_map/all_to_all | solution.py:83
  70.1 7.4 %reshape.82.r_ref = bf16[16,2,4,3,32,40]{5,4,3,2,1,0:T(8,128)(2,1)} reshape(bf16[32,12,1280]{2,1,0:T(8,128)(2,1)} %copy-done.2) | data formatting | bytes 1966080 | tf_op jit(solution)/shard_map/reshape | solution.py:84
  77.5 12.2 %shard_map.56 = bf16[16,2,4,3,32,40]{5,4,3,2,1,0:T(8,128)(2,1)} custom-call(bf16[8,960,1920]{2,1,0:T(8,128)(2,1)} %t_ref.3, bf16[16,2,4,3,32,40]{5,4,3,2,1,0:T(8,128)(2,1)} %reshape.82.r_ref, f32[8,1,960]{2,1,0:T(1,128)} %reshape.42.m_ref), custom_call_target="tpu_custom_call" | custom-call | tf_op jit(solution)/shard_map/pallas_call | solution.py:45
  89.8 6.9 %reshape.83 = bf16[32,12,1280]{2,1,0:T(8,128)(2,1)} reshape(bf16[16,2,4,3,32,40]{5,4,3,2,1,0:T(8,128)(2,1)} %shard_map.56) | data formatting | bytes 1966080 | tf_op jit(solution)/shard_map/reshape | solution.py:86
  96.7 4.6 %all-to-all-done = bf16[32,12,1280]{2,1,0:T(8,128)(2,1)S(1)} async-done(((bf16[32,12,1280]{2,1,0:T(8,128)(2,1)}), bf16[32,12,1280]{2,1,0:T(8,128)(2,1)S(1)}, u32[]{:S(2)}, u32[]{:S(2)}) %all-to-all-start) | async-done | bytes 983072 | tf_op jit(solution)/shard_map/all_to_all | solution.py:83
  101.3 3.8 %all-to-all-start.3 = ((bf16[32,12,1280]{2,1,0:T(8,128)(2,1)}), bf16[32,12,1280]{2,1,0:T(8,128)(2,1)S(1)}, u32[]{:S(2)}, u32[]{:S(2)}) async-start(bf16[32,12,1280]{2,1,0:T(8,128)(2,1)} %reshape.83), calls=%async_computation.3 | async-start | bytes 2621440 | tf_op jit(solution)/shard_map/all_to_all | solution.py:87
  105.1 6.6 %reshape.79.r_ref = bf16[16,2,4,3,32,40]{5,4,3,2,1,0:T(8,128)(2,1)} reshape(bf16[32,12,1280]{2,1,0:T(8,128)(2,1)S(1)} %all-to-all-done) | data formatting | bytes 1966080 | tf_op jit(solution)/shard_map/reshape | solution.py:84
  111.7 12.2 %shard_map.55 = bf16[16,2,4,3,32,40]{5,4,3,2,1,0:T(8,128)(2,1)} custom-call(bf16[8,960,1920]{2,1,0:T(8,128)(2,1)} %t_ref.3, bf16[16,2,4,3,32,40]{5,4,3,2,1,0:T(8,128)(2,1)} %reshape.79.r_ref, f32[8,1,960]{2,1,0:T(1,128)} %reshape.42.m_ref), custom_call_target="tpu_custom_call" | custom-call | tf_op jit(solution)/shard_map/pallas_call | solution.py:45
  123.9 6.9 %reshape.80 = bf16[32,12,1280]{2,1,0:T(8,128)(2,1)} reshape(bf16[16,2,4,3,32,40]{5,4,3,2,1,0:T(8,128)(2,1)} %shard_map.55) | data formatting | bytes 1966080 | tf_op jit(solution)/shard_map/reshape | solution.py:86
  130.9 5.9 %all-to-all-done.3 = bf16[32,12,1280]{2,1,0:T(8,128)(2,1)S(1)} async-done(((bf16[32,12,1280]{2,1,0:T(8,128)(2,1)}), bf16[32,12,1280]{2,1,0:T(8,128)(2,1)S(1)}, u32[]{:S(2)}, u32[]{:S(2)}) %all-to-all-start.3) | async-done | bytes 983072 | tf_op jit(solution)/shard_map/all_to_all | solution.py:87
  136.8 3.6 %all-to-all-start.1 = ((bf16[32,12,1280]{2,1,0:T(8,128)(2,1)}), bf16[32,12,1280]{2,1,0:T(8,128)(2,1)S(1)}, u32[]{:S(2)}, u32[]{:S(2)}) async-start(bf16[32,12,1280]{2,1,0:T(8,128)(2,1)} %reshape.80), calls=%async_computation.1 | async-start | bytes 2621440 | tf_op jit(solution)/shard_map/all_to_all | solution.py:87
  140.4 1.5 reshape.48
  142.0 30.2 %all-to-all-done.1 = bf16[32,12,1280]{2,1,0:T(8,128)(2,1)S(1)} async-done(((bf16[32,12,1280]{2,1,0:T(8,128)(2,1)}), bf16[32,12,1280]{2,1,0:T(8,128)(2,1)S(1)}, u32[]{:S(2)}, u32[]{:S(2)}) %all-to-all-start.1) | async-done | bytes 983072 | tf_op jit(solution)/shard_map/all_to_all | solution.py:87
  172.2 1.5 reshape.44
  173.7 2.4 %pad_maximum_fusion = bf16[32,8,3840]{2,1,0:T(8,128)(2,1)S(1)} fusion(bf16[32,4,3840]{2,1,0:T(4,128)(2,1)} %reshape.48, bf16[32,4,3840]{2,1,0:T(4,128)(2,1)} %reshape.44), kind=kLoop, calls=%fused_computation.7 | loop fusion | flops 3932160 | bytes 3932160 | tf_op jit(solution)/shard_map/concatenate | solution.py:89
  176.2 1.9 squeeze_reshape.3
  178.1 2.2 %gather_fusion.2 = bf16[16,48,1280]{2,1,0:T(8,128)(2,1)S(1)} fusion(bf16[16,48,1280]{2,1,0:T(8,128)(2,1)} %squeeze_reshape.3, s32[1024]{0:T(1024)S(1)} %pad_clamp_fusion), kind=kCustom, calls=%fused_computation.2 | custom fusion | bytes 3932224 | tf_op jit(solution)/shard_map/jit(_take)/gather | solution.py:92
  180.3 12.5 %reshape.49 = bf16[16,16,3,32,40]{4,3,2,1,0:T(8,128)(2,1)} reshape(bf16[16,48,1280]{2,1,0:T(8,128)(2,1)S(1)} %gather_fusion.2) | data formatting | bytes 3932160 | tf_op jit(solution)/shard_map/reshape | solution.py:93
  192.8 7.5 %copy.65 = bf16[16,16,3,32,40]{4,3,0,2,1:T(8,128)(2,1)} copy(bf16[16,16,3,32,40]{4,3,2,1,0:T(8,128)(2,1)} %reshape.49) | data formatting | bytes 3932160 | tf_op jit(solution)/shard_map/reshape | solution.py:93
  (16 shorter events, 1.3 us)
Async XLA Ops:
  0.0 19.2 %copy-start = (bf16[20,16]{0,1:T(8,128)(2,1)S(1)}, bf16[20,16]{0,1:T(8,128)(2,1)}, u32[]{:S(2)}) copy-start(bf16[20,16]{0,1:T(8,128)(2,1)} %param.6) | copy-start | bytes 1924
  25.6 39.2 %all-to-all-start.2 = ((bf16[32,12,1280]{2,1,0:T(8,128)(2,1)}), bf16[32,12,1280]{2,1,0:T(8,128)(2,1)S(1)}, u32[]{:S(2)}, u32[]{:S(2)}) async-start(bf16[32,12,1280]{2,1,0:T(8,128)(2,1)} %reshape.81), calls=%async_computation.2 | async-start | bytes 2621440 | tf_op jit(solution)/shard_map/all_to_all | solution.py:83
  36.5 33.0 %copy-start.3 = (s32[8,960]{1,0:T(8,128)S(1)}, s32[8,960]{1,0:T(8,128)}, u32[]{:S(2)}) copy-start(s32[8,960]{1,0:T(8,128)} %param.9) | copy-start | bytes 92164
  64.8 1.1 copy-start.2
  65.8 35.4 %all-to-all-start = ((bf16[32,12,1280]{2,1,0:T(8,128)(2,1)}), bf16[32,12,1280]{2,1,0:T(8,128)(2,1)S(1)}, u32[]{:S(2)}, u32[]{:S(2)}) async-start(bf16[32,12,1280]{2,1,0:T(8,128)(2,1)} %reshape.78), calls=%async_computation | async-start | bytes 2621440 | tf_op jit(solution)/shard_map/all_to_all | solution.py:83
  101.3 35.5 %all-to-all-start.3 = ((bf16[32,12,1280]{2,1,0:T(8,128)(2,1)}), bf16[32,12,1280]{2,1,0:T(8,128)(2,1)S(1)}, u32[]{:S(2)}, u32[]{:S(2)}) async-start(bf16[32,12,1280]{2,1,0:T(8,128)(2,1)} %reshape.83), calls=%async_computation.3 | async-start | bytes 2621440 | tf_op jit(solution)/shard_map/all_to_all | solution.py:87
  130.9 9.5 %copy-start.4 = (s32[16]{0:T(128)S(1)}, s32[16]{0:T(128)}, u32[]{:S(2)}) copy-start(s32[16]{0:T(128)} %param.7) | copy-start | bytes 196
  136.8 35.4 %all-to-all-start.1 = ((bf16[32,12,1280]{2,1,0:T(8,128)(2,1)}), bf16[32,12,1280]{2,1,0:T(8,128)(2,1)S(1)}, u32[]{:S(2)}, u32[]{:S(2)}) async-start(bf16[32,12,1280]{2,1,0:T(8,128)(2,1)} %reshape.80), calls=%async_computation.1 | async-start | bytes 2621440 | tf_op jit(solution)/shard_map/all_to_all | solution.py:87
  192.8 7.5 %copy-start.1 = (bf16[20,16]{0,1:T(8,128)(2,1)S(1)}, bf16[20,16]{0,1:T(8,128)(2,1)}, u32[]{:S(2)}) copy-start(bf16[20,16]{0,1:T(8,128)(2,1)} %param.6) | copy-start | bytes 1924

commit v9 on v8

--- a/solution.py
+++ b/solution.py
@@ -5,6 +5,7 @@
 from jax.experimental import pallas as pl
 from jax.experimental.pallas import tpu as pltpu
 from jax.sharding import PartitionSpec as P
+
 
 AXES = ("lat", "tm")
 CHUNKS = 2
@@ -56,7 +57,7 @@
     )(hough_table, received, mask)
 
 
-def body(fields, vmodes, owner_map, hough_table, keep_mask):
+def body_inner(fields, vmodes, owner_map, hough_table, keep_mask):
     n_lat = lax.axis_size("lat")
     n_tm = lax.axis_size("tm")
     orders = owner_map.shape[0]
@@ -85,11 +86,11 @@
         synth = filter_rows(hough_table, incoming, mask, out_dtype, q * k_chunk)
         synth = synth.reshape(n_lat * n_tm, k_chunk * variables, block)
         back = lax.all_to_all(synth, AXES, 0, 0, tiled=True)
-        pieces.append(back.reshape(n_lat * n_tm, k_chunk, variables * block))
-    returned = jnp.concatenate(pieces, axis=1) if chunks > 1 else pieces[0]
-    returned = returned.reshape(orders, group_size, n_tm * k_loc * variables, block)
-    returned = returned.sum(axis=1) if group_size > 1 else returned[:, 0]
-    result = jnp.take(returned, owner_map, axis=0, mode="clip")
+        back = back.reshape(orders, group_size, n_tm * k_chunk * variables, block)
+        back = back.sum(axis=1) if group_size > 1 else back[:, 0]
+        back = jnp.take(back, owner_map, axis=0, mode="clip")
+        pieces.append(back.reshape(orders, n_tm, k_chunk, variables, span, lat_count))
+    result = jnp.concatenate(pieces, axis=2) if chunks > 1 else pieces[0]
     result = result.reshape(orders, kmodes, variables, span, lat_count)
     return result.transpose(1, 2, 4, 0, 3).astype(jnp.bfloat16)
 
@@ -97,4 +98,4 @@
 def solution(mesh):
     in_specs = (P(None, None, "lat", None, "tm"), P(), P(), P("tm", "lat", None), P("tm", "lat"))
     out_specs = P(None, None, "lat", None, "tm")
-    return jax.shard_map(body, mesh=mesh, in_specs=in_specs, out_specs=out_specs, check_vma=False)
+    return jax.shard_map(body_inner, mesh=mesh, in_specs=in_specs, out_specs=out_specs, check_vma=False)

time: 201 us -> 197 us (0.980)
  local copies, waits for them, and re-layouts: 82.6 us -> 80 us
  waiting for transfers between devices: 69 us -> 66.6 us
    reshape x15 -> x13, local copies, waits for them, and re-layouts: 72.8 us -> 64.1 us  [the longest x2 15.4 us: body_inner(): fields.transpose(3, 0, 1, 4, 2).reshape(orders, variables, lev, block)]
    concatenate x0 -> x1, local copies, waits for them, and re-layouts: none -> 4.54 us  [body_inner(): result = jnp.concatenate(pieces, axis=2) if chunks > 1 else pieces[0]]
    all_to_all x4, waiting for transfers between devices: 69 us -> 66.6 us  [the longest x2 33.8 us: body_inner(): back = lax.all_to_all(synth, AXES, 0, 0, tiled=True)]
    gather x3 -> x4, local copies, waits for them, and re-layouts: 5.21 us -> 7.36 us  [the longest x2 4.36 us: body_inner(): back = jnp.take(back, owner_map, axis=0, mode='clip')]
  transfers between devices with their start and end apart: 4 -> 4, of which waited for: 4 -> 4; matrix products, arithmetic and copies ran while one was open for 17% -> 18% of each run, Pallas kernels for 12% -> 12%
where the time goes in v9:
time: 197 us; the launch traced here: 196 us
  local copies, waits for them, and re-layouts  80 us (41%)
  waiting for transfers between devices  66.6 us (34%)
  Pallas kernels  24.4 us (12%)
  starting transfers between devices  18.4 us (9%)
  other arithmetic  3.91 us (2%)
  matrix products  2.49 us (1%)
    all_to_all x2, waiting for transfers between devices, body_inner(): back = lax.all_to_all(synth, AXES, 0, 0, tiled=True)  33.8 us
    all_to_all x2, waiting for transfers between devices, body_inner(): incoming = lax.all_to_all(part, AXES, 0, 0, tiled=True)  32.8 us
    pallas_call x2, Pallas kernels, filter_rows(): pl.pallas_call(filter_kernel, grid=(k_loc,), in_specs=[pl.BlockSpec((1, r...  24.4 us
    reshape x2, local copies, waits for them, and re-layouts, body_inner(): fields.transpose(3, 0, 1, 4, 2).reshape(orders, variables, lev, block)  15.4 us
    reshape x2, local copies, waits for them, and re-layouts, body_inner(): back.reshape(orders, n_tm, k_chunk, variables, span, lat_count)  14.2 us
    reshape x2, local copies, waits for them, and re-layouts, body_inner(): incoming.reshape(n_lat, n_tm, k_chunk, variables, span, lat_count)  14.1 us
    reshape x2, local copies, waits for them, and re-layouts, body_inner(): synth = synth.reshape(n_lat * n_tm, k_chunk * variables, block)  13.9 us
    all_to_all x2, starting transfers between devices, body_inner(): incoming = lax.all_to_all(part, AXES, 0, 0, tiled=True)  10.9 us
  transfers between devices with their start and end apart: 4, of which 4 were waited for; matrix products, arithmetic and copies ran while one was open for 18% of the time, Pallas kernels for 12%

profile of v9, /device:TPU:0, one launch (start us, length us, event | category | flops | bytes accessed | tf_op | source)
XLA Modules:
  0.0 195.9 jit_solution(17549582470125522394)
XLA Ops:
  0.0 0.8 select_reduce_fusion
  0.8 0.7 gather_fusion
  1.5 12.9 %reshape.38 = bf16[16,3,20,1280]{3,0,2,1:T(8,128)(2,1)} reshape(bf16[16,3,20,32,40]{4,3,0,2,1:T(8,128)(2,1)} %bitcast.26) | data formatting | bytes 4915200 | tf_op jit(solution)/shard_map/reshape | solution.py:69
  14.4 2.5 %copy.42 = bf16[16,3,20,1280]{3,2,1,0:T(8,128)(2,1)S(1)} copy(bf16[16,3,20,1280]{3,0,2,1:T(8,128)(2,1)} %reshape.38) | data formatting | bytes 4915200 | tf_op jit(solution)/shard_map/reshape | solution.py:69
  16.8 2.3 %gather_fusion.1 = bf16[16,3,20,1280]{3,2,1,0:T(8,128)(2,1)} fusion(bf16[16,3,20,1280]{3,2,1,0:T(8,128)(2,1)S(1)} %copy.42, s32[1024]{0:T(1024)S(1)} %pad_clamp_fusion.1), kind=kCustom, calls=%fused_computation.1 | custom fusion | bytes 4915264 | tf_op jit(solution)/shard_map/jit(_take)/gather | solution.py:71
  19.2 2.5 %fusion = bf16[16,2,8,3,1280]{4,2,1,3,0:T(8,128)(2,1)S(1)} fusion(bf16[16,3,20,1280]{3,2,1,0:T(8,128)(2,1)} %gather_fusion.1, bf16[20,16]{0,1:T(8,128)(2,1)S(1)} %copy-done), kind=kOutput, calls=%fused_computation.6 | convolution fusion | flops 40304640 | bytes 4424320 | tf_op jit(solution)/shard_map/jvlx,lus->jusvx/dot_general | solution.py:73
  21.7 1.6 fusion.3
  23.9 1.7 reshape.90
  25.6 7.3 %all-to-all-start.2 = ((bf16[32,12,1280]{2,1,0:T(8,128)(2,1)}), bf16[32,12,1280]{2,1,0:T(8,128)(2,1)S(1)}, u32[]{:S(2)}, u32[]{:S(2)}) async-start(bf16[32,12,1280]{2,1,0:T(8,128)(2,1)} %reshape.90), calls=%async_computation.2 | async-start | bytes 2621440 | tf_op jit(solution)/shard_map/all_to_all | solution.py:84
  32.9 1.8 copy.58
  34.8 1.7 reshape.87
  36.5 28.3 %all-to-all-done.2 = bf16[32,12,1280]{2,1,0:T(8,128)(2,1)S(1)} async-done(((bf16[32,12,1280]{2,1,0:T(8,128)(2,1)}), bf16[32,12,1280]{2,1,0:T(8,128)(2,1)S(1)}, u32[]{:S(2)}, u32[]{:S(2)}) %all-to-all-start.2) | async-done | bytes 983072 | tf_op jit(solution)/shard_map/all_to_all | solution.py:84
  64.8 1.1 copy-done.2
  65.8 3.6 %all-to-all-start = ((bf16[32,12,1280]{2,1,0:T(8,128)(2,1)}), bf16[32,12,1280]{2,1,0:T(8,128)(2,1)S(1)}, u32[]{:S(2)}, u32[]{:S(2)}) async-start(bf16[32,12,1280]{2,1,0:T(8,128)(2,1)} %reshape.87), calls=%async_computation | async-start | bytes 2621440 | tf_op jit(solution)/shard_map/all_to_all | solution.py:84
  70.1 7.4 %reshape.91.r_ref = bf16[16,2,4,3,32,40]{5,4,3,2,1,0:T(8,128)(2,1)} reshape(bf16[32,12,1280]{2,1,0:T(8,128)(2,1)} %copy-done.2) | data formatting | bytes 1966080 | tf_op jit(solution)/shard_map/reshape | solution.py:85
  77.5 12.2 %shard_map.56 = bf16[16,2,4,3,32,40]{5,4,3,2,1,0:T(8,128)(2,1)} custom-call(bf16[8,960,1920]{2,1,0:T(8,128)(2,1)} %t_ref.3, bf16[16,2,4,3,32,40]{5,4,3,2,1,0:T(8,128)(2,1)} %reshape.91.r_ref, f32[8,1,960]{2,1,0:T(1,128)} %reshape.42.m_ref), custom_call_target="tpu_custom_call" | custom-call | tf_op jit(solution)/shard_map/pallas_call | solution.py:46
  89.8 6.9 %reshape.92 = bf16[32,12,1280]{2,1,0:T(8,128)(2,1)} reshape(bf16[16,2,4,3,32,40]{5,4,3,2,1,0:T(8,128)(2,1)} %shard_map.56) | data formatting | bytes 1966080 | tf_op jit(solution)/shard_map/reshape | solution.py:87
  96.7 4.6 %all-to-all-done = bf16[32,12,1280]{2,1,0:T(8,128)(2,1)S(1)} async-done(((bf16[32,12,1280]{2,1,0:T(8,128)(2,1)}), bf16[32,12,1280]{2,1,0:T(8,128)(2,1)S(1)}, u32[]{:S(2)}, u32[]{:S(2)}) %all-to-all-start) | async-done | bytes 983072 | tf_op jit(solution)/shard_map/all_to_all | solution.py:84
  101.3 3.8 %all-to-all-start.3 = ((bf16[32,12,1280]{2,1,0:T(8,128)(2,1)}), bf16[32,12,1280]{2,1,0:T(8,128)(2,1)S(1)}, u32[]{:S(2)}, u32[]{:S(2)}) async-start(bf16[32,12,1280]{2,1,0:T(8,128)(2,1)} %reshape.92), calls=%async_computation.3 | async-start | bytes 2621440 | tf_op jit(solution)/shard_map/all_to_all | solution.py:88
  105.1 6.6 %reshape.88.r_ref = bf16[16,2,4,3,32,40]{5,4,3,2,1,0:T(8,128)(2,1)} reshape(bf16[32,12,1280]{2,1,0:T(8,128)(2,1)S(1)} %all-to-all-done) | data formatting | bytes 1966080 | tf_op jit(solution)/shard_map/reshape | solution.py:85
  111.7 12.2 %shard_map.55 = bf16[16,2,4,3,32,40]{5,4,3,2,1,0:T(8,128)(2,1)} custom-call(bf16[8,960,1920]{2,1,0:T(8,128)(2,1)} %t_ref.3, bf16[16,2,4,3,32,40]{5,4,3,2,1,0:T(8,128)(2,1)} %reshape.88.r_ref, f32[8,1,960]{2,1,0:T(1,128)} %reshape.42.m_ref), custom_call_target="tpu_custom_call" | custom-call | tf_op jit(solution)/shard_map/pallas_call | solution.py:46
  123.9 6.9 %reshape.89 = bf16[32,12,1280]{2,1,0:T(8,128)(2,1)} reshape(bf16[16,2,4,3,32,40]{5,4,3,2,1,0:T(8,128)(2,1)} %shard_map.55) | data formatting | bytes 1966080 | tf_op jit(solution)/shard_map/reshape | solution.py:87
  130.9 5.9 %all-to-all-done.3 = bf16[32,12,1280]{2,1,0:T(8,128)(2,1)S(1)} async-done(((bf16[32,12,1280]{2,1,0:T(8,128)(2,1)}), bf16[32,12,1280]{2,1,0:T(8,128)(2,1)S(1)}, u32[]{:S(2)}, u32[]{:S(2)}) %all-to-all-start.3) | async-done | bytes 983072 | tf_op jit(solution)/shard_map/all_to_all | solution.py:88
  136.8 3.6 %all-to-all-start.1 = ((bf16[32,12,1280]{2,1,0:T(8,128)(2,1)}), bf16[32,12,1280]{2,1,0:T(8,128)(2,1)S(1)}, u32[]{:S(2)}, u32[]{:S(2)}) async-start(bf16[32,12,1280]{2,1,0:T(8,128)(2,1)} %reshape.89), calls=%async_computation.1 | async-start | bytes 2621440 | tf_op jit(solution)/shard_map/all_to_all | solution.py:88
  140.4 1.1 squeeze_reshape.7
  141.5 2.8 %gather_fusion.3 = bf16[16,24,1280]{2,1,0:T(8,128)(2,1)} fusion(bf16[16,24,1280]{2,1,0:T(8,128)(2,1)} %squeeze_reshape.7, s32[1024]{0:T(1024)S(1)} %pad_clamp_fusion), kind=kCustom, calls=%fused_computation.3 | custom fusion | bytes 1966144 | tf_op jit(solution)/shard_map/jit(_take)/gather | solution.py:91
  144.3 27.9 %all-to-all-done.1 = bf16[32,12,1280]{2,1,0:T(8,128)(2,1)S(1)} async-done(((bf16[32,12,1280]{2,1,0:T(8,128)(2,1)}), bf16[32,12,1280]{2,1,0:T(8,128)(2,1)S(1)}, u32[]{:S(2)}, u32[]{:S(2)}) %all-to-all-start.1) | async-done | bytes 983072 | tf_op jit(solution)/shard_map/all_to_all | solution.py:88
  172.5 1.6 gather_fusion.2
  174.0 6.7 %reshape.44 = bf16[16,2,4,3,32,40]{5,4,3,2,1,0:T(8,128)(2,1)S(1)} reshape(bf16[16,24,1280]{2,1,0:T(8,128)(2,1)} %gather_fusion.2) | data formatting | bytes 1966080 | tf_op jit(solution)/shard_map/reshape | solution.py:92
  180.7 7.5 %reshape.48 = bf16[16,2,4,3,32,40]{5,4,3,2,1,0:T(8,128)(2,1)} reshape(bf16[16,24,1280]{2,1,0:T(8,128)(2,1)} %gather_fusion.3) | data formatting | bytes 1966080 | tf_op jit(solution)/shard_map/reshape | solution.py:92
  188.3 3.1 %pad_maximum_fusion = bf16[16,2,8,3,32,40]{5,4,3,2,1,0:T(8,128)(2,1)S(1)} fusion(bf16[16,2,4,3,32,40]{5,4,3,2,1,0:T(8,128)(2,1)} %reshape.48, bf16[16,2,4,3,32,40]{5,4,3,2,1,0:T(8,128)(2,1)S(1)} %reshape.44), kind=kLoop, calls=%fused_computation.4 | loop fusion | flops 983040 | bytes 3932160 | tf_op jit(solution)/shard_map/concatenate | solution.py:93
  191.4 4.5 %copy.55 = bf16[16,2,8,3,32,40]{5,4,0,3,2,1:T(8,128)(2,1)} copy(bf16[16,2,8,3,32,40]{5,4,3,2,1,0:T(8,128)(2,1)S(1)} %pad_maximum_fusion) | data formatting | bytes 3932160 | tf_op jit(solution)/shard_map/concatenate | solution.py:93
  (17 shorter events, 1.6 us)
Async XLA Ops:
  0.0 19.2 %copy-start = (bf16[20,16]{0,1:T(8,128)(2,1)S(1)}, bf16[20,16]{0,1:T(8,128)(2,1)}, u32[]{:S(2)}) copy-start(bf16[20,16]{0,1:T(8,128)(2,1)} %param.6) | copy-start | bytes 1924
  25.6 39.2 %all-to-all-start.2 = ((bf16[32,12,1280]{2,1,0:T(8,128)(2,1)}), bf16[32,12,1280]{2,1,0:T(8,128)(2,1)S(1)}, u32[]{:S(2)}, u32[]{:S(2)}) async-start(bf16[32,12,1280]{2,1,0:T(8,128)(2,1)} %reshape.90), calls=%async_computation.2 | async-start | bytes 2621440 | tf_op jit(solution)/shard_map/all_to_all | solution.py:84
  34.8 34.7 %copy-start.3 = (s32[8,960]{1,0:T(8,128)S(1)}, s32[8,960]{1,0:T(8,128)}, u32[]{:S(2)}) copy-start(s32[8,960]{1,0:T(8,128)} %param.9) | copy-start | bytes 92164
  64.8 1.1 copy-start.2
  65.8 35.4 %all-to-all-start = ((bf16[32,12,1280]{2,1,0:T(8,128)(2,1)}), bf16[32,12,1280]{2,1,0:T(8,128)(2,1)S(1)}, u32[]{:S(2)}, u32[]{:S(2)}) async-start(bf16[32,12,1280]{2,1,0:T(8,128)(2,1)} %reshape.87), calls=%async_computation | async-start | bytes 2621440 | tf_op jit(solution)/shard_map/all_to_all | solution.py:84
  101.3 35.5 %all-to-all-start.3 = ((bf16[32,12,1280]{2,1,0:T(8,128)(2,1)}), bf16[32,12,1280]{2,1,0:T(8,128)(2,1)S(1)}, u32[]{:S(2)}, u32[]{:S(2)}) async-start(bf16[32,12,1280]{2,1,0:T(8,128)(2,1)} %reshape.92), calls=%async_computation.3 | async-start | bytes 2621440 | tf_op jit(solution)/shard_map/all_to_all | solution.py:88
  123.9 16.4 %copy-start.4 = (s32[16]{0:T(128)S(1)}, s32[16]{0:T(128)}, u32[]{:S(2)}) copy-start(s32[16]{0:T(128)} %param.7) | copy-start | bytes 196
  136.8 35.4 %all-to-all-start.1 = ((bf16[32,12,1280]{2,1,0:T(8,128)(2,1)}), bf16[32,12,1280]{2,1,0:T(8,128)(2,1)S(1)}, u32[]{:S(2)}, u32[]{:S(2)}) async-start(bf16[32,12,1280]{2,1,0:T(8,128)(2,1)} %reshape.89), calls=%async_computation.1 | async-start | bytes 2621440 | tf_op jit(solution)/shard_map/all_to_all | solution.py:88
  191.4 4.6 %copy-start.1 = (bf16[20,16]{0,1:T(8,128)(2,1)S(1)}, bf16[20,16]{0,1:T(8,128)(2,1)}, u32[]{:S(2)}) copy-start(bf16[20,16]{0,1:T(8,128)(2,1)} %param.6) | copy-start | bytes 1924

commit v10 on v9

--- a/solution.py
+++ b/solution.py
@@ -62,24 +62,25 @@
     n_tm = lax.axis_size("tm")
     orders = owner_map.shape[0]
     group_size = n_lat // orders
-    variables, lev, lat_count, _, span = fields.shape
+    variables, _, lat_count, _, span = fields.shape
     kmodes = vmodes.shape[1]
     k_loc = kmodes // n_tm
     block = lat_count * span
-    flat = fields.transpose(3, 0, 1, 4, 2).reshape(orders, variables, lev, block)
+    by_order = fields.transpose(3, 0, 1, 4, 2)
     dest_order = order_of_slot(owner_map)[jnp.arange(n_lat, dtype=jnp.int32) // group_size]
-    picked = jnp.take(flat, dest_order, axis=0, mode="clip")
-    vm = vmodes.reshape(lev, n_tm, k_loc)
-    outgoing = jnp.einsum(
-        "jvlx,lus->jusvx", picked, vm, preferred_element_type=jnp.float32
+    projected = jnp.einsum(
+        "mvlca,lk->mkvca", by_order, vmodes, preferred_element_type=jnp.float32
     ).astype(jnp.bfloat16)
+    projected = projected.reshape(orders, n_tm, k_loc, variables, span, lat_count)
     mask = keep_mask.astype(jnp.float32).reshape(k_loc, 1, -1)
     out_dtype = jnp.bfloat16 if group_size == 1 else jnp.float32
     chunks = math.gcd(k_loc, CHUNKS)
     k_chunk = k_loc // chunks
     pieces = []
     for q in range(chunks):
-        part = outgoing[:, :, q * k_chunk:(q + 1) * k_chunk]
+        part = projected[:, :, q * k_chunk:(q + 1) * k_chunk]
+        part = part.reshape(orders, n_tm, k_chunk, variables, block)
+        part = jnp.take(part, dest_order, axis=0, mode="clip")
         part = part.reshape(n_lat * n_tm, k_chunk * variables, block)
         incoming = lax.all_to_all(part, AXES, 0, 0, tiled=True)
         incoming = incoming.reshape(n_lat, n_tm, k_chunk, variables, span, lat_count)

time: 197 us -> 193 us (0.980)
  waiting for transfers between devices: 66.6 us -> 52 us
  matrix products: 2.49 us -> 9.22 us
  local copies, waits for them, and re-layouts: 80 us -> 84.4 us
    all_to_all x2, waiting for transfers between devices: 32.8 us -> 22.9 us  [body_inner(): incoming = lax.all_to_all(part, AXES, 0, 0, tiled=True)]
    dot_general x1, matrix products: 2.49 us -> 9.22 us  [body_inner(): jnp.einsum('mvlca,lk->mkvca', by_order, vmodes, preferred_element_type=jn...]
    all_to_all x2, waiting for transfers between devices: 33.8 us -> 29.1 us  [body_inner(): back = lax.all_to_all(synth, AXES, 0, 0, tiled=True)]
    gather x1 -> x2, local copies, waits for them, and re-layouts: 2.34 us -> 5.26 us  [body_inner(): part = jnp.take(part, dest_order, axis=0, mode='clip')]
    slice x1, local copies, waits for them, and re-layouts: 1.58 us -> 4.21 us  [body_inner(): part = projected[:, :, q * k_chunk:(q + 1) * k_chunk]]
    reshape x2 -> x4, local copies, waits for them, and re-layouts: 15.4 us -> 14.7 us  [body_inner(): part = part.reshape(orders, n_tm, k_chunk, variables, block)]
  transfers between devices with their start and end apart: 4 -> 4, of which waited for: 4 -> 4; matrix products, arithmetic and copies ran while one was open for 18% -> 26% of each run, Pallas kernels for 12% -> 13%
where the time goes in v10:
time: 193 us; the launch traced here: 192 us
  local copies, waits for them, and re-layouts  84.4 us (44%)
  waiting for transfers between devices  52 us (27%)
  Pallas kernels  24.4 us (13%)
  starting transfers between devices  18.8 us (10%)
  matrix products  9.22 us (5%)
  other arithmetic  3.25 us (2%)
    all_to_all x2, waiting for transfers between devices, body_inner(): back = lax.all_to_all(synth, AXES, 0, 0, tiled=True)  29.1 us
    pallas_call x2, Pallas kernels, filter_rows(): pl.pallas_call(filter_kernel, grid=(k_loc,), in_specs=[pl.BlockSpec((1, r...  24.4 us
    all_to_all x2, waiting for transfers between devices, body_inner(): incoming = lax.all_to_all(part, AXES, 0, 0, tiled=True)  22.9 us
    reshape x4, local copies, waits for them, and re-layouts, body_inner(): part = part.reshape(orders, n_tm, k_chunk, variables, block)  14.7 us
    reshape x2, local copies, waits for them, and re-layouts, body_inner(): back.reshape(orders, n_tm, k_chunk, variables, span, lat_count)  14.2 us
    reshape x2, local copies, waits for them, and re-layouts, body_inner(): incoming.reshape(n_lat, n_tm, k_chunk, variables, span, lat_count)  14.1 us
    reshape x2, local copies, waits for them, and re-layouts, body_inner(): synth = synth.reshape(n_lat * n_tm, k_chunk * variables, block)  13.9 us
    all_to_all x2, starting transfers between devices, body_inner(): incoming = lax.all_to_all(part, AXES, 0, 0, tiled=True)  11.2 us
  transfers between devices with their start and end apart: 4, of which 4 were waited for; matrix products, arithmetic and copies ran while one was open for 26% of the time, Pallas kernels for 13%

profile of v10, /device:TPU:0, one launch (start us, length us, event | category | flops | bytes accessed | tf_op | source)
XLA Modules:
  0.0 192.2 jit_solution(2324038656306300020)
XLA Ops:
  0.0 0.7 copy-done
  0.7 9.2 %convert_bitcast_fusion = bf16[16,2,8,3,32,40]{5,2,1,4,3,0:T(8,128)(2,1)S(1)} fusion(bf16[16,3,20,32,40]{4,3,0,2,1:T(8,128)(2,1)} %bitcast.25, bf16[20,16]{0,1:T(8,128)(2,1)S(1)} %copy-done), kind=kOutput, calls=%fused_computation.8 | convolution fusion | flops 40304640 | bytes 4424320 | tf_op jit(solution)/shard_map/mvlca,lk->mkvca/dot_general | solution.py:71
  9.9 4.2 %fusion.5 = (bf16[16,2,4,3,32,40]{5,2,1,4,3,0:T(4,128)(2,1)S(1)}, bf16[16,2,4,3,32,40]{5,2,1,4,3,0:T(4,128)(2,1)}) fusion(bf16[16,2,8,3,32,40]{5,2,1,4,3,0:T(8,128)(2,1)S(1)} %convert_bitcast_fusion), kind=kLoop, calls=%fused_computation.15 | loop fusion | bytes 3932160 | tf_op jit(solution)/shard_map/slice | solution.py:81
  14.1 1.0 copy.82
  15.1 5.5 %reshape.105 = bf16[16,2,4,3,1280]{4,2,3,1,0:T(4,128)(2,1)} reshape(bf16[16,2,4,3,32,40]{5,4,2,3,1,0:T(8,128)(2,1)S(1)} %copy.82) | data formatting | bytes 1966080 | tf_op jit(solution)/shard_map/reshape | solution.py:82
  21.4 2.6 %gather_fusion.1 = bf16[16,2,4,3,1280]{4,2,3,1,0:T(4,128)(2,1)S(1)} fusion(bf16[16,2,4,3,1280]{4,2,3,1,0:T(4,128)(2,1)} %reshape.105, s32[1024]{0:T(1024)S(1)} %pad_clamp_fusion.1), kind=kCustom, calls=%fused_computation.1 | custom fusion | bytes 1966144 | tf_op jit(solution)/shard_map/jit(_take)/gather | solution.py:83
  24.7 1.7 reshape.99
  26.4 7.6 %all-to-all-start = ((bf16[32,12,1280]{2,1,0:T(8,128)(2,1)}), bf16[32,12,1280]{2,1,0:T(8,128)(2,1)}, u32[]{:S(2)}, u32[]{:S(2)}) async-start(bf16[32,12,1280]{2,1,0:T(8,128)(2,1)} %reshape.99), calls=%async_computation | async-start | bytes 2621440 | tf_op jit(solution)/shard_map/all_to_all | solution.py:85
  34.0 2.8 %copy.83 = bf16[16,2,4,3,32,40]{5,4,2,3,1,0:T(8,128)(2,1)S(1)} copy(bf16[16,2,4,3,32,40]{5,2,1,4,3,0:T(4,128)(2,1)} %get-tuple-element.6) | data formatting | bytes 1966080 | tf_op jit(solution)/shard_map/reshape | solution.py:82
  36.9 5.5 %reshape.106 = bf16[16,2,4,3,1280]{4,2,3,1,0:T(4,128)(2,1)} reshape(bf16[16,2,4,3,32,40]{5,4,2,3,1,0:T(8,128)(2,1)S(1)} %copy.83) | data formatting | bytes 1966080 | tf_op jit(solution)/shard_map/reshape | solution.py:82
  42.3 2.6 %gather_fusion.3 = bf16[16,2,4,3,1280]{4,2,3,1,0:T(4,128)(2,1)S(1)} fusion(bf16[16,2,4,3,1280]{4,2,3,1,0:T(4,128)(2,1)} %reshape.106, s32[1024]{0:T(1024)S(1)} %pad_clamp_fusion.1), kind=kCustom, calls=%fused_computation.3 | custom fusion | bytes 1966144 | tf_op jit(solution)/shard_map/jit(_take)/gather | solution.py:83
  45.7 1.7 reshape.102
  47.3 18.3 %all-to-all-done = bf16[32,12,1280]{2,1,0:T(8,128)(2,1)} async-done(((bf16[32,12,1280]{2,1,0:T(8,128)(2,1)}), bf16[32,12,1280]{2,1,0:T(8,128)(2,1)}, u32[]{:S(2)}, u32[]{:S(2)}) %all-to-all-start) | async-done | bytes 983072 | tf_op jit(solution)/shard_map/all_to_all | solution.py:85
  65.7 3.6 %all-to-all-start.2 = ((bf16[32,12,1280]{2,1,0:T(8,128)(2,1)}), bf16[32,12,1280]{2,1,0:T(8,128)(2,1)S(1)}, u32[]{:S(2)}, u32[]{:S(2)}) async-start(bf16[32,12,1280]{2,1,0:T(8,128)(2,1)} %reshape.102), calls=%async_computation.2 | async-start | bytes 2621440 | tf_op jit(solution)/shard_map/all_to_all | solution.py:85
  69.9 7.4 %reshape.100.r_ref = bf16[16,2,4,3,32,40]{5,4,3,2,1,0:T(8,128)(2,1)} reshape(bf16[32,12,1280]{2,1,0:T(8,128)(2,1)} %all-to-all-done) | data formatting | bytes 1966080 | tf_op jit(solution)/shard_map/reshape | solution.py:86
  77.4 12.2 %shard_map.55 = bf16[16,2,4,3,32,40]{5,4,3,2,1,0:T(8,128)(2,1)} custom-call(bf16[8,960,1920]{2,1,0:T(8,128)(2,1)} %t_ref.3, bf16[16,2,4,3,32,40]{5,4,3,2,1,0:T(8,128)(2,1)} %reshape.100.r_ref, f32[8,1,960]{2,1,0:T(1,128)} %reshape.45.m_ref), custom_call_target="tpu_custom_call" | custom-call | tf_op jit(solution)/shard_map/pallas_call | solution.py:46
  89.6 6.9 %reshape.101 = bf16[32,12,1280]{2,1,0:T(8,128)(2,1)} reshape(bf16[16,2,4,3,32,40]{5,4,3,2,1,0:T(8,128)(2,1)} %shard_map.55) | data formatting | bytes 1966080 | tf_op jit(solution)/shard_map/reshape | solution.py:88
  96.5 4.6 %all-to-all-done.2 = bf16[32,12,1280]{2,1,0:T(8,128)(2,1)S(1)} async-done(((bf16[32,12,1280]{2,1,0:T(8,128)(2,1)}), bf16[32,12,1280]{2,1,0:T(8,128)(2,1)S(1)}, u32[]{:S(2)}, u32[]{:S(2)}) %all-to-all-start.2) | async-done | bytes 983072 | tf_op jit(solution)/shard_map/all_to_all | solution.py:85
  101.1 3.8 %all-to-all-start.1 = ((bf16[32,12,1280]{2,1,0:T(8,128)(2,1)}), bf16[32,12,1280]{2,1,0:T(8,128)(2,1)S(1)}, u32[]{:S(2)}, u32[]{:S(2)}) async-start(bf16[32,12,1280]{2,1,0:T(8,128)(2,1)} %reshape.101), calls=%async_computation.1 | async-start | bytes 2621440 | tf_op jit(solution)/shard_map/all_to_all | solution.py:89
  105.0 6.6 %reshape.103.r_ref = bf16[16,2,4,3,32,40]{5,4,3,2,1,0:T(8,128)(2,1)} reshape(bf16[32,12,1280]{2,1,0:T(8,128)(2,1)S(1)} %all-to-all-done.2) | data formatting | bytes 1966080 | tf_op jit(solution)/shard_map/reshape | solution.py:86
  111.6 12.2 %shard_map.56 = bf16[16,2,4,3,32,40]{5,4,3,2,1,0:T(8,128)(2,1)} custom-call(bf16[8,960,1920]{2,1,0:T(8,128)(2,1)} %t_ref.3, bf16[16,2,4,3,32,40]{5,4,3,2,1,0:T(8,128)(2,1)} %reshape.103.r_ref, f32[8,1,960]{2,1,0:T(1,128)} %reshape.45.m_ref), custom_call_target="tpu_custom_call" | custom-call | tf_op jit(solution)/shard_map/pallas_call | solution.py:46
  123.8 6.9 %reshape.104 = bf16[32,12,1280]{2,1,0:T(8,128)(2,1)} reshape(bf16[16,2,4,3,32,40]{5,4,3,2,1,0:T(8,128)(2,1)} %shard_map.56) | data formatting | bytes 1966080 | tf_op jit(solution)/shard_map/reshape | solution.py:88
  130.7 5.8 %all-to-all-done.1 = bf16[32,12,1280]{2,1,0:T(8,128)(2,1)S(1)} async-done(((bf16[32,12,1280]{2,1,0:T(8,128)(2,1)}), bf16[32,12,1280]{2,1,0:T(8,128)(2,1)S(1)}, u32[]{:S(2)}, u32[]{:S(2)}) %all-to-all-start.1) | async-done | bytes 983072 | tf_op jit(solution)/shard_map/all_to_all | solution.py:89
  136.6 3.7 %all-to-all-start.3 = ((bf16[32,12,1280]{2,1,0:T(8,128)(2,1)}), bf16[32,12,1280]{2,1,0:T(8,128)(2,1)}, u32[]{:S(2)}, u32[]{:S(2)}) async-start(bf16[32,12,1280]{2,1,0:T(8,128)(2,1)} %reshape.104), calls=%async_computation.3 | async-start | bytes 2621440 | tf_op jit(solution)/shard_map/all_to_all | solution.py:89
  140.6 1.6 gather_fusion.2
  142.1 6.7 %reshape.47 = bf16[16,2,4,3,32,40]{5,4,3,2,1,0:T(8,128)(2,1)S(1)} reshape(bf16[16,24,1280]{2,1,0:T(8,128)(2,1)} %gather_fusion.2) | data formatting | bytes 1966080 | tf_op jit(solution)/shard_map/reshape | solution.py:93
  148.9 23.2 %all-to-all-done.3 = bf16[32,12,1280]{2,1,0:T(8,128)(2,1)} async-done(((bf16[32,12,1280]{2,1,0:T(8,128)(2,1)}), bf16[32,12,1280]{2,1,0:T(8,128)(2,1)}, u32[]{:S(2)}, u32[]{:S(2)}) %all-to-all-start.3) | async-done | bytes 983072 | tf_op jit(solution)/shard_map/all_to_all | solution.py:89
  172.1 2.2 %squeeze_reshape.7 = bf16[16,24,1280]{2,1,0:T(8,128)(2,1)} reshape(bf16[32,12,1280]{2,1,0:T(8,128)(2,1)} %all-to-all-done.3) | data formatting | bytes 1966080 | tf_op jit(solution)/shard_map/squeeze;reshape | solution.py:91
  174.3 2.8 %gather_fusion.4 = bf16[16,24,1280]{2,1,0:T(8,128)(2,1)} fusion(bf16[16,24,1280]{2,1,0:T(8,128)(2,1)} %squeeze_reshape.7, s32[1024]{0:T(1024)S(1)} %pad_clamp_fusion), kind=kCustom, calls=%fused_computation.4 | custom fusion | bytes 1966144 | tf_op jit(solution)/shard_map/jit(_take)/gather | solution.py:92
  177.0 7.5 %reshape.52 = bf16[16,2,4,3,32,40]{5,4,3,2,1,0:T(8,128)(2,1)} reshape(bf16[16,24,1280]{2,1,0:T(8,128)(2,1)} %gather_fusion.4) | data formatting | bytes 1966080 | tf_op jit(solution)/shard_map/reshape | solution.py:93
  184.6 3.1 %pad_maximum_fusion = bf16[16,2,8,3,32,40]{5,4,3,2,1,0:T(8,128)(2,1)S(1)} fusion(bf16[16,2,4,3,32,40]{5,4,3,2,1,0:T(8,128)(2,1)} %reshape.52, bf16[16,2,4,3,32,40]{5,4,3,2,1,0:T(8,128)(2,1)S(1)} %reshape.47), kind=kLoop, calls=%fused_computation.7 | loop fusion | flops 983040 | bytes 3932160 | tf_op jit(solution)/shard_map/concatenate | solution.py:94
  187.7 4.5 %copy.70 = bf16[16,2,8,3,32,40]{5,4,0,3,2,1:T(8,128)(2,1)} copy(bf16[16,2,8,3,32,40]{5,4,3,2,1,0:T(8,128)(2,1)S(1)} %pad_maximum_fusion) | data formatting | bytes 3932160 | tf_op jit(solution)/shard_map/concatenate | solution.py:94
  (18 shorter events, 3.1 us)
Async XLA Ops:
  0.0 0.7 copy-start
  15.1 5.5 %copy-start.3 = (s32[16]{0:T(128)S(1)}, s32[16]{0:T(128)}, u32[]{:S(2)}) copy-start(s32[16]{0:T(128)} %param.7) | copy-start | bytes 196
  26.4 39.3 %all-to-all-start = ((bf16[32,12,1280]{2,1,0:T(8,128)(2,1)}), bf16[32,12,1280]{2,1,0:T(8,128)(2,1)}, u32[]{:S(2)}, u32[]{:S(2)}) async-start(bf16[32,12,1280]{2,1,0:T(8,128)(2,1)} %reshape.99), calls=%async_computation | async-start | bytes 2621440 | tf_op jit(solution)/shard_map/all_to_all | solution.py:85
  45.6 23.6 %copy-start.2 = (s32[8,960]{1,0:T(8,128)S(1)}, s32[8,960]{1,0:T(8,128)}, u32[]{:S(2)}) copy-start(s32[8,960]{1,0:T(8,128)} %param.9) | copy-start | bytes 92164
  65.7 35.4 %all-to-all-start.2 = ((bf16[32,12,1280]{2,1,0:T(8,128)(2,1)}), bf16[32,12,1280]{2,1,0:T(8,128)(2,1)S(1)}, u32[]{:S(2)}, u32[]{:S(2)}) async-start(bf16[32,12,1280]{2,1,0:T(8,128)(2,1)} %reshape.102), calls=%async_computation.2 | async-start | bytes 2621440 | tf_op jit(solution)/shard_map/all_to_all | solution.py:85
  101.1 35.5 %all-to-all-start.1 = ((bf16[32,12,1280]{2,1,0:T(8,128)(2,1)}), bf16[32,12,1280]{2,1,0:T(8,128)(2,1)S(1)}, u32[]{:S(2)}, u32[]{:S(2)}) async-start(bf16[32,12,1280]{2,1,0:T(8,128)(2,1)} %reshape.101), calls=%async_computation.1 | async-start | bytes 2621440 | tf_op jit(solution)/shard_map/all_to_all | solution.py:89
  136.6 35.6 %all-to-all-start.3 = ((bf16[32,12,1280]{2,1,0:T(8,128)(2,1)}), bf16[32,12,1280]{2,1,0:T(8,128)(2,1)}, u32[]{:S(2)}, u32[]{:S(2)}) async-start(bf16[32,12,1280]{2,1,0:T(8,128)(2,1)} %reshape.104), calls=%async_computation.3 | async-start | bytes 2621440 | tf_op jit(solution)/shard_map/all_to_all | solution.py:89
  187.7 4.6 %copy-start.1 = (bf16[20,16]{0,1:T(8,128)(2,1)S(1)}, bf16[20,16]{0,1:T(8,128)(2,1)}, u32[]{:S(2)}) copy-start(bf16[20,16]{0,1:T(8,128)(2,1)} %param.6) | copy-start | bytes 1924

commit v11 on v9

--- a/solution.py
+++ b/solution.py
@@ -1,4 +1,3 @@
-import math
 import jax
 import jax.numpy as jnp
 from jax import lax
@@ -8,7 +7,6 @@
 
 
 AXES = ("lat", "tm")
-CHUNKS = 2
 
 
 def order_of_slot(owner_map):
@@ -75,22 +73,22 @@
     ).astype(jnp.bfloat16)
     mask = keep_mask.astype(jnp.float32).reshape(k_loc, 1, -1)
     out_dtype = jnp.bfloat16 if group_size == 1 else jnp.float32
-    chunks = math.gcd(k_loc, CHUNKS)
-    k_chunk = k_loc // chunks
+    bounds = sorted({0, (k_loc * 2) // 8, max(1, (k_loc * 5) // 8), k_loc})
     pieces = []
-    for q in range(chunks):
-        part = outgoing[:, :, q * k_chunk:(q + 1) * k_chunk]
+    for q in range(len(bounds) - 1):
+        first, k_chunk = bounds[q], bounds[q + 1] - bounds[q]
+        part = outgoing[:, :, first:first + k_chunk]
         part = part.reshape(n_lat * n_tm, k_chunk * variables, block)
         incoming = lax.all_to_all(part, AXES, 0, 0, tiled=True)
         incoming = incoming.reshape(n_lat, n_tm, k_chunk, variables, span, lat_count)
-        synth = filter_rows(hough_table, incoming, mask, out_dtype, q * k_chunk)
+        synth = filter_rows(hough_table, incoming, mask, out_dtype, first)
         synth = synth.reshape(n_lat * n_tm, k_chunk * variables, block)
         back = lax.all_to_all(synth, AXES, 0, 0, tiled=True)
         back = back.reshape(orders, group_size, n_tm * k_chunk * variables, block)
         back = back.sum(axis=1) if group_size > 1 else back[:, 0]
         back = jnp.take(back, owner_map, axis=0, mode="clip")
         pieces.append(back.reshape(orders, n_tm, k_chunk, variables, span, lat_count))
-    result = jnp.concatenate(pieces, axis=2) if chunks > 1 else pieces[0]
+    result = jnp.concatenate(pieces, axis=2) if len(pieces) > 1 else pieces[0]
     result = result.reshape(orders, kmodes, variables, span, lat_count)
     return result.transpose(1, 2, 4, 0, 3).astype(jnp.bfloat16)
 

time: 197 us -> 237 us (1.20)
  waiting for transfers between devices: 66.6 us -> 90.1 us
  starting transfers between devices: 18.4 us -> 28 us
  Pallas kernels: 24.4 us -> 27.6 us
  other arithmetic: 3.91 us -> 6.58 us
    all_to_all x2 -> x3, waiting for transfers between devices: 32.8 us -> 59.5 us  [body_inner(): incoming = lax.all_to_all(part, AXES, 0, 0, tiled=True)]
    all_to_all x2 -> x3, starting transfers between devices: 7.42 us -> 13.3 us  [body_inner(): back = lax.all_to_all(synth, AXES, 0, 0, tiled=True)]
    concatenate x1 -> x0, local copies, waits for them, and re-layouts: 4.54 us -> none  [body_inner(): result = jnp.concatenate(pieces, axis=2) if chunks > 1 else pieces[0]]
    all_to_all x2 -> x3, starting transfers between devices: 10.9 us -> 14.7 us  [body_inner(): incoming = lax.all_to_all(part, AXES, 0, 0, tiled=True)]
    pallas_call x2 -> x3, Pallas kernels: 24.4 us -> 27.6 us  [filter_rows(): pl.pallas_call(filter_kernel, grid=(k_loc,), in_specs=[pl.BlockSpec((1, r...]
    all_to_all x2 -> x3, waiting for transfers between devices: 33.8 us -> 30.6 us  [body_inner(): back = lax.all_to_all(synth, AXES, 0, 0, tiled=True)]
    concatenate x1, other arithmetic: 3.11 us -> 5.77 us  [body_inner(): result = jnp.concatenate(pieces, axis=2) if len(pieces) > 1 else pieces[0]]
    reshape x2 -> x3, local copies, waits for them, and re-layouts: 13.9 us -> 16.5 us  [body_inner(): synth = synth.reshape(n_lat * n_tm, k_chunk * variables, block)]
  transfers between devices with their start and end apart: 4 -> 6, of which waited for: 4 -> 5; matrix products, arithmetic and copies ran while one was open for 18% -> 21% of each run, Pallas kernels for 12% -> 12%
where the time goes in v11:
time: 237 us; the launch traced here: 236 us
  waiting for transfers between devices  90.1 us (38%)
  local copies, waits for them, and re-layouts  81 us (34%)
  starting transfers between devices  28 us (12%)
  Pallas kernels  27.6 us (12%)
  other arithmetic  6.58 us (3%)
  matrix products  2.49 us (1%)
    all_to_all x3, waiting for transfers between devices, body_inner(): incoming = lax.all_to_all(part, AXES, 0, 0, tiled=True)  59.5 us
    all_to_all x3, waiting for transfers between devices, body_inner(): back = lax.all_to_all(synth, AXES, 0, 0, tiled=True)  30.6 us
    pallas_call x3, Pallas kernels, filter_rows(): pl.pallas_call(filter_kernel, grid=(k_loc,), in_specs=[pl.BlockSpec((1, r...  27.6 us
    reshape x3, local copies, waits for them, and re-layouts, body_inner(): synth = synth.reshape(n_lat * n_tm, k_chunk * variables, block)  16.5 us
    reshape x2, local copies, waits for them, and re-layouts, body_inner(): fields.transpose(3, 0, 1, 4, 2).reshape(orders, variables, lev, block)  15.4 us
    reshape x3, local copies, waits for them, and re-layouts, body_inner(): incoming.reshape(n_lat, n_tm, k_chunk, variables, span, lat_count)  15.3 us
    reshape x3, local copies, waits for them, and re-layouts, body_inner(): back.reshape(orders, n_tm, k_chunk, variables, span, lat_count)  15.2 us
    all_to_all x3, starting transfers between devices, body_inner(): incoming = lax.all_to_all(part, AXES, 0, 0, tiled=True)  14.7 us
  transfers between devices with their start and end apart: 6, of which 5 were waited for; matrix products, arithmetic and copies ran while one was open for 21% of the time, Pallas kernels for 12%

profile of v11, /device:TPU:0, one launch (start us, length us, event | category | flops | bytes accessed | tf_op | source)
XLA Modules:
  0.0 236.0 jit_solution(15166603183209715920)
XLA Ops:
  1.5 12.9 %reshape.50 = bf16[16,3,20,1280]{3,0,2,1:T(8,128)(2,1)} reshape(bf16[16,3,20,32,40]{4,3,0,2,1:T(8,128)(2,1)} %bitcast.34) | data formatting | bytes 4915200 | tf_op jit(solution)/shard_map/reshape | solution.py:67
  14.4 2.5 %copy.61 = bf16[16,3,20,1280]{3,2,1,0:T(8,128)(2,1)S(1)} copy(bf16[16,3,20,1280]{3,0,2,1:T(8,128)(2,1)} %reshape.50) | data formatting | bytes 4915200 | tf_op jit(solution)/shard_map/reshape | solution.py:67
  16.8 2.3 gather_fusion.1
  19.2 2.5 %fusion = bf16[16,2,8,3,1280]{4,2,1,3,0:T(8,128)(2,1)S(1)} fusion(bf16[16,3,20,1280]{3,2,1,0:T(8,128)(2,1)} %gather_fusion.1, bf16[20,16]{0,1:T(8,128)(2,1)S(1)} %copy-done), kind=kOutput, calls=%fused_computation.7 | convolution fusion | flops 40304640 | bytes 4424320 | tf_op jit(solution)/shard_map/jvlx,lus->jusvx/dot_general | solution.py:71
  23.4 7.4 %all-to-all-start = ((bf16[32,6,1280]{2,1,0:T(8,128)(2,1)}), bf16[32,6,1280]{2,1,0:T(8,128)(2,1)}, u32[]{:S(2)}, u32[]{:S(2)}) async-start(bf16[32,6,1280]{2,1,0:T(8,128)(2,1)} %reshape.112), calls=%async_computation | async-start | bytes 1310720 | tf_op jit(solution)/shard_map/all_to_all | solution.py:82
  32.2 1.5 reshape.115
  33.8 14.9 %all-to-all-done = bf16[32,6,1280]{2,1,0:T(8,128)(2,1)} async-done(((bf16[32,6,1280]{2,1,0:T(8,128)(2,1)}), bf16[32,6,1280]{2,1,0:T(8,128)(2,1)}, u32[]{:S(2)}, u32[]{:S(2)}) %all-to-all-start) | async-done | bytes 491552 | tf_op jit(solution)/shard_map/all_to_all | solution.py:82
  48.7 3.6 %all-to-all-start.2 = ((bf16[32,9,1280]{2,1,0:T(8,128)(2,1)}), bf16[32,9,1280]{2,1,0:T(8,128)(2,1)S(1)}, u32[]{:S(2)}, u32[]{:S(2)}) async-start(bf16[32,9,1280]{2,1,0:T(8,128)(2,1)} %reshape.115), calls=%async_computation.2 | async-start | bytes 2621440 | tf_op jit(solution)/shard_map/all_to_all | solution.py:82
  52.7 1.6 reshape.118
  54.3 29.8 %all-to-all-done.2 = bf16[32,9,1280]{2,1,0:T(8,128)(2,1)S(1)} async-done(((bf16[32,9,1280]{2,1,0:T(8,128)(2,1)}), bf16[32,9,1280]{2,1,0:T(8,128)(2,1)S(1)}, u32[]{:S(2)}, u32[]{:S(2)}) %all-to-all-start.2) | async-done | bytes 737312 | tf_op jit(solution)/shard_map/all_to_all | solution.py:82
  84.1 3.6 %all-to-all-start.4 = ((bf16[32,9,1280]{2,1,0:T(8,128)(2,1)}), bf16[32,9,1280]{2,1,0:T(8,128)(2,1)S(1)}, u32[]{:S(2)}, u32[]{:S(2)}) async-start(bf16[32,9,1280]{2,1,0:T(8,128)(2,1)} %reshape.118), calls=%async_computation.4 | async-start | bytes 2621440 | tf_op jit(solution)/shard_map/all_to_all | solution.py:82
  88.4 4.6 %reshape.113.r_ref = bf16[16,2,2,3,32,40]{5,4,3,2,1,0:T(8,128)(2,1)} reshape(bf16[32,6,1280]{2,1,0:T(8,128)(2,1)} %all-to-all-done) | data formatting | bytes 983040 | tf_op jit(solution)/shard_map/reshape | solution.py:83
  93.0 7.5 %shard_map.55 = bf16[16,2,2,3,32,40]{5,4,3,2,1,0:T(8,128)(2,1)} custom-call(bf16[8,960,1920]{2,1,0:T(8,128)(2,1)} %t_ref.5, bf16[16,2,2,3,32,40]{5,4,3,2,1,0:T(8,128)(2,1)} %reshape.113.r_ref, f32[8,1,960]{2,1,0:T(1,128)} %reshape.54.m_ref), custom_call_target="tpu_custom_call" | custom-call | tf_op jit(solution)/shard_map/pallas_call | solution.py:44
  100.5 4.2 %reshape.114 = bf16[32,6,1280]{2,1,0:T(8,128)(2,1)} reshape(bf16[16,2,2,3,32,40]{5,4,3,2,1,0:T(8,128)(2,1)} %shard_map.55) | data formatting | bytes 983040 | tf_op jit(solution)/shard_map/reshape | solution.py:85
  104.8 14.8 %all-to-all-done.4 = bf16[32,9,1280]{2,1,0:T(8,128)(2,1)S(1)} async-done(((bf16[32,9,1280]{2,1,0:T(8,128)(2,1)}), bf16[32,9,1280]{2,1,0:T(8,128)(2,1)S(1)}, u32[]{:S(2)}, u32[]{:S(2)}) %all-to-all-start.4) | async-done | bytes 737312 | tf_op jit(solution)/shard_map/all_to_all | solution.py:82
  119.6 3.8 %all-to-all-start.1 = ((bf16[32,6,1280]{2,1,0:T(8,128)(2,1)}), bf16[32,6,1280]{2,1,0:T(8,128)(2,1)S(1)}, u32[]{:S(2)}, u32[]{:S(2)}) async-start(bf16[32,6,1280]{2,1,0:T(8,128)(2,1)} %reshape.114), calls=%async_computation.1 | async-start | bytes 1310720 | tf_op jit(solution)/shard_map/all_to_all | solution.py:86
  123.4 5.3 %reshape.119.r_ref = bf16[16,2,3,3,32,40]{5,4,3,2,1,0:T(8,128)(2,1)} reshape(bf16[32,9,1280]{2,1,0:T(8,128)(2,1)S(1)} %all-to-all-done.4) | data formatting | bytes 1474560 | tf_op jit(solution)/shard_map/reshape | solution.py:83
  128.7 10.1 %shard_map.57 = bf16[16,2,3,3,32,40]{5,4,3,2,1,0:T(8,128)(2,1)} custom-call(bf16[8,960,1920]{2,1,0:T(8,128)(2,1)} %t_ref.5, bf16[16,2,3,3,32,40]{5,4,3,2,1,0:T(8,128)(2,1)} %reshape.119.r_ref, f32[8,1,960]{2,1,0:T(1,128)} %reshape.54.m_ref), custom_call_target="tpu_custom_call" | custom-call | tf_op jit(solution)/shard_map/pallas_call | solution.py:44
  138.7 6.1 %reshape.120 = bf16[32,9,1280]{2,1,0:T(8,128)(2,1)} reshape(bf16[16,2,3,3,32,40]{5,4,3,2,1,0:T(8,128)(2,1)} %shard_map.57) | data formatting | bytes 1474560 | tf_op jit(solution)/shard_map/reshape | solution.py:85
  144.8 5.7 %all-to-all-start.5 = ((bf16[32,9,1280]{2,1,0:T(8,128)(2,1)}), bf16[32,9,1280]{2,1,0:T(8,128)(2,1)S(1)}, u32[]{:S(2)}, u32[]{:S(2)}) async-start(bf16[32,9,1280]{2,1,0:T(8,128)(2,1)} %reshape.120), calls=%async_computation.5 | async-start | bytes 2621440 | tf_op jit(solution)/shard_map/all_to_all | solution.py:86
  150.5 5.3 %reshape.116.r_ref = bf16[16,2,3,3,32,40]{5,4,3,2,1,0:T(8,128)(2,1)} reshape(bf16[32,9,1280]{2,1,0:T(8,128)(2,1)S(1)} %all-to-all-done.2) | data formatting | bytes 1474560 | tf_op jit(solution)/shard_map/reshape | solution.py:83
  155.8 10.0 %shard_map.56 = bf16[16,2,3,3,32,40]{5,4,3,2,1,0:T(8,128)(2,1)} custom-call(bf16[8,960,1920]{2,1,0:T(8,128)(2,1)} %t_ref.5, bf16[16,2,3,3,32,40]{5,4,3,2,1,0:T(8,128)(2,1)} %reshape.116.r_ref, f32[8,1,960]{2,1,0:T(1,128)} %reshape.54.m_ref), custom_call_target="tpu_custom_call" | custom-call | tf_op jit(solution)/shard_map/pallas_call | solution.py:44
  165.9 6.1 %reshape.117 = bf16[32,9,1280]{2,1,0:T(8,128)(2,1)} reshape(bf16[16,2,3,3,32,40]{5,4,3,2,1,0:T(8,128)(2,1)} %shard_map.56) | data formatting | bytes 1474560 | tf_op jit(solution)/shard_map/reshape | solution.py:85
  172.0 10.3 %all-to-all-done.5 = bf16[32,9,1280]{2,1,0:T(8,128)(2,1)S(1)} async-done(((bf16[32,9,1280]{2,1,0:T(8,128)(2,1)}), bf16[32,9,1280]{2,1,0:T(8,128)(2,1)S(1)}, u32[]{:S(2)}, u32[]{:S(2)}) %all-to-all-start.5) | async-done | bytes 737312 | tf_op jit(solution)/shard_map/all_to_all | solution.py:86
  182.3 3.8 %all-to-all-start.3 = ((bf16[32,9,1280]{2,1,0:T(8,128)(2,1)}), bf16[32,9,1280]{2,1,0:T(8,128)(2,1)S(1)}, u32[]{:S(2)}, u32[]{:S(2)}) async-start(bf16[32,9,1280]{2,1,0:T(8,128)(2,1)} %reshape.117), calls=%async_computation.3 | async-start | bytes 2621440 | tf_op jit(solution)/shard_map/all_to_all | solution.py:86
  187.2 1.7 gather_fusion.2
  189.8 4.7 %reshape.56 = bf16[16,2,2,3,32,40]{5,4,0,3,2,1:T(8,128)(2,1)} reshape(bf16[16,12,1280]{2,0,1:T(8,128)(2,1)} %copy.68) | data formatting | bytes 983040 | tf_op jit(solution)/shard_map/reshape | solution.py:90
  195.6 1.8 gather_fusion.4
  197.5 20.3 %all-to-all-done.3 = bf16[32,9,1280]{2,1,0:T(8,128)(2,1)S(1)} async-done(((bf16[32,9,1280]{2,1,0:T(8,128)(2,1)}), bf16[32,9,1280]{2,1,0:T(8,128)(2,1)S(1)}, u32[]{:S(2)}, u32[]{:S(2)}) %all-to-all-start.3) | async-done | bytes 737312 | tf_op jit(solution)/shard_map/all_to_all | solution.py:86
  219.6 5.3 %reshape.60 = bf16[16,2,3,3,32,40]{5,4,0,3,2,1:T(8,128)(2,1)S(1)} reshape(bf16[16,18,1280]{2,0,1:T(8,128)(2,1)} %copy.75) | data formatting | bytes 1474560 | tf_op jit(solution)/shard_map/reshape | solution.py:90
  224.9 5.3 %reshape.64 = bf16[16,2,3,3,32,40]{5,4,0,3,2,1:T(8,128)(2,1)} reshape(bf16[16,18,1280]{2,0,1:T(8,128)(2,1)S(1)} %copy.82) | data formatting | bytes 1474560 | tf_op jit(solution)/shard_map/reshape | solution.py:90
  230.2 5.8 %pad_maximum_fusion = bf16[16,2,8,3,32,40]{5,4,0,3,2,1:T(8,128)(2,1)} fusion(bf16[16,2,3,3,32,40]{5,4,0,3,2,1:T(8,128)(2,1)} %reshape.64, bf16[16,2,3,3,32,40]{5,4,0,3,2,1:T(8,128)(2,1)S(1)} %reshape.60, bf16[16,2,2,3,32,40]{5,4,0,3,2,1:T(8,128)(2,1)} %reshape.56), kind=kLoop, calls=%fused_computation.5 | loop fusion | flops 1966080 | bytes 3932160 | tf_op jit(solution)/shard_map/concatenate | solution.py:91
  (30 shorter events, 10.6 us)
Async XLA Ops:
  0.0 19.2 %copy-start = (bf16[20,16]{0,1:T(8,128)(2,1)S(1)}, bf16[20,16]{0,1:T(8,128)(2,1)}, u32[]{:S(2)}) copy-start(bf16[20,16]{0,1:T(8,128)(2,1)} %param.6) | copy-start | bytes 1924
  23.4 25.2 %all-to-all-start = ((bf16[32,6,1280]{2,1,0:T(8,128)(2,1)}), bf16[32,6,1280]{2,1,0:T(8,128)(2,1)}, u32[]{:S(2)}, u32[]{:S(2)}) async-start(bf16[32,6,1280]{2,1,0:T(8,128)(2,1)} %reshape.112), calls=%async_computation | async-start | bytes 1310720 | tf_op jit(solution)/shard_map/all_to_all | solution.py:82
  48.7 35.4 %all-to-all-start.2 = ((bf16[32,9,1280]{2,1,0:T(8,128)(2,1)}), bf16[32,9,1280]{2,1,0:T(8,128)(2,1)S(1)}, u32[]{:S(2)}, u32[]{:S(2)}) async-start(bf16[32,9,1280]{2,1,0:T(8,128)(2,1)} %reshape.115), calls=%async_computation.2 | async-start | bytes 2621440 | tf_op jit(solution)/shard_map/all_to_all | solution.py:82
  52.7 35.0 %copy-start.2 = (s32[8,960]{1,0:T(8,128)S(1)}, s32[8,960]{1,0:T(8,128)}, u32[]{:S(2)}) copy-start(s32[8,960]{1,0:T(8,128)} %param.9) | copy-start | bytes 92164
  84.1 35.4 %all-to-all-start.4 = ((bf16[32,9,1280]{2,1,0:T(8,128)(2,1)}), bf16[32,9,1280]{2,1,0:T(8,128)(2,1)S(1)}, u32[]{:S(2)}, u32[]{:S(2)}) async-start(bf16[32,9,1280]{2,1,0:T(8,128)(2,1)} %reshape.118), calls=%async_computation.4 | async-start | bytes 2621440 | tf_op jit(solution)/shard_map/all_to_all | solution.py:82
  119.6 25.3 %all-to-all-start.1 = ((bf16[32,6,1280]{2,1,0:T(8,128)(2,1)}), bf16[32,6,1280]{2,1,0:T(8,128)(2,1)S(1)}, u32[]{:S(2)}, u32[]{:S(2)}) async-start(bf16[32,6,1280]{2,1,0:T(8,128)(2,1)} %reshape.114), calls=%async_computation.1 | async-start | bytes 1310720 | tf_op jit(solution)/shard_map/all_to_all | solution.py:86
  144.8 37.5 %all-to-all-start.5 = ((bf16[32,9,1280]{2,1,0:T(8,128)(2,1)}), bf16[32,9,1280]{2,1,0:T(8,128)(2,1)S(1)}, u32[]{:S(2)}, u32[]{:S(2)}) async-start(bf16[32,9,1280]{2,1,0:T(8,128)(2,1)} %reshape.120), calls=%async_computation.5 | async-start | bytes 2621440 | tf_op jit(solution)/shard_map/all_to_all | solution.py:86
  165.9 20.3 %copy-start.3 = (s32[16]{0:T(128)S(1)}, s32[16]{0:T(128)}, u32[]{:S(2)}) copy-start(s32[16]{0:T(128)} %param.7) | copy-start | bytes 196
  182.3 35.5 %all-to-all-start.3 = ((bf16[32,9,1280]{2,1,0:T(8,128)(2,1)}), bf16[32,9,1280]{2,1,0:T(8,128)(2,1)S(1)}, u32[]{:S(2)}, u32[]{:S(2)}) async-start(bf16[32,9,1280]{2,1,0:T(8,128)(2,1)} %reshape.117), calls=%async_computation.3 | async-start | bytes 2621440 | tf_op jit(solution)/shard_map/all_to_all | solution.py:86
  230.2 5.8 %copy-start.1 = (bf16[20,16]{0,1:T(8,128)(2,1)S(1)}, bf16[20,16]{0,1:T(8,128)(2,1)}, u32[]{:S(2)}) copy-start(bf16[20,16]{0,1:T(8,128)(2,1)} %param.6) | copy-start | bytes 1924
